TPU v7x, 128 devices: a whole 4x4x4 slice. The times are simulated.
128 devices in a mesh: fsdp: 8 (over x, z_lo), dp: 16 (over z_hi, y, core).
Axes of the slice: x: 4, y: 4, z: 4 (z_hi: 2, z_lo: 2; z = z_hi * 2 + z_lo), core: 2. Of those that a mesh axis runs over, the one named last changes fastest.
Arguments:
- tokens: bfloat16 [8, 2176, 3200], P('fsdp', 'dp'), may hold values from -6 to 6
- norm_gain: float32 [3200], replicated, may hold values from 0.5 to 1.5
- qkv_weight: bfloat16 [3200, 6144], P('fsdp', 'dp'), may hold values from -4 to 4
- qk_gain: float32 [2, 2048], P(None, 'dp'), may hold values from 1 to 8
- out_weight: bfloat16 [2048, 3200], P('dp', 'fsdp'), may hold values from -0.125 to 0.125
- layer_scale: float32 [3200], replicated, may hold values from 0.2 to 1
- tile_counts: int32 [8, 2], replicated, may hold values from 0 to 2, as said below
- owners: int32 [8, 2], replicated, may hold values from 0 to 7, as said below
Outputs:
- vision_tokens: bfloat16 [32, 256, 12800], P('fsdp', None, 'dp')
Inputs may be any that keep to these rules, and one draw needn't show every extreme that they name: `tile_counts`: column 0 is 1 to 2, column 1 is 0 to 2 minus column 0. All owners together get at most 4 live tiles each, and one owner gets exactly 4.
All inputs are finite; a program needn't handle non-finite values.
Results may differ from a plain program's by a relative error of at most 0.006.
The roundings to bfloat16 on the way count: a program that leaves them out, or rounds other values in their place, can miss the bound.
Values may be sent and summed in bfloat16 or wider, within the bound.
No kernel may reach another device: no remote copies, remote signals or barrier semaphores. Data moves between devices by JAX's collectives and lax.ppermute only.
A program may use at most 192 MiB of HBM per device.

v0:
```python
import jax
import jax.numpy as jnp
from jax import lax
from jax.sharding import PartitionSpec as P

HEAD_DIM = 128
GRID = 32
SLOTS = 2
TILE = 1025
CAP = 4


EPSILON = 1e-06


def merge_tiles(values):
    halves = GRID // 2
    columns = values.shape[1]
    tile_list = []
    for tile_slot in range(SLOTS):
        patches = values[tile_slot * TILE + 1 : (tile_slot + 1) * TILE]
        square = patches.reshape(halves, 2, halves, 2, columns).transpose(0, 2, 4, 1, 3)
        tile_list.append(square.reshape(halves * halves, columns * 4))
    return jnp.stack(tile_list)


def tile_owners(tile_counts, owners):
    slot_index = jnp.arange(SLOTS, dtype=jnp.int32)[None, :]
    first_count = tile_counts[:, 0:1]
    holder = jnp.where(slot_index < first_count, owners[:, 0:1], owners[:, 1:2])
    living = slot_index < first_count + tile_counts[:, 1:2]
    return (holder, living)


def place_tiles(received, holder, living, target):
    owned_flag = jnp.logical_and(living, holder == target).reshape(-1).astype(jnp.int32)
    before = jnp.cumsum(owned_flag) - owned_flag
    chosen = jnp.logical_and(
        before[None, :] == jnp.arange(CAP, dtype=jnp.int32)[:, None], owned_flag[None, :] == 1
    )
    flattened = received.reshape(received.shape[0] * received.shape[1], -1)
    placed = jnp.dot(chosen.astype(jnp.bfloat16), flattened, preferred_element_type=jnp.float32)
    return placed.astype(jnp.bfloat16).reshape(CAP, received.shape[2], received.shape[3])


def body(tokens, norm_gain, qkv_weight, qk_gain, out_weight, layer_scale, tile_counts, owners):
    own_rows = tokens[0]
    gathered = lax.all_gather(own_rows, "dp", axis=0, tiled=True)
    length = gathered.shape[0]
    model_width = gathered.shape[1]
    groups = lax.axis_size("dp")
    values = gathered.astype(jnp.float32)
    normed = (
        values * lax.rsqrt(jnp.mean(values * values, axis=-1, keepdims=True) + EPSILON) * norm_gain
    ).astype(jnp.bfloat16)
    projected = jnp.dot(
        normed,
        lax.all_gather(qkv_weight, "fsdp", axis=0, tiled=True),
        preferred_element_type=jnp.float32,
    )
    queries = projected[:, :HEAD_DIM]
    keys_part = projected[:, HEAD_DIM : 2 * HEAD_DIM]
    values_part = projected[:, 2 * HEAD_DIM :].astype(jnp.bfloat16)
    query_sums, key_sums = lax.psum(
        (jnp.sum(queries * queries, axis=-1), jnp.sum(keys_part * keys_part, axis=-1)), "dp"
    )
    window = groups * HEAD_DIM
    queries = (queries * lax.rsqrt(query_sums / window + EPSILON)[:, None] * qk_gain[0]).astype(
        jnp.bfloat16
    )
    keys_part = (keys_part * lax.rsqrt(key_sums / window + EPSILON)[:, None] * qk_gain[1]).astype(
        jnp.bfloat16
    )
    row_index = lax.axis_index("fsdp")
    row_count = lax.axis_size("fsdp")
    factor = HEAD_DIM ** (-0.5)
    covered = SLOTS * TILE
    tile_query = queries[:covered].reshape(SLOTS, TILE, HEAD_DIM)
    tile_key = keys_part[:covered].reshape(SLOTS, TILE, HEAD_DIM)
    tile_value = values_part[:covered].reshape(SLOTS, TILE, HEAD_DIM)
    scores = (
        jnp.einsum("sqc,skc->sqk", tile_query, tile_key, preferred_element_type=jnp.float32)
        * factor
    )
    highest = jnp.max(scores, axis=-1, keepdims=True)
    exponent = jnp.exp(scores - highest)
    weights = (exponent / jnp.sum(exponent, axis=-1, keepdims=True)).astype(jnp.bfloat16)
    tile_out = jnp.einsum(
        "sqk,skc->sqc", weights, tile_value, preferred_element_type=jnp.float32
    ).astype(jnp.bfloat16)
    head_out = jnp.concatenate(
        [
            tile_out.reshape(covered, HEAD_DIM),
            jnp.zeros((length - covered, HEAD_DIM), jnp.bfloat16),
        ],
        axis=0,
    )
    token_heads = lax.all_to_all(head_out, "dp", split_axis=0, concat_axis=1, tiled=True)
    weight_rows = lax.all_gather(out_weight, "dp", axis=0, tiled=True)
    weight_full = lax.all_gather(weight_rows, "fsdp", axis=1, tiled=True)
    rows_here = token_heads.shape[0]
    head_terms = jnp.einsum(
        "shc,hcd->shd",
        token_heads.reshape(rows_here, groups, HEAD_DIM),
        weight_full.reshape(groups, HEAD_DIM, model_width),
        preferred_element_type=jnp.float32,
    ).astype(jnp.bfloat16)
    attention = jnp.sum(lax.optimization_barrier(head_terms).astype(jnp.float32), axis=1)
    token_update = (own_rows.astype(jnp.float32) + layer_scale * attention).astype(jnp.bfloat16)
    updated = lax.all_to_all(token_update, "dp", split_axis=1, concat_axis=0, tiled=True)
    merged = merge_tiles(updated)
    holder, living = tile_owners(tile_counts, owners)
    own_holder = holder[row_index]
    own_living = living[row_index]
    destination = jnp.arange(row_count, dtype=jnp.int32)[:, None]
    sending = jnp.logical_and(destination == own_holder[None, :], own_living[None, :])
    outgoing = jnp.where(sending[:, :, None, None], merged[None], jnp.zeros((), jnp.bfloat16))
    received = lax.all_to_all(outgoing, "fsdp", split_axis=0, concat_axis=0, tiled=True)
    return place_tiles(received, holder, living, row_index)


def solution(mesh):
    placed = (
        P("fsdp", "dp", None),
        P(),
        P("fsdp", "dp"),
        P(None, "dp"),
        P("dp", "fsdp"),
        P(),
        P(),
        P(),
    )
    return jax.shard_map(
        body, mesh=mesh, in_specs=placed, out_specs=P("fsdp", None, "dp"), check_vma=False
    )
```

profile of v0, /device:TPU:8, one launch (start us, length us, event | category | flops | bytes accessed | tf_op | source)
XLA Modules:
  0.0 718.4 jit_solution(17169709936321578698)
XLA Ops:
  8.8 50.6 %all-gather.8.cloned.1.call-done = bf16[2048,400]{0,1:T(8,128)(2,1)} async-done(((bf16[128,400]{0,1:T(8,128)(2,1)}), bf16[2048,400]{0,1:T(8,128)(2,1)}) %all-gather.8.cloned.1.call-update) | async-done | bytes 1638416 | tf_op jit(solution)/shard_map/all_gather | solution.py:99
  60.1 95.9 %all-gather.12.cloned.1.call-done = bf16[1,2176,3200]{2,1,0:T(8,128)(2,1)} async-done(((bf16[1,136,3200]{2,1,0:T(8,128)(2,1)}), bf16[1,2176,3200]{2,1,0:T(8,128)(2,1)}) %all-gather.12.cloned.1.call-update) | async-done | bytes 13926416 | tf_op jit(solution)/shard_map/all_gather | solution.py:48
  156.0 7.7 %fusion.1 = f32[2176]{0:T(1024)S(1)} fusion(bf16[1,2176,3200]{2,1,0:T(8,128)(2,1)} %all-gather.12.cloned.1.call-done), kind=kLoop, calls=%fused_computation.4 | loop fusion | flops 20887424 | bytes 13935104 | tf_op jit(solution)/shard_map/reduce_sum | solution.py:54
  163.8 50.3 %all-gather.6.cloned.1.call-done = bf16[3200,384]{1,0:T(8,128)(2,1)} async-done(((bf16[400,384]{1,0:T(8,128)(2,1)}), bf16[3200,384]{1,0:T(8,128)(2,1)}) %all-gather.6.cloned.1.call-update) | async-done | bytes 2457616 | tf_op jit(solution)/shard_map/all_gather | solution.py:58
  214.1 11.8 %fusion.5 = f32[2176,384]{1,0:T(8,128)S(1)} fusion(bf16[3200,384]{1,0:T(8,128)(2,1)} %all-gather.6.cloned.1.call-done, bf16[1,2176,3200]{2,1,0:T(8,128)(2,1)} %all-gather.12.cloned.1.call-done, f32[3200]{0:T(1024)S(1)} %copy-done.4, f32[2176]{0:T(1024)S(1)} %add_rsqrt_fusion.2), kind=kOutput, calls=%fused_computation.10 | convolution fusion | flops 5375590400 | bytes 19747840 | tf_op jit(solution)/shard_map/dot_general | solution.py:56
  227.4 65.5 %all-reduce.1 = (f32[2176]{0:T(1024)S(1)}, f32[2176]{0:T(1024)S(1)}) all-reduce(f32[2176]{0:T(1024)S(1)} %get-tuple-element.6, f32[2176]{0:T(1024)S(1)} %get-tuple-element.5), channel_id=1, replica_groups=mesh['fsdp'=8,'dp'=16] {'dp'}, use_global_device_ids=true, to_apply=%region_3.0 | all-reduce | flops 4352 | bytes 34816 | tf_op jit(solution)/shard_map/psum | solution.py:64
  295.5 3.2 fusion.30
  298.7 4.9 fusion.12
  304.6 10.4 %all-to-all-start = ((bf16[16,136,128]{2,1,0:T(8,128)(2,1)}), bf16[16,136,128]{2,1,0:T(8,128)(2,1)}, u32[]{:S(2)}, u32[]{:S(2)}) async-start(bf16[16,136,128]{2,1,0:T(8,128)(2,1)} %bitcast.10), calls=%async_computation | async-start | bytes 1114112 | tf_op jit(solution)/shard_map/all_to_all | solution.py:98
  315.0 3.2 reshape.267
  318.4 162.1 %all-gather.10.cloned.1.call-done = bf16[2048,3200]{0,1:T(8,128)(2,1)} async-done(((bf16[2048,400]{0,1:T(8,128)(2,1)}), bf16[2048,3200]{0,1:T(8,128)(2,1)}) %all-gather.10.cloned.1.call-update) | async-done | bytes 13107216 | tf_op jit(solution)/shard_map/all_gather | solution.py:100
  480.5 17.2 %copy.31 = bf16[2048,3200]{1,0:T(8,128)(2,1)} copy(bf16[2048,3200]{0,1:T(8,128)(2,1)} %all-gather.10.cloned.1.call-done) | data formatting | bytes 26214400 | tf_op jit(solution)/shard_map/all_gather | solution.py:100
  497.7 13.9 %convert_bitcast_fusion = bf16[136,16,3200]{2,0,1:T(8,128)(2,1)} fusion(bf16[16,128,3200]{2,1,0:T(8,128)(2,1)} %bitcast.55, bf16[16,136,128]{2,1,0:T(8,128)(2,1)} %all-to-all-done), kind=kOutput, calls=%fused_computation.12 | convolution fusion | flops 1789542400 | bytes 27590656 | tf_op jit(solution)/shard_map/shc,hcd->shd/dot_general | solution.py:102
  511.5 8.5 %convert_reduce_fusion = f32[136,3200]{1,0:T(8,128)} fusion(bf16[136,16,3200]{2,0,1:T(8,128)(2,1)} %convert_bitcast_fusion), kind=kLoop, calls=%fused_computation.7 | loop fusion | flops 13491200 | bytes 15667200 | tf_op jit(solution)/shard_map/reduce_sum | solution.py:108
  520.0 5.4 reduce_sum.52
  525.4 2.2 add_convert_fusion
  529.0 7.8 %all-to-all-start.1 = ((bf16[136,16,200]{2,0,1:T(8,128)(2,1)}), bf16[136,16,200]{2,0,1:T(8,128)(2,1)S(1)}, u32[]{:S(2)}, u32[]{:S(2)}) async-start(bf16[136,16,200]{2,0,1:T(8,128)(2,1)} %copy.32), calls=%async_computation.1 | async-start | bytes 2228224 | tf_op jit(solution)/shard_map/all_to_all | solution.py:110
  537.0 15.2 %all-to-all-done.1 = bf16[136,16,200]{2,0,1:T(8,128)(2,1)S(1)} async-done(((bf16[136,16,200]{2,0,1:T(8,128)(2,1)}), bf16[136,16,200]{2,0,1:T(8,128)(2,1)S(1)}, u32[]{:S(2)}, u32[]{:S(2)}) %all-to-all-start.1) | async-done | bytes 870432 | tf_op jit(solution)/shard_map/all_to_all | solution.py:110
  554.3 4.9 copy.33
  559.2 3.8 stack_reshape.6
  563.0 2.1 reshape.262
  565.1 4.9 copy.34
  570.0 3.9 stack_reshape.7
  575.1 3.4 broadcast_select_fusion
  578.4 4.8 all-to-all-start.2
  583.5 91.6 %all-to-all-done.2 = bf16[8,2,256,800]{2,3,1,0:T(8,128)(2,1)} async-done(((bf16[8,2,256,800]{2,3,1,0:T(8,128)(2,1)}), bf16[8,2,256,800]{2,3,1,0:T(8,128)(2,1)}, u32[]{:S(2)}, u32[]{:S(2)}) %all-to-all-start.2) | async-done | bytes 6553632 | tf_op jit(solution)/shard_map/all_to_all | solution.py:118
  675.2 11.0 %copy.35 = bf16[8,2,256,800]{3,2,1,0:T(8,128)(2,1)} copy(bf16[8,2,256,800]{2,3,1,0:T(8,128)(2,1)} %all-to-all-done.2) | data formatting | bytes 13107200 | tf_op jit(solution)/shard_map/all_to_all | solution.py:118
  686.2 14.7 %reshape.263 = bf16[16,204800]{1,0:T(8,128)(2,1)} reshape(bf16[8,2,256,800]{3,2,1,0:T(8,128)(2,1)} %copy.35) | data formatting | bytes 13107200 | tf_op jit(solution)/shard_map/reshape | solution.py:41
  700.9 4.0 convolution_convert_fusion
  704.9 1.6 reshape.272
  706.5 2.8 reshape.264
  709.3 2.3 copy.36
  (48 shorter events, 13.3 us)
Async XLA Ops:
  6.5 52.8 %all-gather.8.cloned.1.call-start = ((), (), s32[]{:S(2)}) async-start(), calls=%async_computation.4 | async-start | bytes 1740800 | tf_op jit(solution)/shard_map/all_gather | solution.py:99
  7.3 148.8 %all-gather.12.cloned.1.call-start = ((), (), s32[]{:S(2)}) async-start(), calls=%async_computation.6 | async-start | bytes 14796800 | tf_op jit(solution)/shard_map/all_gather | solution.py:48
  8.0 206.1 %all-gather.6.cloned.1.call-start = ((), (), s32[]{:S(2)}) async-start(), calls=%async_computation.3 | async-start | bytes 2764800 | tf_op jit(solution)/shard_map/all_gather | solution.py:58
  8.7 471.7 %all-gather.10.cloned.1.call-start = ((), (), s32[]{:S(2)}) async-start(), calls=%async_computation.5 | async-start | bytes 14745600 | tf_op jit(solution)/shard_map/all_gather | solution.py:100
  60.1 154.0 %copy-start.4 = (f32[3200]{0:T(1024)S(1)}, f32[3200]{0:T(1024)}, u32[]{:S(2)}) copy-start(f32[3200]{0:T(1024)} %param.9) | copy-start | bytes 38404
  298.7 16.2 %copy-start = (bf16[1,136,3200]{2,1,0:T(8,128)(2,1)S(1)}, bf16[1,136,3200]{2,1,0:T(8,128)(2,1)}, u32[]{:S(2)}) copy-start(bf16[1,136,3200]{2,1,0:T(8,128)(2,1)} %param.8) | copy-start | bytes 2611204
  303.6 14.6 %copy-start.1 = (f32[3200]{0:T(1024)S(1)}, f32[3200]{0:T(1024)}, u32[]{:S(2)}) copy-start(f32[3200]{0:T(1024)} %param.13) | copy-start | bytes 38404
  303.6 14.7 %copy-start.2 = (s32[8,2]{0,1:T(2,128)S(1)}, s32[8,2]{0,1:T(2,128)}, u32[]{:S(2)}) copy-start(s32[8,2]{0,1:T(2,128)} %param.15) | copy-start | bytes 196
  303.6 14.7 %copy-start.3 = (s32[8,2]{0,1:T(2,128)S(1)}, s32[8,2]{0,1:T(2,128)}, u32[]{:S(2)}) copy-start(s32[8,2]{0,1:T(2,128)} %param.14) | copy-start | bytes 196
  304.6 193.1 %all-to-all-start = ((bf16[16,136,128]{2,1,0:T(8,128)(2,1)}), bf16[16,136,128]{2,1,0:T(8,128)(2,1)}, u32[]{:S(2)}, u32[]{:S(2)}) async-start(bf16[16,136,128]{2,1,0:T(8,128)(2,1)} %bitcast.10), calls=%async_computation | async-start | bytes 1114112 | tf_op jit(solution)/shard_map/all_to_all | solution.py:98
  529.0 23.2 %all-to-all-start.1 = ((bf16[136,16,200]{2,0,1:T(8,128)(2,1)}), bf16[136,16,200]{2,0,1:T(8,128)(2,1)S(1)}, u32[]{:S(2)}, u32[]{:S(2)}) async-start(bf16[136,16,200]{2,0,1:T(8,128)(2,1)} %copy.32), calls=%async_computation.1 | async-start | bytes 2228224 | tf_op jit(solution)/shard_map/all_to_all | solution.py:110
  578.4 96.8 %all-to-all-start.2 = ((bf16[8,2,256,800]{2,3,1,0:T(8,128)(2,1)}), bf16[8,2,256,800]{2,3,1,0:T(8,128)(2,1)}, u32[]{:S(2)}, u32[]{:S(2)}) async-start(bf16[8,2,256,800]{2,3,1,0:T(8,128)(2,1)} %broadcast_select_fusion), calls=%async_computation.2 | async-start | bytes 13107200 | tf_op jit(solution)/shard_map/all_to_all | solution.py:118
Sparse Core Ops, SparseCore 0:
  9.6 49.7 all-gather.7
  61.8 94.1 all-gather.11
  157.7 56.3 all-gather.5
  215.6 264.8 all-gather.9
where the time goes:
time: 727 us; the launch traced here: 718 us
  waiting for transfers between devices  468 us (64%)
  local copies, waits for them, and re-layouts  85.5 us (12%)
  blocking collectives  65.5 us (9%)
  matrix products  37.7 us (5%)
  other arithmetic  25.2 us (3%)
  starting transfers between devices  23 us (3%)
  between operations  13.6 us (2%)
    all_gather x1, waiting for transfers between devices, body(): weight_full = lax.all_gather(weight_rows, 'fsdp', axis=1, tiled=True)  162 us
    all_gather x1, waiting for transfers between devices, body(): gathered = lax.all_gather(own_rows, 'dp', axis=0, tiled=True)  95.9 us
    all_to_all x1, waiting for transfers between devices, body(): lax.all_to_all(outgoing, 'fsdp', split_axis=0, concat_axis=0, tiled=True)  91.6 us
    psum x1, blocking collectives, body(): lax.psum((jnp.sum(queries * queries, axis=-1), jnp.sum(keys_part * keys_p...  65.5 us
    all_gather x1, waiting for transfers between devices, body(): weight_rows = lax.all_gather(out_weight, 'dp', axis=0, tiled=True)  50.6 us
    all_gather x1, waiting for transfers between devices, body(): lax.all_gather(qkv_weight, 'fsdp', axis=0, tiled=True)  50.3 us
    all_gather x1, local copies, waits for them, and re-layouts, body(): weight_full = lax.all_gather(weight_rows, 'fsdp', axis=1, tiled=True)  17.2 us
    all_to_all x1, waiting for transfers between devices, body(): lax.all_to_all(token_update, 'dp', split_axis=1, concat_axis=0, tiled=True)  15.2 us
  transfers between devices with their start and end apart: 7, of which 6 were waited for; matrix products, arithmetic and copies ran while one was open for 8% of the time, Pallas kernels for 0%

commit v1 on v0

--- a/solution.py
+++ b/solution.py
@@ -95,19 +95,21 @@
         ],
         axis=0,
     )
-    token_heads = lax.all_to_all(head_out, "dp", split_axis=0, concat_axis=1, tiled=True)
-    weight_rows = lax.all_gather(out_weight, "dp", axis=0, tiled=True)
-    weight_full = lax.all_gather(weight_rows, "fsdp", axis=1, tiled=True)
-    rows_here = token_heads.shape[0]
+    dp_index = lax.axis_index("dp")
+    block = model_width // groups
+    head_rows = lax.all_gather(out_weight, "fsdp", axis=1, tiled=True)
+    weight_block = lax.all_to_all(head_rows, "dp", split_axis=1, concat_axis=0, tiled=True)
+    all_heads = lax.all_gather(head_out, "dp", axis=0, tiled=False)
     head_terms = jnp.einsum(
-        "shc,hcd->shd",
-        token_heads.reshape(rows_here, groups, HEAD_DIM),
-        weight_full.reshape(groups, HEAD_DIM, model_width),
+        "hsc,hcd->hsd",
+        all_heads,
+        weight_block.reshape(groups, HEAD_DIM, block),
         preferred_element_type=jnp.float32,
     ).astype(jnp.bfloat16)
-    attention = jnp.sum(lax.optimization_barrier(head_terms).astype(jnp.float32), axis=1)
-    token_update = (own_rows.astype(jnp.float32) + layer_scale * attention).astype(jnp.bfloat16)
-    updated = lax.all_to_all(token_update, "dp", split_axis=1, concat_axis=0, tiled=True)
+    attention = jnp.sum(lax.optimization_barrier(head_terms).astype(jnp.float32), axis=0)
+    own_block = lax.dynamic_slice_in_dim(gathered, dp_index * block, block, axis=1)
+    scale_block = lax.dynamic_slice_in_dim(layer_scale, dp_index * block, block)
+    updated = (own_block.astype(jnp.float32) + scale_block * attention).astype(jnp.bfloat16)
     merged = merge_tiles(updated)
     holder, living = tile_owners(tile_counts, owners)
     own_holder = holder[row_index]

time: 727 us -> 535 us (0.74)
  waiting for transfers between devices: 468 us -> 286 us
  blocking collectives: 65.5 us -> 96.6 us
  local copies, waits for them, and re-layouts: 85.5 us -> 59.9 us
  starting transfers between devices: 23 us -> 14.8 us
    all_gather x2 -> x1, waiting for transfers between devices: 213 us -> 32.3 us  [body(): all_heads = lax.all_gather(head_out, 'dp', axis=0, tiled=False)]
    all_gather x0 -> x1, blocking collectives: none -> 32.8 us  [body(): head_rows = lax.all_gather(out_weight, 'fsdp', axis=1, tiled=True)]
    all_gather x1 -> x0, local copies, waits for them, and re-layouts: 17.2 us -> none  [body(): weight_full = lax.all_gather(weight_rows, 'fsdp', axis=1, tiled=True)]
    all_to_all x2 -> x1, starting transfers between devices: 18.2 us -> 9.72 us  [body(): lax.all_to_all(head_rows, 'dp', split_axis=1, concat_axis=0, tiled=True)]
    all_to_all x2 -> x1, waiting for transfers between devices: 15.2 us -> 12 us  [body(): lax.all_to_all(head_rows, 'dp', split_axis=1, concat_axis=0, tiled=True)]
  transfers between devices with their start and end apart: 7 -> 5, of which waited for: 6 -> 5; matrix products, arithmetic and copies ran while one was open for 8% -> 2% of each run, Pallas kernels for 0% -> 0%
where the time goes in v1:
time: 535 us; the launch traced here: 528 us
  waiting for transfers between devices  286 us (53%)
  blocking collectives  96.6 us (18%)
  local copies, waits for them, and re-layouts  59.9 us (11%)
  matrix products  34.7 us (6%)
  other arithmetic  22 us (4%)
  starting transfers between devices  14.8 us (3%)
  between operations  13.8 us (3%)
    all_gather x1, waiting for transfers between devices, body(): gathered = lax.all_gather(own_rows, 'dp', axis=0, tiled=True)  98.7 us
    all_to_all x1, waiting for transfers between devices, body(): lax.all_to_all(outgoing, 'fsdp', split_axis=0, concat_axis=0, tiled=True)  91.5 us
    psum x1, blocking collectives, body(): lax.psum((jnp.sum(queries * queries, axis=-1), jnp.sum(keys_part * keys_p...  63.8 us
    all_gather x1, waiting for transfers between devices, body(): lax.all_gather(qkv_weight, 'fsdp', axis=0, tiled=True)  50.3 us
    all_gather x1, blocking collectives, body(): head_rows = lax.all_gather(out_weight, 'fsdp', axis=1, tiled=True)  32.8 us
    all_gather x1, waiting for transfers between devices, body(): all_heads = lax.all_gather(head_out, 'dp', axis=0, tiled=False)  32.3 us
    reshape x1, local copies, waits for them, and re-layouts, place_tiles(): flattened = received.reshape(received.shape[0] * received.shape[1], -1)  14.7 us
    all_to_all x1, waiting for transfers between devices, body(): lax.all_to_all(head_rows, 'dp', split_axis=1, concat_axis=0, tiled=True)  12 us
  transfers between devices with their start and end apart: 5, of which 5 were waited for; matrix products, arithmetic and copies ran while one was open for 2% of the time, Pallas kernels for 0%

profile of v1, /device:TPU:8, one launch (start us, length us, event | category | flops | bytes accessed | tf_op | source)
XLA Modules:
  0.0 528.1 jit_solution(8321030742287554255)
XLA Ops:
  8.8 98.7 %all-gather.8.cloned.1.call-done = bf16[1,2176,3200]{2,1,0:T(8,128)(2,1)} async-done(((bf16[1,136,3200]{2,1,0:T(8,128)(2,1)}), bf16[1,2176,3200]{2,1,0:T(8,128)(2,1)}) %all-gather.8.cloned.1.call-update) | async-done | bytes 13926416 | tf_op jit(solution)/shard_map/all_gather | solution.py:48
  107.5 7.7 %fusion.1 = f32[2176]{0:T(1024)S(1)} fusion(bf16[1,2176,3200]{2,1,0:T(8,128)(2,1)} %all-gather.8.cloned.1.call-done), kind=kLoop, calls=%fused_computation.4 | loop fusion | flops 20887424 | bytes 13935104 | tf_op jit(solution)/shard_map/reduce_sum | solution.py:54
  115.2 50.3 %all-gather.6.cloned.1.call-done = bf16[3200,384]{1,0:T(8,128)(2,1)} async-done(((bf16[400,384]{1,0:T(8,128)(2,1)}), bf16[3200,384]{1,0:T(8,128)(2,1)}) %all-gather.6.cloned.1.call-update) | async-done | bytes 2457616 | tf_op jit(solution)/shard_map/all_gather | solution.py:58
  165.5 11.8 %fusion.5 = f32[2176,384]{1,0:T(8,128)S(1)} fusion(bf16[3200,384]{1,0:T(8,128)(2,1)} %all-gather.6.cloned.1.call-done, bf16[1,2176,3200]{2,1,0:T(8,128)(2,1)} %all-gather.8.cloned.1.call-done, f32[3200]{0:T(1024)S(1)} %copy-done.4, f32[2176]{0:T(1024)S(1)} %add_rsqrt_fusion.2), kind=kOutput, calls=%fused_computation.11 | convolution fusion | flops 5375590400 | bytes 19747840 | tf_op jit(solution)/shard_map/dot_general | solution.py:56
  178.1 63.8 %all-reduce.1 = (f32[2176]{0:T(1024)S(1)}, f32[2176]{0:T(1024)S(1)}) all-reduce(f32[2176]{0:T(1024)S(1)} %get-tuple-element.6, f32[2176]{0:T(1024)S(1)} %get-tuple-element.5), channel_id=1, replica_groups=mesh['fsdp'=8,'dp'=16] {'dp'}, use_global_device_ids=true, to_apply=%region_3.0 | all-reduce | flops 4352 | bytes 34816 | tf_op jit(solution)/shard_map/psum | solution.py:64
  241.9 0.9 reshape.243
  242.8 1.1 fusion.15
  244.2 3.2 fusion.32
  247.5 4.9 fusion.12
  253.3 32.8 %all_gather.19 = bf16[128,3200]{0,1:T(8,128)(2,1)} all-gather(bf16[128,400]{0,1:T(8,128)(2,1)S(1)} %copy-done.1), channel_id=1, replica_groups=mesh['fsdp'=8,'dp'=16] {'fsdp'}, dimensions={1}, use_global_device_ids=true | all-gather | bytes 921600 | tf_op jit(solution)/shard_map/all_gather | solution.py:100
  286.1 9.7 %all-to-all-start = ((bf16[128,16,200]{0,2,1:T(8,128)(2,1)}), bf16[128,16,200]{0,2,1:T(8,128)(2,1)S(1)}, u32[]{:S(2)}, u32[]{:S(2)}) async-start(bf16[128,16,200]{0,2,1:T(8,128)(2,1)} %bitcast.12), calls=%async_computation | async-start | bytes 1638400 | tf_op jit(solution)/shard_map/all_to_all | solution.py:101
  296.9 2.5 constant_dynamic-slice_fusion
  300.1 12.0 %all-to-all-done = bf16[128,16,200]{0,2,1:T(8,128)(2,1)S(1)} async-done(((bf16[128,16,200]{0,2,1:T(8,128)(2,1)}), bf16[128,16,200]{0,2,1:T(8,128)(2,1)S(1)}, u32[]{:S(2)}, u32[]{:S(2)}) %all-to-all-start) | async-done | bytes 819232 | tf_op jit(solution)/shard_map/all_to_all | solution.py:101
  312.1 32.3 %all-gather.10.cloned.1.call-done = bf16[34816,128]{1,0:T(8,128)(2,1)} async-done(((bf16[2176,128]{1,0:T(8,128)(2,1)}), bf16[34816,128]{1,0:T(8,128)(2,1)}) %all-gather.10.cloned.1.call-update) | async-done | bytes 8912912 | tf_op jit(solution)/shard_map/all_gather | solution.py:102
  344.4 10.8 %convolution_convert_fusion.1 = bf16[16,2176,200]{1,2,0:T(8,128)(2,1)} fusion(bf16[16,2176,128]{2,1,0:T(8,128)(2,1)} %bitcast.53, bf16[128,16,200]{0,2,1:T(8,128)(2,1)S(1)} %all-to-all-done), kind=kOutput, calls=%fused_computation.8 | convolution fusion | flops 1789542400 | bytes 23658496 | tf_op jit(solution)/shard_map/hsc,hcd->hsd/dot_general | solution.py:103
  355.3 7.3 %convert_reduce_fusion = f32[2176,200]{0,1:T(8,128)S(1)} fusion(bf16[16,2176,200]{1,2,0:T(8,128)(2,1)} %convolution_convert_fusion.1), kind=kLoop, calls=%fused_computation.7 | loop fusion | flops 13491200 | bytes 15667200 | tf_op jit(solution)/shard_map/reduce_sum | solution.py:109
  363.4 1.0 reshape.245
  364.7 1.1 reshape.246
  365.8 4.9 copy.33
  370.6 3.9 stack_reshape.7
  374.5 4.9 copy.31
  379.4 3.8 stack_reshape.6
  383.2 1.2 pad_maximum_fusion
  384.4 3.3 broadcast_select_fusion
  387.8 5.0 all-to-all-start.1
  393.1 91.5 %all-to-all-done.1 = bf16[8,2,256,800]{2,3,1,0:T(8,128)(2,1)} async-done(((bf16[8,2,256,800]{2,3,1,0:T(8,128)(2,1)}), bf16[8,2,256,800]{2,3,1,0:T(8,128)(2,1)}, u32[]{:S(2)}, u32[]{:S(2)}) %all-to-all-start.1) | async-done | bytes 6553632 | tf_op jit(solution)/shard_map/all_to_all | solution.py:120
  484.6 11.1 %copy.34 = bf16[8,2,256,800]{3,2,1,0:T(8,128)(2,1)} copy(bf16[8,2,256,800]{2,3,1,0:T(8,128)(2,1)} %all-to-all-done.1) | data formatting | bytes 13107200 | tf_op jit(solution)/shard_map/all_to_all | solution.py:120
  495.6 14.7 %reshape.247 = bf16[16,204800]{1,0:T(8,128)(2,1)} reshape(bf16[8,2,256,800]{3,2,1,0:T(8,128)(2,1)} %copy.34) | data formatting | bytes 13107200 | tf_op jit(solution)/shard_map/reshape | solution.py:41
  510.4 4.0 convolution_convert_fusion
  514.3 1.6 reshape.258
  516.0 2.8 reshape.248
  518.8 2.3 copy.35
  (44 shorter events, 7.3 us)
Async XLA Ops:
  6.5 100.9 %all-gather.8.cloned.1.call-start = ((), (), s32[]{:S(2)}) async-start(), calls=%async_computation.3 | async-start | bytes 14796800 | tf_op jit(solution)/shard_map/all_gather | solution.py:48
  7.3 158.3 %all-gather.6.cloned.1.call-start = ((), (), s32[]{:S(2)}) async-start(), calls=%async_computation.2 | async-start | bytes 2764800 | tf_op jit(solution)/shard_map/all_gather | solution.py:58
  8.0 336.4 %all-gather.10.cloned.1.call-start = ((), (), s32[]{:S(2)}) async-start(), calls=%async_computation.4 | async-start | bytes 9469952 | tf_op jit(solution)/shard_map/all_gather | solution.py:102
  8.8 156.7 %copy-start.4 = (f32[3200]{0:T(1024)S(1)}, f32[3200]{0:T(1024)}, u32[]{:S(2)}) copy-start(f32[3200]{0:T(1024)} %param.9) | copy-start | bytes 38404
  244.1 3.4 copy-start
  247.4 5.9 %copy-start.1 = (bf16[128,400]{0,1:T(8,128)(2,1)S(1)}, bf16[128,400]{0,1:T(8,128)(2,1)}, u32[]{:S(2)}) copy-start(bf16[128,400]{0,1:T(8,128)(2,1)} %param.12) | copy-start | bytes 307204
  247.5 48.4 %copy-start.2 = (s32[8,2]{0,1:T(2,128)S(1)}, s32[8,2]{0,1:T(2,128)}, u32[]{:S(2)}) copy-start(s32[8,2]{0,1:T(2,128)} %param.15) | copy-start | bytes 196
  247.5 48.4 %copy-start.3 = (s32[8,2]{0,1:T(2,128)S(1)}, s32[8,2]{0,1:T(2,128)}, u32[]{:S(2)}) copy-start(s32[8,2]{0,1:T(2,128)} %param.14) | copy-start | bytes 196
  286.1 26.0 %all-to-all-start = ((bf16[128,16,200]{0,2,1:T(8,128)(2,1)}), bf16[128,16,200]{0,2,1:T(8,128)(2,1)S(1)}, u32[]{:S(2)}, u32[]{:S(2)}) async-start(bf16[128,16,200]{0,2,1:T(8,128)(2,1)} %bitcast.12), calls=%async_computation | async-start | bytes 1638400 | tf_op jit(solution)/shard_map/all_to_all | solution.py:101
  387.8 96.8 %all-to-all-start.1 = ((bf16[8,2,256,800]{2,3,1,0:T(8,128)(2,1)}), bf16[8,2,256,800]{2,3,1,0:T(8,128)(2,1)}, u32[]{:S(2)}, u32[]{:S(2)}) async-start(bf16[8,2,256,800]{2,3,1,0:T(8,128)(2,1)} %broadcast_select_fusion), calls=%async_computation.1 | async-start | bytes 13107200 | tf_op jit(solution)/shard_map/all_to_all | solution.py:120
Sparse Core Ops, SparseCore 0:
  9.8 97.6 all-gather.7
  109.1 56.3 all-gather.5
  253.4 90.9 all-gather.9

commit v2 on v1

--- a/solution.py
+++ b/solution.py
@@ -35,20 +35,34 @@
 def place_tiles(received, holder, living, target):
     owned_flag = jnp.logical_and(living, holder == target).reshape(-1).astype(jnp.int32)
     before = jnp.cumsum(owned_flag) - owned_flag
-    chosen = jnp.logical_and(
-        before[None, :] == jnp.arange(CAP, dtype=jnp.int32)[:, None], owned_flag[None, :] == 1
-    )
-    flattened = received.reshape(received.shape[0] * received.shape[1], -1)
-    placed = jnp.dot(chosen.astype(jnp.bfloat16), flattened, preferred_element_type=jnp.float32)
-    return placed.astype(jnp.bfloat16).reshape(CAP, received.shape[2], received.shape[3])
+    flattened = received.reshape((received.shape[0] * received.shape[1],) + received.shape[2:])
+    sources = jnp.arange(flattened.shape[0], dtype=jnp.int32)
+    placed = []
+    for slot in range(CAP):
+        match = jnp.logical_and(before == slot, owned_flag == 1)
+        source = jnp.max(jnp.where(match, sources, 0))
+        tile = lax.dynamic_index_in_dim(flattened, source, axis=0, keepdims=False)
+        placed.append(jnp.where(jnp.any(match), tile, jnp.zeros((), tile.dtype)))
+    return jnp.stack(placed)
+
+
+def gather_sum(values, axis_name, groups):
+    spread = jnp.broadcast_to(values[None], (groups,) + values.shape)
+    collected = lax.all_to_all(spread, axis_name, split_axis=0, concat_axis=0, tiled=True)
+    return jnp.sum(collected, axis=0)
 
 
 def body(tokens, norm_gain, qkv_weight, qk_gain, out_weight, layer_scale, tile_counts, owners):
     own_rows = tokens[0]
+    groups = lax.axis_size("dp")
+    dp_index = lax.axis_index("dp")
+    model_width = own_rows.shape[1]
+    block = model_width // groups
+    head_rows = lax.all_gather(out_weight, "fsdp", axis=1, tiled=True)
+    weight_block = lax.all_to_all(head_rows, "dp", split_axis=1, concat_axis=0, tiled=True)
     gathered = lax.all_gather(own_rows, "dp", axis=0, tiled=True)
+    gathered, weight_block = lax.optimization_barrier((gathered, weight_block))
     length = gathered.shape[0]
-    model_width = gathered.shape[1]
-    groups = lax.axis_size("dp")
     values = gathered.astype(jnp.float32)
     normed = (
         values * lax.rsqrt(jnp.mean(values * values, axis=-1, keepdims=True) + EPSILON) * norm_gain
@@ -61,9 +75,13 @@
     queries = projected[:, :HEAD_DIM]
     keys_part = projected[:, HEAD_DIM : 2 * HEAD_DIM]
     values_part = projected[:, 2 * HEAD_DIM :].astype(jnp.bfloat16)
-    query_sums, key_sums = lax.psum(
-        (jnp.sum(queries * queries, axis=-1), jnp.sum(keys_part * keys_part, axis=-1)), "dp"
+    sums = gather_sum(
+        jnp.stack([jnp.sum(queries * queries, axis=-1), jnp.sum(keys_part * keys_part, axis=-1)]),
+        "dp",
+        groups,
     )
+    query_sums = sums[0]
+    key_sums = sums[1]
     window = groups * HEAD_DIM
     queries = (queries * lax.rsqrt(query_sums / window + EPSILON)[:, None] * qk_gain[0]).astype(
         jnp.bfloat16
@@ -95,10 +113,6 @@
         ],
         axis=0,
     )
-    dp_index = lax.axis_index("dp")
-    block = model_width // groups
-    head_rows = lax.all_gather(out_weight, "fsdp", axis=1, tiled=True)
-    weight_block = lax.all_to_all(head_rows, "dp", split_axis=1, concat_axis=0, tiled=True)
     all_heads = lax.all_gather(head_out, "dp", axis=0, tiled=False)
     head_terms = jnp.einsum(
         "hsc,hcd->hsd",

time: 535 us -> 451 us (0.84)
  blocking collectives: 96.6 us -> 52.5 us
  waiting for transfers between devices: 286 us -> 248 us
  other arithmetic: 22 us -> 31.6 us
  local copies, waits for them, and re-layouts: 59.9 us -> 51.9 us
  between operations: 13.8 us -> 21 us
    psum x1 -> x0, blocking collectives: 63.8 us -> none  [body(): lax.psum((jnp.sum(queries * queries, axis=-1), jnp.sum(keys_part * keys_p...]
    all_gather x1, waiting for transfers between devices: 98.7 us -> 58 us  [body(): gathered = lax.all_gather(own_rows, 'dp', axis=0, tiled=True)]
    all_gather x1, waiting for transfers between devices: 32.3 us -> 72.4 us  [body(): all_heads = lax.all_gather(head_out, 'dp', axis=0, tiled=False)]
    all_to_all x0 -> x1, blocking collectives: none -> 20.2 us  [body(): lax.all_to_all(head_rows, 'dp', split_axis=1, concat_axis=0, tiled=True)]
    reshape x3 -> x0, local copies, waits for them, and re-layouts: 19.8 us -> none  [the longest x1 14.7 us: place_tiles(): flattened = received.reshape(received.shape[0] * received.shape[1], -1)]
    all_gather x1, waiting for transfers between devices: 50.3 us -> 31.3 us  [body(): lax.all_gather(qkv_weight, 'fsdp', axis=0, tiled=True)]
    all_gather x0 -> x1, local copies, waits for them, and re-layouts: none -> 19 us  [body(): gathered = lax.all_gather(own_rows, 'dp', axis=0, tiled=True)]
    all_to_all x1, local copies, waits for them, and re-layouts: 11.1 us -> 0.09 us  [body(): lax.all_to_all(head_rows, 'dp', split_axis=1, concat_axis=0, tiled=True)]
  transfers between devices with their start and end apart: 5 -> 5, of which waited for: 5 -> 5; matrix products, arithmetic and copies ran while one was open for 2% -> 8% of each run, Pallas kernels for 0% -> 0%
where the time goes in v2:
time: 451 us; the launch traced here: 448 us
  waiting for transfers between devices  248 us (55%)
  blocking collectives  52.5 us (12%)
  local copies, waits for them, and re-layouts  51.9 us (12%)
  other arithmetic  31.6 us (7%)
  matrix products  31.1 us (7%)
  between operations  21 us (5%)
  starting transfers between devices  12.4 us (3%)
    all_to_all x1, waiting for transfers between devices, body(): lax.all_to_all(outgoing, 'fsdp', split_axis=0, concat_axis=0, tiled=True)  81.7 us
    all_gather x1, waiting for transfers between devices, body(): all_heads = lax.all_gather(head_out, 'dp', axis=0, tiled=False)  72.4 us
    all_gather x1, waiting for transfers between devices, body(): gathered = lax.all_gather(own_rows, 'dp', axis=0, tiled=True)  58 us
    all_gather x1, blocking collectives, body(): head_rows = lax.all_gather(out_weight, 'fsdp', axis=1, tiled=True)  32.3 us
    all_gather x1, waiting for transfers between devices, body(): lax.all_gather(qkv_weight, 'fsdp', axis=0, tiled=True)  31.3 us
    all_to_all x1, blocking collectives, body(): lax.all_to_all(head_rows, 'dp', split_axis=1, concat_axis=0, tiled=True)  20.2 us
    all_gather x1, local copies, waits for them, and re-layouts, body(): gathered = lax.all_gather(own_rows, 'dp', axis=0, tiled=True)  19 us
    dot_general x1, matrix products, body(): jnp.dot(normed, lax.all_gather(qkv_weight, 'fsdp', axis=0, tiled=True), p...  12.2 us
  transfers between devices with their start and end apart: 5, of which 5 were waited for; matrix products, arithmetic and copies ran while one was open for 8% of the time, Pallas kernels for 0%

profile of v2, /device:TPU:8, one launch (start us, length us, event | category | flops | bytes accessed | tf_op | source)
XLA Modules:
  0.0 448.1 jit_solution(17744004390682438390)
XLA Ops:
  8.0 32.3 %all_gather.16 = bf16[128,3200]{0,1:T(8,128)(2,1)S(1)} all-gather(bf16[128,400]{0,1:T(8,128)(2,1)} %param.12), channel_id=1, replica_groups=mesh['fsdp'=8,'dp'=16] {'fsdp'}, dimensions={1}, use_global_device_ids=true | all-gather | bytes 921600 | tf_op jit(solution)/shard_map/all_gather | solution.py:61
  40.3 20.2 %all_to_all.29 = bf16[128,16,200]{0,2,1:T(8,128)(2,1)S(1)} all-to-all(bf16[128,16,200]{0,2,1:T(8,128)(2,1)S(1)} %bitcast.56), channel_id=1, replica_groups=mesh['fsdp'=8,'dp'=16] {'dp'}, dimensions={1} | all-to-all | bytes 1638400 | tf_op jit(solution)/shard_map/all_to_all | solution.py:62
  60.6 58.0 %all-gather.8.cloned.1.call-done = bf16[1,2176,3200]{2,1,0:T(8,128)(2,1)} async-done(((bf16[1,136,3200]{2,1,0:T(8,128)(2,1)}), bf16[1,2176,3200]{2,1,0:T(8,128)(2,1)}) %all-gather.8.cloned.1.call-update) | async-done | bytes 13926416 | tf_op jit(solution)/shard_map/all_gather | solution.py:63
  118.6 19.0 %copy.45 = bf16[1,2176,3200]{1,2,0:T(8,128)(2,1)} copy(bf16[1,2176,3200]{2,1,0:T(8,128)(2,1)} %all-gather.8.cloned.1.call-done) | data formatting | bytes 27852800 | tf_op jit(solution)/shard_map/all_gather | solution.py:63
  137.6 7.8 %fusion.1 = f32[2176]{0:T(1024)S(1)} fusion(bf16[2176,3200]{0,1:T(8,128)(2,1)} %bitcast.52), kind=kLoop, calls=%fused_computation.3 | loop fusion | flops 20887424 | bytes 13935104 | tf_op jit(solution)/shard_map/reduce_sum | solution.py:68
  145.4 31.3 %all-gather.6.cloned.1.call-done = bf16[3200,384]{1,0:T(8,128)(2,1)} async-done(((bf16[400,384]{1,0:T(8,128)(2,1)}), bf16[3200,384]{1,0:T(8,128)(2,1)}) %all-gather.6.cloned.1.call-update) | async-done | bytes 2457616 | tf_op jit(solution)/shard_map/all_gather | solution.py:72
  176.7 12.2 %fusion.5 = f32[2176,384]{1,0:T(8,128)S(1)} fusion(bf16[3200,384]{1,0:T(8,128)(2,1)} %all-gather.6.cloned.1.call-done, bf16[2176,3200]{0,1:T(8,128)(2,1)} %bitcast.53, f32[3200]{0:T(1024)S(1)} %copy-done.5, f32[2176]{0:T(1024)S(1)} %add_rsqrt_fusion), kind=kOutput, calls=%fused_computation.10 | convolution fusion | flops 5375590400 | bytes 19747840 | tf_op jit(solution)/shard_map/dot_general | solution.py:70
  188.9 1.7 copy-done
  192.1 7.4 %all-to-all-start.1 = ((f32[16,2,2176]{2,1,0:T(2,128)}), f32[16,2,2176]{2,1,0:T(2,128)S(1)}, u32[]{:S(2)}, u32[]{:S(2)}) async-start(f32[16,2,2176]{2,1,0:T(2,128)} %broadcast_in_dim.75), calls=%async_computation.1 | async-start | bytes 557056 | tf_op jit(solution)/shard_map/all_to_all | solution.py:51
  199.8 2.1 slice.108
  201.9 1.9 reshape.201
  203.8 2.7 all-to-all-done.1
  206.6 2.0 fusion.13
  208.6 1.1 reshape.199
  209.8 1.2 reshape.200
  211.0 3.2 fusion.37
  214.3 4.8 %fusion.11 = bf16[2,1025,128]{2,1,0:T(8,128)(2,1)S(1)} fusion(bf16[2,1025,128]{2,1,0:T(8,128)(2,1)S(1)} %copy-done.1, f32[2,1025]{1,0:T(2,128)S(1)} %fusion.37, bf16[2,1025,128]{2,1,0:T(8,128)(2,1)S(1)} %reshape.199, bf16[2,1025,128]{2,1,0:T(8,128)(2,1)S(1)} %reshape.200), kind=kOutput, calls=%fused_computation.17 | convolution fusion | flops 1084510464 | bytes 2107400 | tf_op jit(solution)/shard_map/sqk,skc->sqc/dot_general | solution.py:106
  221.1 72.4 %all-gather.10.cloned.1.call-done = bf16[34816,128]{1,0:T(8,128)(2,1)} async-done(((bf16[2176,128]{1,0:T(8,128)(2,1)}), bf16[34816,128]{1,0:T(8,128)(2,1)}) %all-gather.10.cloned.1.call-update) | async-done | bytes 8912912 | tf_op jit(solution)/shard_map/all_gather | solution.py:116
  293.5 10.8 %convolution_convert_fusion = bf16[16,2176,200]{1,2,0:T(8,128)(2,1)} fusion(bf16[16,2176,128]{2,1,0:T(8,128)(2,1)} %bitcast.55, bf16[2048,200]{0,1:T(8,128)(2,1)S(1)} %copy_bitcast_fusion), kind=kOutput, calls=%fused_computation.7 | convolution fusion | flops 1789542400 | bytes 23658496 | tf_op jit(solution)/shard_map/hsc,hcd->hsd/dot_general | solution.py:117
  304.3 7.3 %convert_reduce_fusion = f32[2176,200]{0,1:T(8,128)S(1)} fusion(bf16[16,2176,200]{1,2,0:T(8,128)(2,1)} %convolution_convert_fusion), kind=kLoop, calls=%fused_computation.6 | loop fusion | flops 13491200 | bytes 15667200 | tf_op jit(solution)/shard_map/reduce_sum | solution.py:123
  311.6 1.4 add_convert_fusion
  315.4 4.9 %copy.51 = bf16[16,16,200,2,2]{1,0,4,3,2:T(8,128)(2,1)S(1)} copy(bf16[16,16,200,2,2]{2,4,1,3,0:T(2,128)(2,1)} %bitcast.57) | data formatting | bytes 819200 | tf_op jit(solution)/shard_map/transpose | solution.py:22
  320.3 3.8 stack_reshape.6
  324.2 1.2 copy.52
  326.4 4.9 %copy.53 = bf16[16,16,200,2,2]{1,0,4,3,2:T(8,128)(2,1)S(1)} copy(bf16[16,16,200,2,2]{2,4,1,3,0:T(2,128)(2,1)} %bitcast.58) | data formatting | bytes 819200 | tf_op jit(solution)/shard_map/transpose | solution.py:22
  331.3 3.9 stack_reshape.7
  335.1 1.2 pad_maximum_fusion.1
  336.4 3.3 broadcast_select_fusion
  339.7 4.8 %all-to-all-start.2 = ((bf16[8,2,256,800]{2,3,1,0:T(8,128)(2,1)}), bf16[8,2,256,800]{2,3,1,0:T(8,128)(2,1)}, u32[]{:S(2)}, u32[]{:S(2)}) async-start(bf16[8,2,256,800]{2,3,1,0:T(8,128)(2,1)} %broadcast_select_fusion), calls=%async_computation.2 | async-start | bytes 13107200 | tf_op jit(solution)/shard_map/all_to_all | solution.py:134
  354.5 81.7 %all-to-all-done.2 = bf16[8,2,256,800]{2,3,1,0:T(8,128)(2,1)} async-done(((bf16[8,2,256,800]{2,3,1,0:T(8,128)(2,1)}), bf16[8,2,256,800]{2,3,1,0:T(8,128)(2,1)}, u32[]{:S(2)}, u32[]{:S(2)}) %all-to-all-start.2) | async-done | bytes 6553632 | tf_op jit(solution)/shard_map/all_to_all | solution.py:134
  436.2 3.9 dynamic-slice_select_fusion.3
  440.2 1.4 pad_maximum_fusion
  (48 shorter events, 11.1 us)
Async XLA Ops:
  6.5 112.0 %all-gather.8.cloned.1.call-start = ((), (), s32[]{:S(2)}) async-start(), calls=%async_computation.4 | async-start | bytes 14796800 | tf_op jit(solution)/shard_map/all_gather | solution.py:63
  7.3 169.4 %all-gather.6.cloned.1.call-start = ((), (), s32[]{:S(2)}) async-start(), calls=%async_computation.3 | async-start | bytes 2764800 | tf_op jit(solution)/shard_map/all_gather | solution.py:72
  137.6 39.1 %copy-start.5 = (f32[3200]{0:T(1024)S(1)}, f32[3200]{0:T(1024)}, u32[]{:S(2)}) copy-start(f32[3200]{0:T(1024)} %param.9) | copy-start | bytes 38404
  145.4 54.4 %copy-start.2 = (f32[2,128]{1,0:T(2,128)S(1)}, f32[2,128]{1,0:T(2,128)}, u32[]{:S(2)}) copy-start(f32[2,128]{1,0:T(2,128)} %param.11) | copy-start | bytes 3076
  188.9 1.7 copy-start
  192.1 14.4 %all-to-all-start.1 = ((f32[16,2,2176]{2,1,0:T(2,128)}), f32[16,2,2176]{2,1,0:T(2,128)S(1)}, u32[]{:S(2)}, u32[]{:S(2)}) async-start(f32[16,2,2176]{2,1,0:T(2,128)} %broadcast_in_dim.75), calls=%async_computation.1 | async-start | bytes 557056 | tf_op jit(solution)/shard_map/all_to_all | solution.py:51
  199.5 94.0 %all-gather.10.cloned.1.call-start = ((), (), s32[]{:S(2)}) async-start(), calls=%async_computation.5 | async-start | bytes 9469952 | tf_op jit(solution)/shard_map/all_gather | solution.py:116
  209.8 4.5 copy-start.1
  214.2 6.6 %copy-start.3 = (s32[8,2]{0,1:T(2,128)S(1)}, s32[8,2]{0,1:T(2,128)}, u32[]{:S(2)}) copy-start(s32[8,2]{0,1:T(2,128)} %param.14) | copy-start | bytes 196
  214.3 6.6 %copy-start.4 = (s32[8,2]{0,1:T(2,128)S(1)}, s32[8,2]{0,1:T(2,128)}, u32[]{:S(2)}) copy-start(s32[8,2]{0,1:T(2,128)} %param.15) | copy-start | bytes 196
  339.7 96.6 %all-to-all-start.2 = ((bf16[8,2,256,800]{2,3,1,0:T(8,128)(2,1)}), bf16[8,2,256,800]{2,3,1,0:T(8,128)(2,1)}, u32[]{:S(2)}, u32[]{:S(2)}) async-start(bf16[8,2,256,800]{2,3,1,0:T(8,128)(2,1)} %broadcast_select_fusion), calls=%async_computation.2 | async-start | bytes 13107200 | tf_op jit(solution)/shard_map/all_to_all | solution.py:134
Sparse Core Ops, SparseCore 0:
  9.8 108.7 all-gather.7
  120.2 56.3 all-gather.5
  220.2 73.2 all-gather.9

commit v3 on v2

v3 whole, which is shorter than its diff:
```python
import jax
import jax.numpy as jnp
from jax import lax
from jax.sharding import PartitionSpec as P

HEAD_DIM = 128
GRID = 32
SLOTS = 2
TILE = 1025
CAP = 4


EPSILON = 1e-06


def merge_tiles(values):
    halves = GRID // 2
    columns = values.shape[1]
    tile_list = []
    for tile_slot in range(SLOTS):
        patches = values[tile_slot * TILE + 1 : (tile_slot + 1) * TILE]
        square = patches.reshape(halves, 2, halves, 2, columns).transpose(0, 2, 4, 1, 3)
        tile_list.append(square.reshape(halves * halves, columns * 4))
    return jnp.stack(tile_list)


def tile_owners(tile_counts, owners):
    slot_index = jnp.arange(SLOTS, dtype=jnp.int32)[None, :]
    first_count = tile_counts[:, 0:1]
    holder = jnp.where(slot_index < first_count, owners[:, 0:1], owners[:, 1:2])
    living = slot_index < first_count + tile_counts[:, 1:2]
    return (holder, living)


def place_tiles(received, holder, living, target):
    owned_flag = jnp.logical_and(living, holder == target).reshape(-1).astype(jnp.int32)
    before = jnp.cumsum(owned_flag) - owned_flag
    flattened = received.reshape((received.shape[0] * received.shape[1],) + received.shape[2:])
    sources = jnp.arange(flattened.shape[0], dtype=jnp.int32)
    placed = []
    for slot in range(CAP):
        match = jnp.logical_and(before == slot, owned_flag == 1)
        source = jnp.max(jnp.where(match, sources, 0))
        tile = lax.dynamic_index_in_dim(flattened, source, axis=0, keepdims=False)
        placed.append(jnp.where(jnp.any(match), tile, jnp.zeros((), tile.dtype)))
    return jnp.stack(placed)


def gather_sum(values, axis_name, groups):
    spread = jnp.broadcast_to(values[None], (groups,) + values.shape)
    collected = lax.all_to_all(spread, axis_name, split_axis=0, concat_axis=0, tiled=True)
    return jnp.sum(collected, axis=0)


def gather_blocks(block_value, axis_name, groups):
    spread = jnp.broadcast_to(block_value[None], (groups,) + block_value.shape)
    collected = lax.all_to_all(spread, axis_name, split_axis=0, concat_axis=0, tiled=True)
    return collected.reshape((groups * block_value.shape[0],) + block_value.shape[1:])


def body(tokens, norm_gain, qkv_weight, qk_gain, out_weight, layer_scale, tile_counts, owners):
    own_rows = tokens[0]
    groups = lax.axis_size("dp")
    dp_index = lax.axis_index("dp")
    row_index = lax.axis_index("fsdp")
    row_count = lax.axis_size("fsdp")
    model_width = own_rows.shape[1]
    block = model_width // groups
    head_rows = lax.all_gather(out_weight, "fsdp", axis=1, tiled=True)
    weight_block = lax.all_to_all(head_rows, "dp", split_axis=1, concat_axis=0, tiled=True)
    full_qkv = gather_blocks(qkv_weight, "fsdp", row_count)
    full_qkv, weight_block = lax.optimization_barrier((full_qkv, weight_block))
    gathered = lax.all_gather(own_rows, "dp", axis=0, tiled=True)
    values = gathered.astype(jnp.float32)
    normed = (
        values * lax.rsqrt(jnp.mean(values * values, axis=-1, keepdims=True) + EPSILON) * norm_gain
    ).astype(jnp.bfloat16)
    projected = jnp.dot(normed, full_qkv, preferred_element_type=jnp.float32)
    queries = projected[:, :HEAD_DIM]
    keys_part = projected[:, HEAD_DIM : 2 * HEAD_DIM]
    values_part = projected[:, 2 * HEAD_DIM :].astype(jnp.bfloat16)
    sums = gather_sum(
        jnp.stack([jnp.sum(queries * queries, axis=-1), jnp.sum(keys_part * keys_part, axis=-1)]),
        "dp",
        groups,
    )
    window = groups * HEAD_DIM
    queries = (queries * lax.rsqrt(sums[0] / window + EPSILON)[:, None] * qk_gain[0]).astype(
        jnp.bfloat16
    )
    keys_part = (keys_part * lax.rsqrt(sums[1] / window + EPSILON)[:, None] * qk_gain[1]).astype(
        jnp.bfloat16
    )
    factor = HEAD_DIM ** (-0.5)
    own_block = lax.dynamic_slice_in_dim(gathered, dp_index * block, block, axis=1)
    scale_block = lax.dynamic_slice_in_dim(layer_scale, dp_index * block, block)
    holder, living = tile_owners(tile_counts, owners)
    own_holder = holder[row_index]
    own_living = living[row_index]
    destination = jnp.arange(row_count, dtype=jnp.int32)[:, None]
    sending = jnp.logical_and(destination == own_holder[None, :], own_living[None, :])
    halves = GRID // 2
    slot_received = []
    for tile_slot in range(SLOTS):
        first = tile_slot * TILE
        tile_query = queries[first : first + TILE]
        tile_key = keys_part[first : first + TILE]
        tile_value = values_part[first : first + TILE]
        scores = jnp.dot(tile_query[1:], tile_key.T, preferred_element_type=jnp.float32) * factor
        highest = jnp.max(scores, axis=-1, keepdims=True)
        exponent = jnp.exp(scores - highest)
        weights = (exponent / jnp.sum(exponent, axis=-1, keepdims=True)).astype(jnp.bfloat16)
        tile_out = jnp.dot(weights, tile_value, preferred_element_type=jnp.float32).astype(
            jnp.bfloat16
        )
        all_heads = lax.all_gather(tile_out, "dp", axis=0, tiled=False)
        head_terms = jnp.einsum(
            "hsc,hcd->hsd",
            all_heads,
            weight_block.reshape(groups, HEAD_DIM, block),
            preferred_element_type=jnp.float32,
        ).astype(jnp.bfloat16)
        attention = jnp.sum(lax.optimization_barrier(head_terms).astype(jnp.float32), axis=0)
        patches = own_block[first + 1 : first + TILE]
        updated = (patches.astype(jnp.float32) + scale_block * attention).astype(jnp.bfloat16)
        square = updated.reshape(halves, 2, halves, 2, block).transpose(0, 2, 4, 1, 3)
        merged = square.reshape(halves * halves, block * 4)
        outgoing = jnp.where(
            sending[:, tile_slot, None, None], merged[None], jnp.zeros((), jnp.bfloat16)
        )
        slot_received.append(
            lax.all_to_all(outgoing, "fsdp", split_axis=0, concat_axis=0, tiled=True)
        )
    received = jnp.stack(slot_received, axis=1)
    return place_tiles(received, holder, living, row_index)


def solution(mesh):
    placed = (
        P("fsdp", "dp", None),
        P(),
        P("fsdp", "dp"),
        P(None, "dp"),
        P("dp", "fsdp"),
        P(),
        P(),
        P(),
    )
    return jax.shard_map(
        body, mesh=mesh, in_specs=placed, out_specs=P("fsdp", None, "dp"), check_vma=False
    )
```

time: 451 us -> 442 us (0.980)
  local copies, waits for them, and re-layouts: 51.9 us -> 34.4 us
  starting transfers between devices: 12.4 us -> 18.7 us
    all_to_all x0 -> x1, waiting for transfers between devices: none -> 37.4 us  [gather_blocks(): lax.all_to_all(spread, axis_name, split_axis=0, concat_axis=0, tiled=True)]
    all_gather x1 -> x0, local copies, waits for them, and re-layouts: 19 us -> none  [body(): gathered = lax.all_gather(own_rows, 'dp', axis=0, tiled=True)]
    all_gather x1, waiting for transfers between devices: 58 us -> 40 us  [body(): gathered = lax.all_gather(own_rows, 'dp', axis=0, tiled=True)]
    all_to_all x1 -> x2, waiting for transfers between devices: 81.7 us -> 65.5 us  [body(): lax.all_to_all(outgoing, 'fsdp', split_axis=0, concat_axis=0, tiled=True)]
    broadcast_in_dim x1 -> x4, local copies, waits for them, and re-layouts: 0.01 us -> 11.9 us  [the longest x3 9.08 us: body(): jnp.where(sending[:, tile_slot, None, None], merged[None], jnp.zeros((),...]
    another operation x2 -> x0, local copies, waits for them, and re-layouts: 7.69 us -> none  [merge_tiles(): return jnp.stack(tile_list)]
    all_gather x2, waiting for transfers between devices: 104 us -> 96.2 us  [body(): all_heads = lax.all_gather(tile_out, 'dp', axis=0, tiled=False)]
    dot_general x2 -> x5, matrix products: 17.1 us -> 19.7 us  [the longest x1 12.8 us: body(): projected = jnp.dot(normed, full_qkv, preferred_element_type=jnp.float32)]
  transfers between devices with their start and end apart: 5 -> 7, of which waited for: 5 -> 7; matrix products, arithmetic and copies ran while one was open for 8% -> 9% of each run, Pallas kernels for 0% -> 0%
where the time goes in v3:
time: 442 us; the launch traced here: 440 us
  waiting for transfers between devices  247 us (56%)
  blocking collectives  52.5 us (12%)
  other arithmetic  34.8 us (8%)
  local copies, waits for them, and re-layouts  34.4 us (8%)
  matrix products  32.6 us (7%)
  between operations  20.7 us (5%)
  starting transfers between devices  18.7 us (4%)
    all_gather x2, waiting for transfers between devices, body(): all_heads = lax.all_gather(tile_out, 'dp', axis=0, tiled=False)  96.2 us
    all_to_all x2, waiting for transfers between devices, body(): lax.all_to_all(outgoing, 'fsdp', split_axis=0, concat_axis=0, tiled=True)  65.5 us
    all_gather x1, waiting for transfers between devices, body(): gathered = lax.all_gather(own_rows, 'dp', axis=0, tiled=True)  40 us
    all_to_all x1, waiting for transfers between devices, gather_blocks(): lax.all_to_all(spread, axis_name, split_axis=0, concat_axis=0, tiled=True)  37.4 us
    all_gather x1, blocking collectives, body(): head_rows = lax.all_gather(out_weight, 'fsdp', axis=1, tiled=True)  31.9 us
    all_to_all x1, blocking collectives, body(): lax.all_to_all(head_rows, 'dp', split_axis=1, concat_axis=0, tiled=True)  20.6 us
    dot_general x2, matrix products, body(): jnp.einsum('hsc,hcd->hsd', all_heads, weight_block.reshape(groups, HEAD_D...  13 us
    dot_general x1, matrix products, body(): projected = jnp.dot(normed, full_qkv, preferred_element_type=jnp.float32)  12.8 us
  transfers between devices with their start and end apart: 7, of which 7 were waited for; matrix products, arithmetic and copies ran while one was open for 9% of the time, Pallas kernels for 0%

profile of v3, /device:TPU:8, one launch (start us, length us, event | category | flops | bytes accessed | tf_op | source)
XLA Modules:
  0.0 440.4 jit_solution(10808765699950452176)
XLA Ops:
  7.3 31.9 %all_gather.19 = bf16[128,3200]{0,1:T(8,128)(2,1)S(1)} all-gather(bf16[128,400]{0,1:T(8,128)(2,1)} %param.12), channel_id=1, replica_groups=mesh['fsdp'=8,'dp'=16] {'fsdp'}, dimensions={1}, use_global_device_ids=true | all-gather | bytes 921600 | tf_op jit(solution)/shard_map/all_gather | solution.py:69
  39.1 20.6 %all_to_all.39 = bf16[128,16,200]{0,2,1:T(8,128)(2,1)S(1)} all-to-all(bf16[128,16,200]{0,2,1:T(8,128)(2,1)S(1)} %bitcast.79), channel_id=1, replica_groups=mesh['fsdp'=8,'dp'=16] {'dp'}, dimensions={1} | all-to-all | bytes 1638400 | tf_op jit(solution)/shard_map/all_to_all | solution.py:70
  59.7 2.8 broadcast_in_dim.101
  62.6 4.4 all-to-all-start
  67.0 37.4 %all-to-all-done = bf16[8,400,384]{2,1,0:T(8,128)(2,1)} async-done(((bf16[8,400,384]{2,1,0:T(8,128)(2,1)}), bf16[8,400,384]{2,1,0:T(8,128)(2,1)}, u32[]{:S(2)}, u32[]{:S(2)}) %all-to-all-start) | async-done | bytes 2457632 | tf_op jit(solution)/shard_map/all_to_all | solution.py:57
  104.4 40.0 %all-gather.7.cloned.1.call-done = bf16[1,2176,3200]{2,1,0:T(8,128)(2,1)} async-done(((bf16[1,136,3200]{2,1,0:T(8,128)(2,1)}), bf16[1,2176,3200]{2,1,0:T(8,128)(2,1)}) %all-gather.7.cloned.1.call-update) | async-done | bytes 13926416 | tf_op jit(solution)/shard_map/all_gather | solution.py:73
  144.4 7.7 %fusion = f32[2176]{0:T(1024)S(1)} fusion(bf16[1,2176,3200]{2,1,0:T(8,128)(2,1)} %all-gather.7.cloned.1.call-done), kind=kLoop, calls=%fused_computation.2 | loop fusion | flops 20887424 | bytes 13935104 | tf_op jit(solution)/shard_map/reduce_sum | solution.py:76
  152.2 12.8 %fusion.40 = (bf16[2176,384]{1,0:T(8,128)(2,1)}, f32[2176,384]{1,0:T(8,128)S(1)}) fusion(bf16[3200,384]{1,0:T(8,128)(2,1)} %bitcast.10, bf16[1,2176,3200]{2,1,0:T(8,128)(2,1)} %all-gather.7.cloned.1.call-done, f32[3200]{0:T(1024)S(1)} %copy-done.5, f32[2176]{0:T(1024)S(1)} %add_rsqrt_fusion), kind=kOutput, calls=%fused_computation.95 | convolution fusion | flops 5376425984 | bytes 21419008 | tf_op jit(solution)/shard_map/dot_general | solution.py:78
  168.2 5.2 %all-to-all-start.2 = ((f32[16,2,2176]{2,1,0:T(2,128)}), f32[16,2,2176]{2,1,0:T(2,128)S(1)}, u32[]{:S(2)}, u32[]{:S(2)}) async-start(f32[16,2,2176]{2,1,0:T(2,128)} %broadcast_in_dim.102), calls=%async_computation.2 | async-start | bytes 557056 | tf_op jit(solution)/shard_map/all_to_all | solution.py:51
  173.7 6.8 %all-to-all-done.2 = f32[16,2,2176]{2,1,0:T(2,128)S(1)} async-done(((f32[16,2,2176]{2,1,0:T(2,128)}), f32[16,2,2176]{2,1,0:T(2,128)S(1)}, u32[]{:S(2)}, u32[]{:S(2)}) %all-to-all-start.2) | async-done | bytes 278560 | tf_op jit(solution)/shard_map/all_to_all | solution.py:51
  180.6 2.4 multiply_convert_fusion.1
  184.5 2.7 fusion.12
  188.7 2.6 fusion.13
  195.6 46.7 %all-gather.11.cloned.1.call-done = bf16[16384,128]{1,0:T(8,128)(2,1)} async-done(((bf16[1024,128]{1,0:T(8,128)(2,1)}), bf16[16384,128]{1,0:T(8,128)(2,1)}) %all-gather.11.cloned.1.call-update) | async-done | bytes 4194320 | tf_op jit(solution)/shard_map/all_gather | solution.py:116
  242.3 7.8 %convolution_convert_fusion = bf16[16,1024,200]{1,2,0:T(8,128)(2,1)} fusion(bf16[16,1024,128]{2,1,0:T(8,128)(2,1)} %bitcast.77, bf16[2048,200]{0,1:T(8,128)(2,1)S(1)} %copy_bitcast_fusion), kind=kOutput, calls=%fused_computation.11 | convolution fusion | flops 842137600 | bytes 11567104 | tf_op jit(solution)/shard_map/hsc,hcd->hsd/dot_general | solution.py:117
  250.0 49.5 %all-gather.9.cloned.1.call-done = bf16[16384,128]{1,0:T(8,128)(2,1)} async-done(((bf16[1024,128]{1,0:T(8,128)(2,1)}), bf16[16384,128]{1,0:T(8,128)(2,1)}) %all-gather.9.cloned.1.call-update) | async-done | bytes 4194320 | tf_op jit(solution)/shard_map/all_gather | solution.py:116
  299.6 5.2 %convolution_convert_fusion.1 = bf16[16,1024,200]{1,2,0:T(8,128)(2,1)S(1)} fusion(bf16[16,1024,128]{2,1,0:T(8,128)(2,1)} %bitcast.78, bf16[2048,200]{0,1:T(8,128)(2,1)S(1)} %copy_bitcast_fusion), kind=kOutput, calls=%fused_computation.12 | convolution fusion | flops 842137600 | bytes 11567104 | tf_op jit(solution)/shard_map/hsc,hcd->hsd/dot_general | solution.py:117
  304.8 4.1 convert_reduce_fusion
  308.8 2.3 fusion.17
  312.4 4.9 %copy.54 = bf16[16,16,200,2,2]{1,0,4,3,2:T(8,128)(2,1)S(1)} copy(bf16[16,16,200,2,2]{2,4,1,3,0:T(2,128)(2,1)} %bitcast.80) | data formatting | bytes 819200 | tf_op jit(solution)/shard_map/transpose | solution.py:126
  317.2 3.9 broadcast_in_dim.103
  321.1 3.0 broadcast_select_fusion.1
  324.1 4.3 all-to-all-start.3
  330.5 2.1 reshape.166
  332.6 5.6 %copy.57 = bf16[16,16,200,2,2]{1,0,4,3,2:T(8,128)(2,1)} copy(bf16[16,16,200,2,2]{2,4,1,3,0:T(2,128)(2,1)} %bitcast.81) | data formatting | bytes 819200 | tf_op jit(solution)/shard_map/transpose | solution.py:126
  338.2 5.2 %broadcast_in_dim.108 = bf16[256,800]{0,1:T(8,128)(2,1)} reshape(bf16[16,16,200,2,2]{1,0,4,3,2:T(8,128)(2,1)} %copy.57) | data formatting | bytes 819200 | tf_op jit(solution)/shard_map/jit(_where)/broadcast_in_dim | solution.py:128
  343.4 3.0 broadcast_select_fusion
  346.4 29.7 %all-to-all-done.3 = bf16[8,256,800]{1,2,0:T(8,128)(2,1)S(1)} async-done(((bf16[8,256,800]{1,2,0:T(8,128)(2,1)}), bf16[8,256,800]{1,2,0:T(8,128)(2,1)S(1)}, u32[]{:S(2)}, u32[]{:S(2)}) %all-to-all-start.3) | async-done | bytes 3276832 | tf_op jit(solution)/shard_map/all_to_all | solution.py:132
  376.1 4.5 %all-to-all-start.4 = ((bf16[8,256,800]{1,2,0:T(8,128)(2,1)}), bf16[8,256,800]{1,2,0:T(8,128)(2,1)}, u32[]{:S(2)}, u32[]{:S(2)}) async-start(bf16[8,256,800]{1,2,0:T(8,128)(2,1)} %broadcast_select_fusion), calls=%async_computation.4 | async-start | bytes 6553600 | tf_op jit(solution)/shard_map/all_to_all | solution.py:132
  391.6 35.8 %all-to-all-done.4 = bf16[8,256,800]{1,2,0:T(8,128)(2,1)} async-done(((bf16[8,256,800]{1,2,0:T(8,128)(2,1)}), bf16[8,256,800]{1,2,0:T(8,128)(2,1)}, u32[]{:S(2)}, u32[]{:S(2)}) %all-to-all-start.4) | async-done | bytes 3276832 | tf_op jit(solution)/shard_map/all_to_all | solution.py:132
  427.4 2.5 pad_maximum_fusion
  429.9 2.6 dynamic-slice_select_fusion.3
  (56 shorter events, 19.6 us)
Async XLA Ops:
  6.5 137.9 %all-gather.7.cloned.1.call-start = ((), (), s32[]{:S(2)}) async-start(), calls=%async_computation.5 | async-start | bytes 14796800 | tf_op jit(solution)/shard_map/all_gather | solution.py:73
  62.6 41.8 %all-to-all-start = ((bf16[8,400,384]{2,1,0:T(8,128)(2,1)}), bf16[8,400,384]{2,1,0:T(8,128)(2,1)}, u32[]{:S(2)}, u32[]{:S(2)}) async-start(bf16[8,400,384]{2,1,0:T(8,128)(2,1)} %broadcast_in_dim.101), calls=%async_computation | async-start | bytes 4915200 | tf_op jit(solution)/shard_map/all_to_all | solution.py:57
  104.4 47.8 %copy-start.5 = (f32[3200]{0:T(1024)S(1)}, f32[3200]{0:T(1024)}, u32[]{:S(2)}) copy-start(f32[3200]{0:T(1024)} %param.9) | copy-start | bytes 38404
  152.2 21.5 %copy-start.2 = (f32[2,128]{1,0:T(2,128)S(1)}, f32[2,128]{1,0:T(2,128)}, u32[]{:S(2)}) copy-start(f32[2,128]{1,0:T(2,128)} %param.11) | copy-start | bytes 3076
  165.0 1.7 copy-start.1
  168.2 12.3 %all-to-all-start.2 = ((f32[16,2,2176]{2,1,0:T(2,128)}), f32[16,2,2176]{2,1,0:T(2,128)S(1)}, u32[]{:S(2)}, u32[]{:S(2)}) async-start(f32[16,2,2176]{2,1,0:T(2,128)} %broadcast_in_dim.102), calls=%async_computation.2 | async-start | bytes 557056 | tf_op jit(solution)/shard_map/all_to_all | solution.py:51
  173.4 68.8 %all-gather.11.cloned.1.call-start = ((), (), s32[]{:S(2)}) async-start(), calls=%async_computation.7 | async-start | bytes 4456448 | tf_op jit(solution)/shard_map/all_gather | solution.py:116
  187.2 112.3 %all-gather.9.cloned.1.call-start = ((), (), s32[]{:S(2)}) async-start(), calls=%async_computation.6 | async-start | bytes 4456448 | tf_op jit(solution)/shard_map/all_gather | solution.py:116
  188.7 3.5 copy-start.3
  188.7 3.5 copy-start.4
  299.6 5.2 %copy-start = (bf16[16,1024,200]{1,2,0:T(8,128)(2,1)S(1)}, bf16[16,1024,200]{1,2,0:T(8,128)(2,1)}, u32[]{:S(2)}) copy-start(bf16[16,1024,200]{1,2,0:T(8,128)(2,1)} %convolution_convert_fusion) | copy-start | bytes 19660804
  324.1 52.0 %all-to-all-start.3 = ((bf16[8,256,800]{1,2,0:T(8,128)(2,1)}), bf16[8,256,800]{1,2,0:T(8,128)(2,1)S(1)}, u32[]{:S(2)}, u32[]{:S(2)}) async-start(bf16[8,256,800]{1,2,0:T(8,128)(2,1)} %broadcast_select_fusion.1), calls=%async_computation.3 | async-start | bytes 6553600 | tf_op jit(solution)/shard_map/all_to_all | solution.py:132
  376.1 51.3 %all-to-all-start.4 = ((bf16[8,256,800]{1,2,0:T(8,128)(2,1)}), bf16[8,256,800]{1,2,0:T(8,128)(2,1)}, u32[]{:S(2)}, u32[]{:S(2)}) async-start(bf16[8,256,800]{1,2,0:T(8,128)(2,1)} %broadcast_select_fusion), calls=%async_computation.4 | async-start | bytes 6553600 | tf_op jit(solution)/shard_map/all_to_all | solution.py:132
Sparse Core Ops, SparseCore 0:
  9.8 134.5 all-gather.6
  187.3 54.8 all-gather.10
  244.7 54.7 all-gather.8

commit v4 on v3

--- a/solution.py
+++ b/solution.py
@@ -114,6 +114,8 @@
             jnp.bfloat16
         )
         all_heads = lax.all_gather(tile_out, "dp", axis=0, tiled=False)
+        if slot_received:
+            all_heads, slot_received[-1] = lax.optimization_barrier((all_heads, slot_received[-1]))
         head_terms = jnp.einsum(
             "hsc,hcd->hsd",
             all_heads,

time: 442 us -> 417 us (0.943)
  waiting for transfers between devices: 247 us -> 225 us
    all_to_all x2, waiting for transfers between devices: 65.5 us -> 36.7 us  [body(): lax.all_to_all(outgoing, 'fsdp', split_axis=0, concat_axis=0, tiled=True)]
    all_gather x2, waiting for transfers between devices: 96.2 us -> 103 us  [body(): all_heads = lax.all_gather(tile_out, 'dp', axis=0, tiled=False)]
  transfers between devices with their start and end apart: 7 -> 7, of which waited for: 7 -> 6; matrix products, arithmetic and copies ran while one was open for 9% -> 9% of each run, Pallas kernels for 0% -> 0%
where the time goes in v4:
time: 417 us; the launch traced here: 416 us
  waiting for transfers between devices  225 us (54%)
  blocking collectives  52.5 us (13%)
  local copies, waits for them, and re-layouts  36.2 us (9%)
  other arithmetic  32.6 us (8%)
  matrix products  30 us (7%)
  between operations  20.8 us (5%)
  starting transfers between devices  19 us (5%)
    all_gather x2, waiting for transfers between devices, body(): all_heads = lax.all_gather(tile_out, 'dp', axis=0, tiled=False)  103 us
    all_gather x1, waiting for transfers between devices, body(): gathered = lax.all_gather(own_rows, 'dp', axis=0, tiled=True)  40 us
    all_to_all x1, waiting for transfers between devices, gather_blocks(): lax.all_to_all(spread, axis_name, split_axis=0, concat_axis=0, tiled=True)  37.3 us
    all_to_all x2, waiting for transfers between devices, body(): lax.all_to_all(outgoing, 'fsdp', split_axis=0, concat_axis=0, tiled=True)  36.7 us
    all_gather x1, blocking collectives, body(): head_rows = lax.all_gather(out_weight, 'fsdp', axis=1, tiled=True)  31.9 us
    all_to_all x1, blocking collectives, body(): lax.all_to_all(head_rows, 'dp', split_axis=1, concat_axis=0, tiled=True)  20.6 us
    dot_general x1, matrix products, body(): projected = jnp.dot(normed, full_qkv, preferred_element_type=jnp.float32)  12.8 us
    transpose x2, local copies, waits for them, and re-layouts, body(): updated.reshape(halves, 2, halves, 2, block).transpose(0, 2, 4, 1, 3)  10.4 us
  transfers between devices with their start and end apart: 7, of which 6 were waited for; matrix products, arithmetic and copies ran while one was open for 9% of the time, Pallas kernels for 0%

profile of v4, /device:TPU:8, one launch (start us, length us, event | category | flops | bytes accessed | tf_op | source)
XLA Modules:
  0.0 416.1 jit_solution(4726154906487316695)
XLA Ops:
  7.3 31.9 %all_gather.19 = bf16[128,3200]{0,1:T(8,128)(2,1)S(1)} all-gather(bf16[128,400]{0,1:T(8,128)(2,1)} %param.12), channel_id=1, replica_groups=mesh['fsdp'=8,'dp'=16] {'fsdp'}, dimensions={1}, use_global_device_ids=true | all-gather | bytes 921600 | tf_op jit(solution)/shard_map/all_gather | solution.py:69
  39.1 20.6 %all_to_all.39 = bf16[128,16,200]{0,2,1:T(8,128)(2,1)S(1)} all-to-all(bf16[128,16,200]{0,2,1:T(8,128)(2,1)S(1)} %bitcast.79), channel_id=1, replica_groups=mesh['fsdp'=8,'dp'=16] {'dp'}, dimensions={1} | all-to-all | bytes 1638400 | tf_op jit(solution)/shard_map/all_to_all | solution.py:70
  59.7 2.8 broadcast_in_dim.99
  62.6 4.4 %all-to-all-start = ((bf16[8,400,384]{2,1,0:T(8,128)(2,1)}), bf16[8,400,384]{2,1,0:T(8,128)(2,1)}, u32[]{:S(2)}, u32[]{:S(2)}) async-start(bf16[8,400,384]{2,1,0:T(8,128)(2,1)} %broadcast_in_dim.99), calls=%async_computation | async-start | bytes 4915200 | tf_op jit(solution)/shard_map/all_to_all | solution.py:57
  67.1 37.3 %all-to-all-done = bf16[8,400,384]{2,1,0:T(8,128)(2,1)} async-done(((bf16[8,400,384]{2,1,0:T(8,128)(2,1)}), bf16[8,400,384]{2,1,0:T(8,128)(2,1)}, u32[]{:S(2)}, u32[]{:S(2)}) %all-to-all-start) | async-done | bytes 2457632 | tf_op jit(solution)/shard_map/all_to_all | solution.py:57
  104.4 40.0 %all-gather.7.cloned.1.call-done = bf16[1,2176,3200]{2,1,0:T(8,128)(2,1)} async-done(((bf16[1,136,3200]{2,1,0:T(8,128)(2,1)}), bf16[1,2176,3200]{2,1,0:T(8,128)(2,1)}) %all-gather.7.cloned.1.call-update) | async-done | bytes 13926416 | tf_op jit(solution)/shard_map/all_gather | solution.py:73
  144.4 7.7 %fusion = f32[2176]{0:T(1024)S(1)} fusion(bf16[1,2176,3200]{2,1,0:T(8,128)(2,1)} %all-gather.7.cloned.1.call-done), kind=kLoop, calls=%fused_computation.2 | loop fusion | flops 20887424 | bytes 13935104 | tf_op jit(solution)/shard_map/reduce_sum | solution.py:76
  152.2 12.8 %fusion.40 = (bf16[2176,384]{1,0:T(8,128)(2,1)}, f32[2176,384]{1,0:T(8,128)S(1)}) fusion(bf16[3200,384]{1,0:T(8,128)(2,1)} %bitcast.6, bf16[1,2176,3200]{2,1,0:T(8,128)(2,1)} %all-gather.7.cloned.1.call-done, f32[3200]{0:T(1024)S(1)} %copy-done.6, f32[2176]{0:T(1024)S(1)} %add_rsqrt_fusion), kind=kOutput, calls=%fused_computation.95 | convolution fusion | flops 5376425984 | bytes 21419008 | tf_op jit(solution)/shard_map/dot_general | solution.py:78
  168.2 5.2 %all-to-all-start.2 = ((f32[16,2,2176]{2,1,0:T(2,128)}), f32[16,2,2176]{2,1,0:T(2,128)S(1)}, u32[]{:S(2)}, u32[]{:S(2)}) async-start(f32[16,2,2176]{2,1,0:T(2,128)} %broadcast_in_dim.100), calls=%async_computation.2 | async-start | bytes 557056 | tf_op jit(solution)/shard_map/all_to_all | solution.py:51
  173.7 6.8 %all-to-all-done.2 = f32[16,2,2176]{2,1,0:T(2,128)S(1)} async-done(((f32[16,2,2176]{2,1,0:T(2,128)}), f32[16,2,2176]{2,1,0:T(2,128)S(1)}, u32[]{:S(2)}, u32[]{:S(2)}) %all-to-all-start.2) | async-done | bytes 278560 | tf_op jit(solution)/shard_map/all_to_all | solution.py:51
  180.7 2.4 multiply_convert_fusion.1
  184.5 2.6 fusion.12
  188.6 2.7 fusion.13
  192.4 2.8 constant_dynamic-slice_fusion.1
  195.4 46.7 %all-gather.11.cloned.1.call-done = bf16[16384,128]{1,0:T(8,128)(2,1)} async-done(((bf16[1024,128]{1,0:T(8,128)(2,1)}), bf16[16384,128]{1,0:T(8,128)(2,1)}) %all-gather.11.cloned.1.call-update) | async-done | bytes 4194320 | tf_op jit(solution)/shard_map/all_gather | solution.py:116
  242.1 5.0 %convolution_convert_fusion.1 = bf16[16,1024,200]{1,2,0:T(8,128)(2,1)S(1)} fusion(bf16[16,1024,128]{2,1,0:T(8,128)(2,1)} %bitcast.78, bf16[2048,200]{0,1:T(8,128)(2,1)S(1)} %copy_bitcast_fusion), kind=kOutput, calls=%fused_computation.12 | convolution fusion | flops 842137600 | bytes 11567104 | tf_op jit(solution)/shard_map/hsc,hcd->hsd/dot_general | solution.py:119
  250.1 4.9 %copy.54 = bf16[16,16,200,2,2]{1,0,4,3,2:T(8,128)(2,1)S(1)} copy(bf16[16,16,200,2,2]{2,4,1,3,0:T(2,128)(2,1)} %bitcast.80) | data formatting | bytes 819200 | tf_op jit(solution)/shard_map/transpose | solution.py:128
  255.0 3.9 broadcast_in_dim.103
  258.8 3.0 broadcast_select_fusion.1
  261.8 4.3 %all-to-all-start.3 = ((bf16[8,256,800]{1,2,0:T(8,128)(2,1)}), bf16[8,256,800]{1,2,0:T(8,128)(2,1)S(1)}, u32[]{:S(2)}, u32[]{:S(2)}) async-start(bf16[8,256,800]{1,2,0:T(8,128)(2,1)} %broadcast_select_fusion.1), calls=%async_computation.3 | async-start | bytes 6553600 | tf_op jit(solution)/shard_map/all_to_all | solution.py:134
  266.2 2.0 copy.64
  268.2 56.7 %all-gather.9.cloned.1.call-done = bf16[16384,128]{1,0:T(8,128)(2,1)} async-done(((bf16[1024,128]{1,0:T(8,128)(2,1)}), bf16[16384,128]{1,0:T(8,128)(2,1)}) %all-gather.9.cloned.1.call-update) | async-done | bytes 4194320 | tf_op jit(solution)/shard_map/all_gather | solution.py:116
  324.9 5.3 %convolution_convert_fusion = bf16[16,1024,200]{1,2,0:T(8,128)(2,1)S(1)} fusion(bf16[16,1024,128]{2,1,0:T(8,128)(2,1)} %bitcast.77, bf16[2048,200]{0,1:T(8,128)(2,1)} %copy-done), kind=kOutput, calls=%fused_computation.11 | convolution fusion | flops 842137600 | bytes 11567104 | tf_op jit(solution)/shard_map/hsc,hcd->hsd/dot_general | solution.py:119
  332.6 2.0 copy.56
  334.6 2.1 reshape.166
  336.7 5.6 %copy.57 = bf16[16,16,200,2,2]{1,0,4,3,2:T(8,128)(2,1)} copy(bf16[16,16,200,2,2]{2,4,1,3,0:T(2,128)(2,1)} %bitcast.81) | data formatting | bytes 819200 | tf_op jit(solution)/shard_map/transpose | solution.py:128
  342.3 5.2 %broadcast_in_dim.108 = bf16[256,800]{0,1:T(8,128)(2,1)} reshape(bf16[16,16,200,2,2]{1,0,4,3,2:T(8,128)(2,1)} %copy.57) | data formatting | bytes 819200 | tf_op jit(solution)/shard_map/jit(_where)/broadcast_in_dim | solution.py:130
  347.5 3.0 broadcast_select_fusion
  350.5 4.8 %all-to-all-start.4 = ((bf16[8,256,800]{1,2,0:T(8,128)(2,1)}), bf16[8,256,800]{1,2,0:T(8,128)(2,1)}, u32[]{:S(2)}, u32[]{:S(2)}) async-start(bf16[8,256,800]{1,2,0:T(8,128)(2,1)} %broadcast_select_fusion), calls=%async_computation.4 | async-start | bytes 6553600 | tf_op jit(solution)/shard_map/all_to_all | solution.py:134
  366.4 36.7 %all-to-all-done.4 = bf16[8,256,800]{1,2,0:T(8,128)(2,1)} async-done(((bf16[8,256,800]{1,2,0:T(8,128)(2,1)}), bf16[8,256,800]{1,2,0:T(8,128)(2,1)}, u32[]{:S(2)}, u32[]{:S(2)}) %all-to-all-start.4) | async-done | bytes 3276832 | tf_op jit(solution)/shard_map/all_to_all | solution.py:134
  403.1 2.5 pad_maximum_fusion
  405.6 2.6 dynamic-slice_select_fusion.3
  (60 shorter events, 18.9 us)
Async XLA Ops:
  6.5 137.9 %all-gather.7.cloned.1.call-start = ((), (), s32[]{:S(2)}) async-start(), calls=%async_computation.5 | async-start | bytes 14796800 | tf_op jit(solution)/shard_map/all_gather | solution.py:73
  62.6 41.8 %all-to-all-start = ((bf16[8,400,384]{2,1,0:T(8,128)(2,1)}), bf16[8,400,384]{2,1,0:T(8,128)(2,1)}, u32[]{:S(2)}, u32[]{:S(2)}) async-start(bf16[8,400,384]{2,1,0:T(8,128)(2,1)} %broadcast_in_dim.99), calls=%async_computation | async-start | bytes 4915200 | tf_op jit(solution)/shard_map/all_to_all | solution.py:57
  67.1 175.0 %copy-start = (bf16[2048,200]{0,1:T(8,128)(2,1)}, bf16[2048,200]{0,1:T(8,128)(2,1)S(1)}, u32[]{:S(2)}) copy-start(bf16[2048,200]{0,1:T(8,128)(2,1)S(1)} %copy_bitcast_fusion) | copy-start | bytes 2457604
  104.4 47.8 %copy-start.6 = (f32[3200]{0:T(1024)S(1)}, f32[3200]{0:T(1024)}, u32[]{:S(2)}) copy-start(f32[3200]{0:T(1024)} %param.9) | copy-start | bytes 38404
  152.2 21.5 %copy-start.3 = (f32[2,128]{1,0:T(2,128)S(1)}, f32[2,128]{1,0:T(2,128)}, u32[]{:S(2)}) copy-start(f32[2,128]{1,0:T(2,128)} %param.11) | copy-start | bytes 3076
  165.0 1.7 copy-start.1
  168.2 12.3 %all-to-all-start.2 = ((f32[16,2,2176]{2,1,0:T(2,128)}), f32[16,2,2176]{2,1,0:T(2,128)S(1)}, u32[]{:S(2)}, u32[]{:S(2)}) async-start(f32[16,2,2176]{2,1,0:T(2,128)} %broadcast_in_dim.100), calls=%async_computation.2 | async-start | bytes 557056 | tf_op jit(solution)/shard_map/all_to_all | solution.py:51
  173.4 68.6 %all-gather.11.cloned.1.call-start = ((), (), s32[]{:S(2)}) async-start(), calls=%async_computation.7 | async-start | bytes 4456448 | tf_op jit(solution)/shard_map/all_gather | solution.py:116
  187.1 137.8 %all-gather.9.cloned.1.call-start = ((), (), s32[]{:S(2)}) async-start(), calls=%async_computation.6 | async-start | bytes 4456448 | tf_op jit(solution)/shard_map/all_gather | solution.py:116
  188.6 3.6 copy-start.4
  188.6 3.6 copy-start.5
  261.8 63.0 %all-to-all-start.3 = ((bf16[8,256,800]{1,2,0:T(8,128)(2,1)}), bf16[8,256,800]{1,2,0:T(8,128)(2,1)S(1)}, u32[]{:S(2)}, u32[]{:S(2)}) async-start(bf16[8,256,800]{1,2,0:T(8,128)(2,1)} %broadcast_select_fusion.1), calls=%async_computation.3 | async-start | bytes 6553600 | tf_op jit(solution)/shard_map/all_to_all | solution.py:134
  330.1 1.6 copy-start.2
  350.5 52.5 %all-to-all-start.4 = ((bf16[8,256,800]{1,2,0:T(8,128)(2,1)}), bf16[8,256,800]{1,2,0:T(8,128)(2,1)}, u32[]{:S(2)}, u32[]{:S(2)}) async-start(bf16[8,256,800]{1,2,0:T(8,128)(2,1)} %broadcast_select_fusion), calls=%async_computation.4 | async-start | bytes 6553600 | tf_op jit(solution)/shard_map/all_to_all | solution.py:134
Sparse Core Ops, SparseCore 0:
  9.8 134.5 all-gather.6
  187.2 54.7 all-gather.10
  244.5 80.2 all-gather.8

commit v5 on v2

--- a/solution.py
+++ b/solution.py
@@ -1,7 +1,7 @@
 import jax
 import jax.numpy as jnp
 from jax import lax
-from jax.sharding import PartitionSpec as P
+from jax.sharding import Mesh, PartitionSpec as P
 
 HEAD_DIM = 128
 GRID = 32
@@ -52,50 +52,72 @@
     return jnp.sum(collected, axis=0)
 
 
+def gather_blocks(block_value, axis_name, groups):
+    spread = jnp.broadcast_to(block_value[None], (groups,) + block_value.shape)
+    collected = lax.all_to_all(spread, axis_name, split_axis=0, concat_axis=0, tiled=True)
+    return collected.reshape((groups * block_value.shape[0],) + block_value.shape[1:])
+
+
 def body(tokens, norm_gain, qkv_weight, qk_gain, out_weight, layer_scale, tile_counts, owners):
     own_rows = tokens[0]
-    groups = lax.axis_size("dp")
-    dp_index = lax.axis_index("dp")
+    chips = lax.axis_size("chip")
+    cores = lax.axis_size("core")
+    groups = chips * cores
+    chip = lax.axis_index("chip")
+    core = lax.axis_index("core")
+    row_index = lax.axis_index("fsdp")
+    row_count = lax.axis_size("fsdp")
     model_width = own_rows.shape[1]
     block = model_width // groups
+    swap = [(0, 1), (1, 0)]
     head_rows = lax.all_gather(out_weight, "fsdp", axis=1, tiled=True)
-    weight_block = lax.all_to_all(head_rows, "dp", split_axis=1, concat_axis=0, tiled=True)
-    gathered = lax.all_gather(own_rows, "dp", axis=0, tiled=True)
-    gathered, weight_block = lax.optimization_barrier((gathered, weight_block))
-    length = gathered.shape[0]
-    values = gathered.astype(jnp.float32)
+    weight_block = lax.all_to_all(
+        head_rows, ("chip", "core"), split_axis=1, concat_axis=0, tiled=True
+    )
+    pair_weight = lax.all_gather(weight_block, "core", axis=1, tiled=True)
+    full_qkv = gather_blocks(qkv_weight, "fsdp", row_count)
+    pair_qkv = lax.all_gather(full_qkv, "core", axis=1, tiled=True)
+    pair_qkv, pair_weight = lax.optimization_barrier((pair_qkv, pair_weight))
+    pair_gain = lax.all_gather(qk_gain, "core", axis=1, tiled=True).reshape(2, cores, HEAD_DIM)
+    half = lax.all_gather(own_rows, "chip", axis=0, tiled=True)
+    half_length = half.shape[0]
+    piece = own_rows.shape[0]
+    values = half.astype(jnp.float32)
     normed = (
         values * lax.rsqrt(jnp.mean(values * values, axis=-1, keepdims=True) + EPSILON) * norm_gain
     ).astype(jnp.bfloat16)
-    projected = jnp.dot(
-        normed,
-        lax.all_gather(qkv_weight, "fsdp", axis=0, tiled=True),
-        preferred_element_type=jnp.float32,
+    projected = jnp.dot(normed, pair_qkv, preferred_element_type=jnp.float32)
+    projected = projected.reshape(half_length, cores, 3, HEAD_DIM)
+    queries = projected[:, :, 0]
+    keys_part = projected[:, :, 1]
+    values_part = projected[:, :, 2].astype(jnp.bfloat16)
+    sums = gather_sum(
+        jnp.stack(
+            [jnp.sum(queries * queries, axis=(1, 2)), jnp.sum(keys_part * keys_part, axis=(1, 2))]
+        ),
+        "chip",
+        chips,
     )
-    queries = projected[:, :HEAD_DIM]
-    keys_part = projected[:, HEAD_DIM : 2 * HEAD_DIM]
-    values_part = projected[:, 2 * HEAD_DIM :].astype(jnp.bfloat16)
-    sums = gather_sum(
-        jnp.stack([jnp.sum(queries * queries, axis=-1), jnp.sum(keys_part * keys_part, axis=-1)]),
-        "dp",
-        groups,
-    )
-    query_sums = sums[0]
-    key_sums = sums[1]
     window = groups * HEAD_DIM
-    queries = (queries * lax.rsqrt(query_sums / window + EPSILON)[:, None] * qk_gain[0]).astype(
-        jnp.bfloat16
-    )
-    keys_part = (keys_part * lax.rsqrt(key_sums / window + EPSILON)[:, None] * qk_gain[1]).astype(
-        jnp.bfloat16
-    )
-    row_index = lax.axis_index("fsdp")
-    row_count = lax.axis_size("fsdp")
+    queries = (
+        queries * lax.rsqrt(sums[0] / window + EPSILON)[:, None, None] * pair_gain[0][None]
+    ).astype(jnp.bfloat16)
+    keys_part = (
+        keys_part * lax.rsqrt(sums[1] / window + EPSILON)[:, None, None] * pair_gain[1][None]
+    ).astype(jnp.bfloat16)
+    stacked = jnp.stack([queries, keys_part, values_part])
+    mine = lax.dynamic_index_in_dim(stacked, core, axis=2, keepdims=False)
+    theirs = lax.dynamic_index_in_dim(stacked, 1 - core, axis=2, keepdims=False)
+    got = lax.ppermute(theirs, "core", swap)
+    first_half = jnp.where(core == 0, mine, got).reshape(3, chips, piece, HEAD_DIM)
+    second_half = jnp.where(core == 0, got, mine).reshape(3, chips, piece, HEAD_DIM)
+    whole = jnp.stack([first_half, second_half], axis=2).reshape(3, groups * piece, HEAD_DIM)
+    length = whole.shape[1]
     factor = HEAD_DIM ** (-0.5)
     covered = SLOTS * TILE
-    tile_query = queries[:covered].reshape(SLOTS, TILE, HEAD_DIM)
-    tile_key = keys_part[:covered].reshape(SLOTS, TILE, HEAD_DIM)
-    tile_value = values_part[:covered].reshape(SLOTS, TILE, HEAD_DIM)
+    tile_query = whole[0, :covered].reshape(SLOTS, TILE, HEAD_DIM)
+    tile_key = whole[1, :covered].reshape(SLOTS, TILE, HEAD_DIM)
+    tile_value = whole[2, :covered].reshape(SLOTS, TILE, HEAD_DIM)
     scores = (
         jnp.einsum("sqc,skc->sqk", tile_query, tile_key, preferred_element_type=jnp.float32)
         * factor
@@ -113,17 +135,32 @@
         ],
         axis=0,
     )
-    all_heads = lax.all_gather(head_out, "dp", axis=0, tiled=False)
+    by_half = head_out.reshape(chips, cores, piece, HEAD_DIM).transpose(1, 0, 2, 3)
+    by_half = by_half.reshape(cores, half_length, HEAD_DIM)
+    outgoing = jnp.broadcast_to(by_half[None], (chips, cores, half_length, HEAD_DIM))
+    all_heads = lax.all_to_all(
+        outgoing.reshape(groups, half_length, HEAD_DIM),
+        ("chip", "core"),
+        split_axis=0,
+        concat_axis=0,
+        tiled=True,
+    )
     head_terms = jnp.einsum(
         "hsc,hcd->hsd",
         all_heads,
-        weight_block.reshape(groups, HEAD_DIM, block),
+        pair_weight.reshape(groups, HEAD_DIM, cores * block),
         preferred_element_type=jnp.float32,
     ).astype(jnp.bfloat16)
     attention = jnp.sum(lax.optimization_barrier(head_terms).astype(jnp.float32), axis=0)
-    own_block = lax.dynamic_slice_in_dim(gathered, dp_index * block, block, axis=1)
-    scale_block = lax.dynamic_slice_in_dim(layer_scale, dp_index * block, block)
-    updated = (own_block.astype(jnp.float32) + scale_block * attention).astype(jnp.bfloat16)
+    pair_tokens = lax.dynamic_slice_in_dim(half, chip * cores * block, cores * block, axis=1)
+    pair_scale = lax.dynamic_slice_in_dim(layer_scale, chip * cores * block, cores * block)
+    updated_half = (pair_tokens.astype(jnp.float32) + pair_scale * attention).astype(jnp.bfloat16)
+    keep = lax.dynamic_slice_in_dim(updated_half, core * block, block, axis=1)
+    give = lax.dynamic_slice_in_dim(updated_half, (1 - core) * block, block, axis=1)
+    taken = lax.ppermute(give, "core", swap)
+    first_half = jnp.where(core == 0, keep, taken).reshape(chips, piece, block)
+    second_half = jnp.where(core == 0, taken, keep).reshape(chips, piece, block)
+    updated = jnp.stack([first_half, second_half], axis=1).reshape(length, block)
     merged = merge_tiles(updated)
     holder, living = tile_owners(tile_counts, owners)
     own_holder = holder[row_index]
@@ -136,16 +173,22 @@
 
 
 def solution(mesh):
+    fsdp_size = mesh.shape["fsdp"]
+    dp_size = mesh.shape["dp"]
+    split = Mesh(
+        mesh.devices.reshape(fsdp_size, dp_size // 2, 2), ("fsdp", "chip", "core")
+    )
+    heads = ("chip", "core")
     placed = (
-        P("fsdp", "dp", None),
+        P("fsdp", heads, None),
         P(),
-        P("fsdp", "dp"),
-        P(None, "dp"),
-        P("dp", "fsdp"),
+        P("fsdp", heads),
+        P(None, heads),
+        P(heads, "fsdp"),
         P(),
         P(),
         P(),
     )
     return jax.shard_map(
-        body, mesh=mesh, in_specs=placed, out_specs=P("fsdp", None, "dp"), check_vma=False
+        body, mesh=split, in_specs=placed, out_specs=P("fsdp", None, heads), check_vma=False
     )

time: 451 us -> 484 us (1.073)
  waiting for transfers between devices: 248 us -> 292 us
  local copies, waits for them, and re-layouts: 51.9 us -> 37.3 us
  starting transfers between devices: 12.4 us -> 21.2 us
    all_to_all x0 -> x2, waiting for transfers between devices: none -> 92.6 us  [the longest x1 56.4 us: body(): lax.all_to_all(outgoing.reshape(groups, half_length, HEAD_DIM), ('chip',...]
    all_gather x3, waiting for transfers between devices: 162 us -> 109 us  [the longest x1 97.7 us: body(): half = lax.all_gather(own_rows, 'chip', axis=0, tiled=True)]
    all_gather x1 -> x0, local copies, waits for them, and re-layouts: 19 us -> none  [body(): gathered = lax.all_gather(own_rows, 'dp', axis=0, tiled=True)]
    all_to_all x0 -> x2, starting transfers between devices: none -> 10.1 us  [the longest x1 5.7 us: body(): lax.all_to_all(outgoing.reshape(groups, half_length, HEAD_DIM), ('chip',...]
    broadcast_in_dim x0 -> x2, local copies, waits for them, and re-layouts: none -> 5.64 us  [the longest x1 3.02 us: body(): jnp.broadcast_to(by_half[None], (chips, cores, half_length, HEAD_DIM))]
  transfers between devices with their start and end apart: 5 -> 9, of which waited for: 5 -> 8; matrix products, arithmetic and copies ran while one was open for 8% -> 2% of each run, Pallas kernels for 0% -> 0%
where the time goes in v5:
time: 484 us; the launch traced here: 483 us
  waiting for transfers between devices  292 us (60%)
  blocking collectives  52.7 us (11%)
  local copies, waits for them, and re-layouts  37.3 us (8%)
  matrix products  29.3 us (6%)
  other arithmetic  28.8 us (6%)
  starting transfers between devices  21.2 us (4%)
  between operations  21.2 us (4%)
    all_gather x1, waiting for transfers between devices, body(): half = lax.all_gather(own_rows, 'chip', axis=0, tiled=True)  97.7 us
    all_to_all x1, waiting for transfers between devices, body(): lax.all_to_all(outgoing, 'fsdp', split_axis=0, concat_axis=0, tiled=True)  80.9 us
    all_to_all x1, waiting for transfers between devices, body(): lax.all_to_all(outgoing.reshape(groups, half_length, HEAD_DIM), ('chip',...  56.4 us
    all_to_all x1, waiting for transfers between devices, gather_blocks(): lax.all_to_all(spread, axis_name, split_axis=0, concat_axis=0, tiled=True)  36.2 us
    all_gather x1, blocking collectives, body(): head_rows = lax.all_gather(out_weight, 'fsdp', axis=1, tiled=True)  30.1 us
    all_to_all x1, blocking collectives, body(): lax.all_to_all(head_rows, ('chip', 'core'), split_axis=1, concat_axis=0,...  20.8 us
    dot_general x1, matrix products, body(): jnp.einsum('hsc,hcd->hsd', all_heads, pair_weight.reshape(groups, HEAD_DI...  11.6 us
    all_gather x1, waiting for transfers between devices, body(): pair_qkv = lax.all_gather(full_qkv, 'core', axis=1, tiled=True)  11.3 us
  transfers between devices with their start and end apart: 9, of which 8 were waited for; matrix products, arithmetic and copies ran while one was open for 2% of the time, Pallas kernels for 0%

profile of v5, /device:TPU:8, one launch (start us, length us, event | category | flops | bytes accessed | tf_op | source)
XLA Modules:
  0.0 482.8 jit_solution(3672274988927092672)
XLA Ops:
  6.5 30.1 %all_gather.17 = bf16[128,3200]{0,1:T(8,128)(2,1)S(1)} all-gather(bf16[128,400]{0,1:T(8,128)(2,1)} %param.12), channel_id=1, replica_groups=mesh['fsdp'=8,'chip'=8,'core'=2] {'fsdp'}, dimensions={1}, use_global_device_ids=true | all-gather | bytes 921600 | tf_op jit(solution)/shard_map/all_gather | solution.py:73
  36.7 20.8 %all_to_all.39 = bf16[128,16,200]{0,2,1:T(8,128)(2,1)S(1)} all-to-all(bf16[128,16,200]{0,2,1:T(8,128)(2,1)S(1)} %bitcast.102), channel_id=1, replica_groups=mesh['fsdp'=8,'chip'=8,'core'=2] {'chip','core'}, dimensions={1} | all-to-all | bytes 1638400 | tf_op jit(solution)/shard_map/all_to_all | solution.py:74
  57.4 2.6 broadcast_in_dim.88
  60.0 4.4 all-to-all-start
  65.5 36.2 %all-to-all-done = bf16[8,400,384]{2,1,0:T(8,128)(2,1)S(1)} async-done(((bf16[8,400,384]{2,1,0:T(8,128)(2,1)}), bf16[8,400,384]{2,1,0:T(8,128)(2,1)S(1)}, u32[]{:S(2)}, u32[]{:S(2)}) %all-to-all-start) | async-done | bytes 2457632 | tf_op jit(solution)/shard_map/all_to_all | solution.py:57
  101.7 1.5 copy-done
  104.0 1.8 all_gather.19
  106.4 11.3 %all-gather.5.cloned.1.call-done = bf16[3200,768]{1,0:T(8,128)(2,1)} async-done(((bf16[3200,384]{1,0:T(8,128)(2,1)}), bf16[3200,768]{1,0:T(8,128)(2,1)}) %all-gather.5.cloned.1.call-update) | async-done | bytes 4915216 | tf_op jit(solution)/shard_map/all_gather | solution.py:79
  117.7 97.7 %all-gather.9.cloned.1.call-done = bf16[1,1088,3200]{2,1,0:T(8,128)(2,1)} async-done(((bf16[1,136,3200]{2,1,0:T(8,128)(2,1)}), bf16[1,1088,3200]{2,1,0:T(8,128)(2,1)}) %all-gather.9.cloned.1.call-update) | async-done | bytes 6963216 | tf_op jit(solution)/shard_map/all_gather | solution.py:82
  215.5 4.6 fusion.2
  220.4 9.6 %fusion.6 = f32[1088,768]{0,1:T(8,128)S(1)} fusion(bf16[3200,768]{1,0:T(8,128)(2,1)} %all-gather.5.cloned.1.call-done, bf16[1,1088,3200]{2,1,0:T(8,128)(2,1)S(1)} %copy-done.1, f32[3200]{0:T(1024)} %param.9, f32[1088]{0:T(1024)S(1)} %add_rsqrt_fusion), kind=kOutput, calls=%fused_computation.12 | convolution fusion | flops 5361664000 | bytes 15237888 | tf_op jit(solution)/shard_map/dot_general | solution.py:89
  230.9 5.6 %all-to-all-start.2 = ((f32[8,2,1088]{2,1,0:T(2,128)}), f32[8,2,1088]{2,1,0:T(2,128)}, u32[]{:S(2)}, u32[]{:S(2)}) async-start(f32[8,2,1088]{2,1,0:T(2,128)} %broadcast_in_dim.89), calls=%async_computation.2 | async-start | bytes 147456 | tf_op jit(solution)/shard_map/all_to_all | solution.py:51
  237.4 5.9 %all-to-all-done.2 = f32[8,2,1088]{2,1,0:T(2,128)} async-done(((f32[8,2,1088]{2,1,0:T(2,128)}), f32[8,2,1088]{2,1,0:T(2,128)}, u32[]{:S(2)}, u32[]{:S(2)}) %all-to-all-start.2) | async-done | bytes 69664 | tf_op jit(solution)/shard_map/all_to_all | solution.py:51
  247.8 1.4 collective-permute-done
  250.1 3.2 fusion.44
  253.3 4.9 %fusion.12 = bf16[2,1025,128]{2,1,0:T(8,128)(2,1)S(1)} fusion(bf16[2,1025,128]{2,1,0:T(8,128)(2,1)S(1)} %reshape_squeeze.11, f32[2,1025]{1,0:T(2,128)S(1)} %fusion.44, bf16[2,1025,128]{2,1,0:T(8,128)(2,1)S(1)} %reshape_squeeze.9, bf16[2,1025,128]{2,1,0:T(8,128)(2,1)S(1)} %reshape_squeeze.10), kind=kOutput, calls=%fused_computation.18 | convolution fusion | flops 1084510464 | bytes 2107400 | tf_op jit(solution)/shard_map/sqk,skc->sqc/dot_general | solution.py:128
  258.4 3.0 broadcast_in_dim.91
  261.4 5.7 %all-to-all-start.3 = ((bf16[16,1088,128]{2,1,0:T(8,128)(2,1)}), bf16[16,1088,128]{2,1,0:T(8,128)(2,1)}, u32[]{:S(2)}, u32[]{:S(2)}) async-start(bf16[16,1088,128]{2,1,0:T(8,128)(2,1)} %bitcast.92), calls=%async_computation.3 | async-start | bytes 8912896 | tf_op jit(solution)/shard_map/all_to_all | solution.py:141
  268.1 1.9 constant_dynamic-slice_fusion.3
  270.8 56.4 %all-to-all-done.3 = bf16[16,1088,128]{2,1,0:T(8,128)(2,1)} async-done(((bf16[16,1088,128]{2,1,0:T(8,128)(2,1)}), bf16[16,1088,128]{2,1,0:T(8,128)(2,1)}, u32[]{:S(2)}, u32[]{:S(2)}) %all-to-all-start.3) | async-done | bytes 4456480 | tf_op jit(solution)/shard_map/all_to_all | solution.py:141
  327.2 11.6 %convolution_convert_fusion = bf16[16,1088,400]{1,2,0:T(8,128)(2,1)} fusion(bf16[16,1088,128]{2,1,0:T(8,128)(2,1)} %all-to-all-done.3, bf16[2048,400]{0,1:T(8,128)(2,1)} %all-gather.7.cloned.1.call-done), kind=kOutput, calls=%fused_computation.2 | convolution fusion | flops 1789542400 | bytes 20021248 | tf_op jit(solution)/shard_map/hsc,hcd->hsd/dot_general | solution.py:148
  338.8 7.8 %convert_reduce_fusion = f32[1088,400]{0,1:T(8,128)S(1)} fusion(bf16[16,1088,400]{1,2,0:T(8,128)(2,1)} %convolution_convert_fusion), kind=kLoop, calls=%fused_computation.1 | loop fusion | flops 13491200 | bytes 15667200 | tf_op jit(solution)/shard_map/reduce_sum | solution.py:154
  347.4 1.8 collective-permute-done.1
  352.4 4.9 %copy.118 = bf16[16,16,200,2,2]{1,0,4,3,2:T(8,128)(2,1)S(1)} copy(bf16[16,16,200,2,2]{2,4,1,3,0:T(2,128)(2,1)} %bitcast.108) | data formatting | bytes 819200 | tf_op jit(solution)/shard_map/transpose | solution.py:22
  357.3 3.9 stack_reshape.23
  361.2 4.9 %copy.117 = bf16[16,16,200,2,2]{1,0,4,3,2:T(8,128)(2,1)S(1)} copy(bf16[16,16,200,2,2]{2,4,1,3,0:T(2,128)(2,1)} %bitcast.107) | data formatting | bytes 819200 | tf_op jit(solution)/shard_map/transpose | solution.py:22
  366.0 3.8 stack_reshape.22
  371.1 3.3 broadcast_select_fusion
  374.4 4.8 all-to-all-start.4
  390.0 80.9 %all-to-all-done.4 = bf16[8,2,256,800]{2,3,1,0:T(8,128)(2,1)} async-done(((bf16[8,2,256,800]{2,3,1,0:T(8,128)(2,1)}), bf16[8,2,256,800]{2,3,1,0:T(8,128)(2,1)}, u32[]{:S(2)}, u32[]{:S(2)}) %all-to-all-start.4) | async-done | bytes 6553632 | tf_op jit(solution)/shard_map/all_to_all | solution.py:171
  470.9 4.0 dynamic-slice_select_fusion.3
  474.9 1.4 pad_maximum_fusion.2
  (75 shorter events, 20.0 us)
Async XLA Ops:
  60.0 41.7 %all-to-all-start = ((bf16[8,400,384]{2,1,0:T(8,128)(2,1)}), bf16[8,400,384]{2,1,0:T(8,128)(2,1)S(1)}, u32[]{:S(2)}, u32[]{:S(2)}) async-start(bf16[8,400,384]{2,1,0:T(8,128)(2,1)} %broadcast_in_dim.88), calls=%async_computation | async-start | bytes 4915200 | tf_op jit(solution)/shard_map/all_to_all | solution.py:57
  64.4 39.6 %copy-start.3 = (f32[2,128]{1,0:T(2,128)S(1)}, f32[2,128]{1,0:T(2,128)}, u32[]{:S(2)}) copy-start(f32[2,128]{1,0:T(2,128)} %param.11) | copy-start | bytes 3076
  64.4 42.0 %all-gather.7.cloned.1.call-start = ((), (), s32[]{:S(2)}) async-start(), calls=%async_computation.6 | async-start | bytes 2457600 | tf_op jit(solution)/shard_map/all_gather | solution.py:77
  65.5 52.2 %all-gather.5.cloned.1.call-start = ((), (), s32[]{:S(2)}) async-start(), calls=%async_computation.5 | async-start | bytes 7372800 | tf_op jit(solution)/shard_map/all_gather | solution.py:79
  101.7 1.5 copy-start
  103.3 112.2 %all-gather.9.cloned.1.call-start = ((), (), s32[]{:S(2)}) async-start(), calls=%async_computation.7 | async-start | bytes 7833600 | tf_op jit(solution)/shard_map/all_gather | solution.py:82
  215.5 5.0 %copy-start.1 = (bf16[1,1088,3200]{2,1,0:T(8,128)(2,1)S(1)}, bf16[1,1088,3200]{2,1,0:T(8,128)(2,1)}, u32[]{:S(2)}) copy-start(bf16[1,1088,3200]{2,1,0:T(8,128)(2,1)} %all-gather.9.cloned.1.call-done) | copy-start | bytes 20889604
  230.9 12.4 %all-to-all-start.2 = ((f32[8,2,1088]{2,1,0:T(2,128)}), f32[8,2,1088]{2,1,0:T(2,128)}, u32[]{:S(2)}, u32[]{:S(2)}) async-start(f32[8,2,1088]{2,1,0:T(2,128)} %broadcast_in_dim.89), calls=%async_computation.2 | async-start | bytes 147456 | tf_op jit(solution)/shard_map/all_to_all | solution.py:51
  244.2 1.1 copy-start.2
  246.6 2.6 collective-permute-start
  261.4 6.5 %copy-start.4 = (s32[8,2]{0,1:T(2,128)S(1)}, s32[8,2]{0,1:T(2,128)}, u32[]{:S(2)}) copy-start(s32[8,2]{0,1:T(2,128)} %param.14) | copy-start | bytes 196
  261.4 6.5 %copy-start.5 = (s32[8,2]{0,1:T(2,128)S(1)}, s32[8,2]{0,1:T(2,128)}, u32[]{:S(2)}) copy-start(s32[8,2]{0,1:T(2,128)} %param.15) | copy-start | bytes 196
  261.4 65.7 %all-to-all-start.3 = ((bf16[16,1088,128]{2,1,0:T(8,128)(2,1)}), bf16[16,1088,128]{2,1,0:T(8,128)(2,1)}, u32[]{:S(2)}, u32[]{:S(2)}) async-start(bf16[16,1088,128]{2,1,0:T(8,128)(2,1)} %bitcast.92), calls=%async_computation.3 | async-start | bytes 8912896 | tf_op jit(solution)/shard_map/all_to_all | solution.py:141
  347.0 2.2 collective-permute-start.1
  374.4 96.5 %all-to-all-start.4 = ((bf16[8,2,256,800]{2,3,1,0:T(8,128)(2,1)}), bf16[8,2,256,800]{2,3,1,0:T(8,128)(2,1)}, u32[]{:S(2)}, u32[]{:S(2)}) async-start(bf16[8,2,256,800]{2,3,1,0:T(8,128)(2,1)} %broadcast_select_fusion), calls=%async_computation.4 | async-start | bytes 13107200 | tf_op jit(solution)/shard_map/all_to_all | solution.py:171
Sparse Core Ops, SparseCore 0:
  66.9 12.7 all-gather.6
  103.4 14.2 all-gather.4
  120.0 95.3 all-gather.8

commit v6 on v5

--- a/solution.py
+++ b/solution.py
@@ -56,6 +56,13 @@
     spread = jnp.broadcast_to(block_value[None], (groups,) + block_value.shape)
     collected = lax.all_to_all(spread, axis_name, split_axis=0, concat_axis=0, tiled=True)
     return collected.reshape((groups * block_value.shape[0],) + block_value.shape[1:])
+
+
+def pair_up(value, core, swap, axis):
+    other = lax.ppermute(value, "core", swap)
+    low = jnp.where(core == 0, value, other)
+    high = jnp.where(core == 0, other, value)
+    return jnp.concatenate([low, high], axis=axis)
 
 
 def body(tokens, norm_gain, qkv_weight, qk_gain, out_weight, layer_scale, tile_counts, owners):
@@ -74,11 +81,11 @@
     weight_block = lax.all_to_all(
         head_rows, ("chip", "core"), split_axis=1, concat_axis=0, tiled=True
     )
-    pair_weight = lax.all_gather(weight_block, "core", axis=1, tiled=True)
+    pair_weight = pair_up(weight_block, core, swap, 1)
     full_qkv = gather_blocks(qkv_weight, "fsdp", row_count)
-    pair_qkv = lax.all_gather(full_qkv, "core", axis=1, tiled=True)
+    pair_qkv = pair_up(full_qkv, core, swap, 1)
     pair_qkv, pair_weight = lax.optimization_barrier((pair_qkv, pair_weight))
-    pair_gain = lax.all_gather(qk_gain, "core", axis=1, tiled=True).reshape(2, cores, HEAD_DIM)
+    pair_gain = pair_up(qk_gain, core, swap, 1).reshape(2, cores, HEAD_DIM)
     half = lax.all_gather(own_rows, "chip", axis=0, tiled=True)
     half_length = half.shape[0]
     piece = own_rows.shape[0]

time: 484 us -> 409 us (0.85)
  waiting for transfers between devices: 292 us -> 190 us
  blocking collectives: 52.7 us -> 63.1 us
  starting transfers between devices: 21.2 us -> 31.4 us
  other arithmetic: 28.8 us -> 36.7 us
    all_gather x1, waiting for transfers between devices: 97.7 us -> 26.6 us  [body(): half = lax.all_gather(own_rows, 'chip', axis=0, tiled=True)]
    all_to_all x1, waiting for transfers between devices: 36.2 us -> 0.01 us  [gather_blocks(): lax.all_to_all(spread, axis_name, split_axis=0, concat_axis=0, tiled=True)]
    all_gather x1, blocking collectives: 30.1 us -> 63.1 us  [body(): head_rows = lax.all_gather(out_weight, 'fsdp', axis=1, tiled=True)]
    all_to_all x1 -> x0, blocking collectives: 20.8 us -> none  [body(): lax.all_to_all(head_rows, ('chip', 'core'), split_axis=1, concat_axis=0,...]
    all_to_all x0 -> x1, waiting for transfers between devices: none -> 15 us  [body(): lax.all_to_all(head_rows, ('chip', 'core'), split_axis=1, concat_axis=0,...]
    all_gather x2 -> x0, waiting for transfers between devices: 11.3 us -> none  [the longest x1 11.3 us: body(): pair_qkv = lax.all_gather(full_qkv, 'core', axis=1, tiled=True)]
    all_to_all x0 -> x1, starting transfers between devices: none -> 8.23 us  [body(): lax.all_to_all(head_rows, ('chip', 'core'), split_axis=1, concat_axis=0,...]
  transfers between devices with their start and end apart: 9 -> 11, of which waited for: 8 -> 8; matrix products, arithmetic and copies ran while one was open for 2% -> 5% of each run, Pallas kernels for 0% -> 0%
where the time goes in v6:
time: 409 us; the launch traced here: 408 us
  waiting for transfers between devices  190 us (46%)
  blocking collectives  63.1 us (15%)
  other arithmetic  36.7 us (9%)
  local copies, waits for them, and re-layouts  36.2 us (9%)
  starting transfers between devices  31.4 us (8%)
  matrix products  29 us (7%)
  between operations  21.5 us (5%)
    all_to_all x1, waiting for transfers between devices, body(): lax.all_to_all(outgoing, 'fsdp', split_axis=0, concat_axis=0, tiled=True)  80.9 us
    all_gather x1, blocking collectives, body(): head_rows = lax.all_gather(out_weight, 'fsdp', axis=1, tiled=True)  63.1 us
    all_to_all x1, waiting for transfers between devices, body(): lax.all_to_all(outgoing.reshape(groups, half_length, HEAD_DIM), ('chip',...  55.5 us
    all_gather x1, waiting for transfers between devices, body(): half = lax.all_gather(own_rows, 'chip', axis=0, tiled=True)  26.6 us
    all_to_all x1, waiting for transfers between devices, body(): lax.all_to_all(head_rows, ('chip', 'core'), split_axis=1, concat_axis=0,...  15 us
    dot_general x1, matrix products, body(): jnp.einsum('hsc,hcd->hsd', all_heads, pair_weight.reshape(groups, HEAD_DI...  11.4 us
    transpose x2, local copies, waits for them, and re-layouts, merge_tiles(): patches.reshape(halves, 2, halves, 2, columns).transpose(0, 2, 4, 1, 3)  9.74 us
    dot_general x1, matrix products, body(): projected = jnp.dot(normed, pair_qkv, preferred_element_type=jnp.float32)  9.55 us
  transfers between devices with their start and end apart: 11, of which 8 were waited for; matrix products, arithmetic and copies ran while one was open for 5% of the time, Pallas kernels for 0%

profile of v6, /device:TPU:8, one launch (start us, length us, event | category | flops | bytes accessed | tf_op | source)
XLA Modules:
  0.0 408.2 jit_solution(5735256708975385093)
XLA Ops:
  7.3 2.7 broadcast_in_dim.88
  9.9 5.8 %all-to-all-start = ((bf16[8,400,384]{2,1,0:T(8,128)(2,1)}), bf16[8,400,384]{2,1,0:T(8,128)(2,1)S(1)}, u32[]{:S(2)}, u32[]{:S(2)}) async-start(bf16[8,400,384]{2,1,0:T(8,128)(2,1)} %broadcast_in_dim.88), calls=%async_computation | async-start | bytes 4915200 | tf_op jit(solution)/shard_map/all_to_all | solution.py:57
  15.7 63.1 %all_gather.7 = bf16[128,3200]{0,1:T(8,128)(2,1)} all-gather(bf16[128,400]{0,1:T(8,128)(2,1)S(1)} %copy-done.4), channel_id=1, replica_groups=mesh['fsdp'=8,'chip'=8,'core'=2] {'fsdp'}, dimensions={1}, use_global_device_ids=true | all-gather | bytes 921600 | tf_op jit(solution)/shard_map/all_gather | solution.py:80
  78.9 8.2 %all-to-all-start.1 = ((bf16[128,16,200]{0,2,1:T(8,128)(2,1)}), bf16[128,16,200]{0,2,1:T(8,128)(2,1)S(1)}, u32[]{:S(2)}, u32[]{:S(2)}) async-start(bf16[128,16,200]{0,2,1:T(8,128)(2,1)} %bitcast.110), calls=%async_computation.1 | async-start | bytes 1638400 | tf_op jit(solution)/shard_map/all_to_all | solution.py:81
  87.2 15.0 %all-to-all-done.1 = bf16[128,16,200]{0,2,1:T(8,128)(2,1)S(1)} async-done(((bf16[128,16,200]{0,2,1:T(8,128)(2,1)}), bf16[128,16,200]{0,2,1:T(8,128)(2,1)S(1)}, u32[]{:S(2)}, u32[]{:S(2)}) %all-to-all-start.1) | async-done | bytes 819232 | tf_op jit(solution)/shard_map/all_to_all | solution.py:81
  103.9 2.3 collective-permute-done.2
  106.7 1.5 broadcast_select_fusion.4
  109.5 2.1 broadcast_select_fusion.2
  111.6 2.7 pad_maximum_fusion
  114.3 26.6 %all-gather.3.cloned.1.call-done = bf16[1,1088,3200]{2,1,0:T(8,128)(2,1)} async-done(((bf16[1,136,3200]{2,1,0:T(8,128)(2,1)}), bf16[1,1088,3200]{2,1,0:T(8,128)(2,1)}) %all-gather.3.cloned.1.call-update) | async-done | bytes 6963216 | tf_op jit(solution)/shard_map/all_gather | solution.py:89
  140.9 4.6 %fusion.2 = f32[1088]{0:T(1024)S(1)} fusion(bf16[1,1088,3200]{2,1,0:T(8,128)(2,1)} %all-gather.3.cloned.1.call-done), kind=kLoop, calls=%fused_computation.7 | loop fusion | flops 10443712 | bytes 6967552 | tf_op jit(solution)/shard_map/reduce_sum | solution.py:94
  145.9 9.5 %fusion.6 = f32[1088,768]{0,1:T(8,128)S(1)} fusion(bf16[3200,768]{1,0:T(8,128)(2,1)} %pad_maximum_fusion, bf16[1,1088,3200]{2,1,0:T(8,128)(2,1)S(1)} %copy-done, f32[3200]{0:T(1024)S(1)} %copy-done.8, f32[1088]{0:T(1024)S(1)} %add_rsqrt_fusion), kind=kOutput, calls=%fused_computation.12 | convolution fusion | flops 5361664000 | bytes 15237888 | tf_op jit(solution)/shard_map/dot_general | solution.py:96
  156.3 5.5 %all-to-all-start.2 = ((f32[8,2,1088]{2,1,0:T(2,128)}), f32[8,2,1088]{2,1,0:T(2,128)}, u32[]{:S(2)}, u32[]{:S(2)}) async-start(f32[8,2,1088]{2,1,0:T(2,128)} %broadcast_in_dim.89), calls=%async_computation.2 | async-start | bytes 147456 | tf_op jit(solution)/shard_map/all_to_all | solution.py:51
  162.8 5.9 %all-to-all-done.2 = f32[8,2,1088]{2,1,0:T(2,128)} async-done(((f32[8,2,1088]{2,1,0:T(2,128)}), f32[8,2,1088]{2,1,0:T(2,128)}, u32[]{:S(2)}, u32[]{:S(2)}) %all-to-all-start.2) | async-done | bytes 69664 | tf_op jit(solution)/shard_map/all_to_all | solution.py:51
  175.4 3.2 fusion.44
  178.7 4.9 %fusion.12 = bf16[2,1025,128]{2,1,0:T(8,128)(2,1)S(1)} fusion(bf16[2,1025,128]{2,1,0:T(8,128)(2,1)S(1)} %reshape_squeeze.11, f32[2,1025]{1,0:T(2,128)S(1)} %fusion.44, bf16[2,1025,128]{2,1,0:T(8,128)(2,1)S(1)} %reshape_squeeze.9, bf16[2,1025,128]{2,1,0:T(8,128)(2,1)S(1)} %reshape_squeeze.10), kind=kOutput, calls=%fused_computation.19 | convolution fusion | flops 1084510464 | bytes 2107400 | tf_op jit(solution)/shard_map/sqk,skc->sqc/dot_general | solution.py:135
  183.7 3.0 broadcast_in_dim.91
  186.8 5.7 %all-to-all-start.3 = ((bf16[16,1088,128]{2,1,0:T(8,128)(2,1)}), bf16[16,1088,128]{2,1,0:T(8,128)(2,1)}, u32[]{:S(2)}, u32[]{:S(2)}) async-start(bf16[16,1088,128]{2,1,0:T(8,128)(2,1)} %bitcast.100), calls=%async_computation.3 | async-start | bytes 8912896 | tf_op jit(solution)/shard_map/all_to_all | solution.py:148
  193.6 1.9 constant_dynamic-slice_fusion.3
  195.4 1.6 copy.123
  197.0 55.5 %all-to-all-done.3 = bf16[16,1088,128]{2,1,0:T(8,128)(2,1)} async-done(((bf16[16,1088,128]{2,1,0:T(8,128)(2,1)}), bf16[16,1088,128]{2,1,0:T(8,128)(2,1)}, u32[]{:S(2)}, u32[]{:S(2)}) %all-to-all-start.3) | async-done | bytes 4456480 | tf_op jit(solution)/shard_map/all_to_all | solution.py:148
  252.5 11.4 %convolution_convert_fusion = bf16[16,1088,400]{1,2,0:T(8,128)(2,1)} fusion(bf16[16,1088,128]{2,1,0:T(8,128)(2,1)} %all-to-all-done.3, bf16[2048,400]{0,1:T(8,128)(2,1)S(1)} %copy-done.1), kind=kOutput, calls=%fused_computation.2 | convolution fusion | flops 1789542400 | bytes 20021248 | tf_op jit(solution)/shard_map/hsc,hcd->hsd/dot_general | solution.py:155
  263.9 7.8 %convert_reduce_fusion = f32[1088,400]{0,1:T(8,128)S(1)} fusion(bf16[16,1088,400]{1,2,0:T(8,128)(2,1)} %convolution_convert_fusion), kind=kLoop, calls=%fused_computation.1 | loop fusion | flops 13491200 | bytes 15667200 | tf_op jit(solution)/shard_map/reduce_sum | solution.py:161
  272.5 1.8 collective-permute-done.4
  277.6 4.9 %copy.118 = bf16[16,16,200,2,2]{1,0,4,3,2:T(8,128)(2,1)S(1)} copy(bf16[16,16,200,2,2]{2,4,1,3,0:T(2,128)(2,1)} %bitcast.116) | data formatting | bytes 819200 | tf_op jit(solution)/shard_map/transpose | solution.py:22
  282.5 3.9 stack_reshape.23
  286.3 4.9 %copy.117 = bf16[16,16,200,2,2]{1,0,4,3,2:T(8,128)(2,1)S(1)} copy(bf16[16,16,200,2,2]{2,4,1,3,0:T(2,128)(2,1)} %bitcast.115) | data formatting | bytes 819200 | tf_op jit(solution)/shard_map/transpose | solution.py:22
  291.2 3.8 stack_reshape.22
  296.3 3.3 broadcast_select_fusion
  299.6 4.8 %all-to-all-start.4 = ((bf16[8,2,256,800]{2,3,1,0:T(8,128)(2,1)}), bf16[8,2,256,800]{2,3,1,0:T(8,128)(2,1)}, u32[]{:S(2)}, u32[]{:S(2)}) async-start(bf16[8,2,256,800]{2,3,1,0:T(8,128)(2,1)} %broadcast_select_fusion), calls=%async_computation.4 | async-start | bytes 13107200 | tf_op jit(solution)/shard_map/all_to_all | solution.py:178
  315.2 80.9 %all-to-all-done.4 = bf16[8,2,256,800]{2,3,1,0:T(8,128)(2,1)} async-done(((bf16[8,2,256,800]{2,3,1,0:T(8,128)(2,1)}), bf16[8,2,256,800]{2,3,1,0:T(8,128)(2,1)}, u32[]{:S(2)}, u32[]{:S(2)}) %all-to-all-start.4) | async-done | bytes 6553632 | tf_op jit(solution)/shard_map/all_to_all | solution.py:178
  396.1 3.9 dynamic-slice_select_fusion.3
  (86 shorter events, 24.1 us)
Async XLA Ops:
  6.5 134.4 %all-gather.3.cloned.1.call-start = ((), (), s32[]{:S(2)}) async-start(), calls=%async_computation.5 | async-start | bytes 7833600 | tf_op jit(solution)/shard_map/all_gather | solution.py:89
  9.9 5.8 %copy-start.4 = (bf16[128,400]{0,1:T(8,128)(2,1)S(1)}, bf16[128,400]{0,1:T(8,128)(2,1)}, u32[]{:S(2)}) copy-start(bf16[128,400]{0,1:T(8,128)(2,1)} %param.12) | copy-start | bytes 307204
  9.9 69.0 %all-to-all-start = ((bf16[8,400,384]{2,1,0:T(8,128)(2,1)}), bf16[8,400,384]{2,1,0:T(8,128)(2,1)S(1)}, u32[]{:S(2)}, u32[]{:S(2)}) async-start(bf16[8,400,384]{2,1,0:T(8,128)(2,1)} %broadcast_in_dim.88), calls=%async_computation | async-start | bytes 4915200 | tf_op jit(solution)/shard_map/all_to_all | solution.py:57
  15.7 88.1 %copy-start.7 = (f32[2,128]{1,0:T(2,128)S(1)}, f32[2,128]{1,0:T(2,128)}, u32[]{:S(2)}) copy-start(f32[2,128]{1,0:T(2,128)} %param.11) | copy-start | bytes 3076
  78.9 23.3 %all-to-all-start.1 = ((bf16[128,16,200]{0,2,1:T(8,128)(2,1)}), bf16[128,16,200]{0,2,1:T(8,128)(2,1)S(1)}, u32[]{:S(2)}, u32[]{:S(2)}) async-start(bf16[128,16,200]{0,2,1:T(8,128)(2,1)} %bitcast.110), calls=%async_computation.1 | async-start | bytes 1638400 | tf_op jit(solution)/shard_map/all_to_all | solution.py:81
  87.1 22.3 %collective-permute-start = (bf16[3200,384]{1,0:T(8,128)(2,1)S(1)}, bf16[3200,384]{1,0:T(8,128)(2,1)}, u32[]{:S(2)}, u32[]{:S(2)}) collective-permute-start(bf16[3200,384]{1,0:T(8,128)(2,1)S(1)} %bitcast.101), channel_id=1, source_target_pairs={{0,1},{1,0},{2,3},{3,2},{4,5},{5,4},{6,7},{7,6},{8,9},{9,8},{10,11... | collective-permute-start | bytes 7372808 | tf_op jit(solution)/shard_map/ppermute | solution.py:62
  103.2 3.5 collective-permute-start.1
  103.9 2.3 collective-permute-start.2
  140.9 5.0 %copy-start = (bf16[1,1088,3200]{2,1,0:T(8,128)(2,1)S(1)}, bf16[1,1088,3200]{2,1,0:T(8,128)(2,1)}, u32[]{:S(2)}) copy-start(bf16[1,1088,3200]{2,1,0:T(8,128)(2,1)} %all-gather.3.cloned.1.call-done) | copy-start | bytes 20889604
  140.9 5.0 %copy-start.8 = (f32[3200]{0:T(1024)S(1)}, f32[3200]{0:T(1024)}, u32[]{:S(2)}) copy-start(f32[3200]{0:T(1024)} %param.9) | copy-start | bytes 38404
  156.3 12.3 %all-to-all-start.2 = ((f32[8,2,1088]{2,1,0:T(2,128)}), f32[8,2,1088]{2,1,0:T(2,128)}, u32[]{:S(2)}, u32[]{:S(2)}) async-start(f32[8,2,1088]{2,1,0:T(2,128)} %broadcast_in_dim.89), calls=%async_computation.2 | async-start | bytes 147456 | tf_op jit(solution)/shard_map/all_to_all | solution.py:51
  169.6 1.1 copy-start.3
  172.0 2.6 collective-permute-start.3
  186.8 6.6 %copy-start.5 = (s32[8,2]{0,1:T(2,128)S(1)}, s32[8,2]{0,1:T(2,128)}, u32[]{:S(2)}) copy-start(s32[8,2]{0,1:T(2,128)} %param.14) | copy-start | bytes 196
  186.8 6.6 %copy-start.6 = (s32[8,2]{0,1:T(2,128)S(1)}, s32[8,2]{0,1:T(2,128)}, u32[]{:S(2)}) copy-start(s32[8,2]{0,1:T(2,128)} %param.15) | copy-start | bytes 196
  186.8 65.7 %all-to-all-start.3 = ((bf16[16,1088,128]{2,1,0:T(8,128)(2,1)}), bf16[16,1088,128]{2,1,0:T(8,128)(2,1)}, u32[]{:S(2)}, u32[]{:S(2)}) async-start(bf16[16,1088,128]{2,1,0:T(8,128)(2,1)} %bitcast.100), calls=%async_computation.3 | async-start | bytes 8912896 | tf_op jit(solution)/shard_map/all_to_all | solution.py:148
  192.5 60.0 %copy-start.1 = (bf16[2048,400]{0,1:T(8,128)(2,1)S(1)}, bf16[2048,400]{0,1:T(8,128)(2,1)}, u32[]{:S(2)}) copy-start(bf16[2048,400]{0,1:T(8,128)(2,1)} %pad_maximum_fusion.3) | copy-start | bytes 4915204
  263.9 7.8 %copy-start.2 = (bf16[1,1088,400]{1,2,0:T(8,128)(2,1)S(1)}, bf16[1,1088,400]{1,2,0:T(8,128)(2,1)}, u32[]{:S(2)}) copy-start(bf16[1,1088,400]{1,2,0:T(8,128)(2,1)} %copy.123) | copy-start | bytes 2611204
  272.1 2.2 collective-permute-start.4
  299.6 96.5 %all-to-all-start.4 = ((bf16[8,2,256,800]{2,3,1,0:T(8,128)(2,1)}), bf16[8,2,256,800]{2,3,1,0:T(8,128)(2,1)}, u32[]{:S(2)}, u32[]{:S(2)}) async-start(bf16[8,2,256,800]{2,3,1,0:T(8,128)(2,1)} %broadcast_select_fusion), calls=%async_computation.4 | async-start | bytes 13107200 | tf_op jit(solution)/shard_map/all_to_all | solution.py:178
Sparse Core Ops, SparseCore 0:
  9.7 131.2 all-gather.2

commit v7 on v4

--- a/solution.py
+++ b/solution.py
@@ -66,10 +66,7 @@
     row_count = lax.axis_size("fsdp")
     model_width = own_rows.shape[1]
     block = model_width // groups
-    head_rows = lax.all_gather(out_weight, "fsdp", axis=1, tiled=True)
-    weight_block = lax.all_to_all(head_rows, "dp", split_axis=1, concat_axis=0, tiled=True)
     full_qkv = gather_blocks(qkv_weight, "fsdp", row_count)
-    full_qkv, weight_block = lax.optimization_barrier((full_qkv, weight_block))
     gathered = lax.all_gather(own_rows, "dp", axis=0, tiled=True)
     values = gathered.astype(jnp.float32)
     normed = (
@@ -113,7 +110,14 @@
         tile_out = jnp.dot(weights, tile_value, preferred_element_type=jnp.float32).astype(
             jnp.bfloat16
         )
+        if not slot_received:
+            late_weight, tile_out = lax.optimization_barrier((out_weight, tile_out))
         all_heads = lax.all_gather(tile_out, "dp", axis=0, tiled=False)
+        if not slot_received:
+            head_rows = lax.all_gather(late_weight, "fsdp", axis=1, tiled=True)
+            weight_block = lax.all_to_all(
+                head_rows, "dp", split_axis=1, concat_axis=0, tiled=True
+            )
         if slot_received:
             all_heads, slot_received[-1] = lax.optimization_barrier((all_heads, slot_received[-1]))
         head_terms = jnp.einsum(

time: 417 us -> 413 us (level)
  blocking collectives: 52.5 us -> 32.9 us
  starting transfers between devices: 19 us -> 30.7 us
    all_gather x1, waiting for transfers between devices: 40 us -> 111 us  [body(): gathered = lax.all_gather(own_rows, 'dp', axis=0, tiled=True)]
    all_gather x2, waiting for transfers between devices: 103 us -> 59.9 us  [body(): all_heads = lax.all_gather(tile_out, 'dp', axis=0, tiled=False)]
    all_to_all x1, waiting for transfers between devices: 37.3 us -> 0.01 us  [gather_blocks(): lax.all_to_all(spread, axis_name, split_axis=0, concat_axis=0, tiled=True)]
    all_to_all x1 -> x0, blocking collectives: 20.6 us -> none  [body(): lax.all_to_all(head_rows, 'dp', split_axis=1, concat_axis=0, tiled=True)]
    all_to_all x0 -> x1, waiting for transfers between devices: none -> 11.8 us  [body(): lax.all_to_all(head_rows, 'dp', split_axis=1, concat_axis=0, tiled=True)]
    all_to_all x0 -> x1, starting transfers between devices: none -> 5.69 us  [body(): lax.all_to_all(head_rows, 'dp', split_axis=1, concat_axis=0, tiled=True)]
  transfers between devices with their start and end apart: 7 -> 8, of which waited for: 6 -> 6; matrix products, arithmetic and copies ran while one was open for 9% -> 11% of each run, Pallas kernels for 0% -> 0%
where the time goes in v7:
time: 413 us; the launch traced here: 412 us
  waiting for transfers between devices  228 us (55%)
  local copies, waits for them, and re-layouts  36.5 us (9%)
  blocking collectives  32.9 us (8%)
  other arithmetic  32.3 us (8%)
  matrix products  31 us (8%)
  starting transfers between devices  30.7 us (7%)
  between operations  20.8 us (5%)
    all_gather x1, waiting for transfers between devices, body(): gathered = lax.all_gather(own_rows, 'dp', axis=0, tiled=True)  111 us
    all_gather x2, waiting for transfers between devices, body(): all_heads = lax.all_gather(tile_out, 'dp', axis=0, tiled=False)  59.9 us
    all_to_all x2, waiting for transfers between devices, body(): lax.all_to_all(outgoing, 'fsdp', split_axis=0, concat_axis=0, tiled=True)  36.7 us
    all_gather x1, blocking collectives, body(): head_rows = lax.all_gather(late_weight, 'fsdp', axis=1, tiled=True)  32.9 us
    all_to_all x2, starting transfers between devices, body(): lax.all_to_all(outgoing, 'fsdp', split_axis=0, concat_axis=0, tiled=True)  13.2 us
    dot_general x1, matrix products, body(): projected = jnp.dot(normed, full_qkv, preferred_element_type=jnp.float32)  12.8 us
    all_to_all x1, waiting for transfers between devices, body(): lax.all_to_all(head_rows, 'dp', split_axis=1, concat_axis=0, tiled=True)  11.8 us
    transpose x2, local copies, waits for them, and re-layouts, body(): updated.reshape(halves, 2, halves, 2, block).transpose(0, 2, 4, 1, 3)  10.4 us
  transfers between devices with their start and end apart: 8, of which 6 were waited for; matrix products, arithmetic and copies ran while one was open for 11% of the time, Pallas kernels for 0%

profile of v7, /device:TPU:8, one launch (start us, length us, event | category | flops | bytes accessed | tf_op | source)
XLA Modules:
  0.0 411.8 jit_solution(36467992526789169)
XLA Ops:
  7.3 2.6 broadcast_in_dim.99
  9.9 5.7 %all-to-all-start = ((bf16[8,400,384]{2,1,0:T(8,128)(2,1)}), bf16[8,400,384]{2,1,0:T(8,128)(2,1)S(1)}, u32[]{:S(2)}, u32[]{:S(2)}) async-start(bf16[8,400,384]{2,1,0:T(8,128)(2,1)} %broadcast_in_dim.99), calls=%async_computation | async-start | bytes 4915200 | tf_op jit(solution)/shard_map/all_to_all | solution.py:57
  15.5 111.4 %all-gather.7.cloned.1.call-done = bf16[1,2176,3200]{2,1,0:T(8,128)(2,1)} async-done(((bf16[1,136,3200]{2,1,0:T(8,128)(2,1)}), bf16[1,2176,3200]{2,1,0:T(8,128)(2,1)}) %all-gather.7.cloned.1.call-update) | async-done | bytes 13926416 | tf_op jit(solution)/shard_map/all_gather | solution.py:70
  127.0 7.7 %fusion = f32[2176]{0:T(1024)S(1)} fusion(bf16[1,2176,3200]{2,1,0:T(8,128)(2,1)} %all-gather.7.cloned.1.call-done), kind=kLoop, calls=%fused_computation.2 | loop fusion | flops 20887424 | bytes 13935104 | tf_op jit(solution)/shard_map/reduce_sum | solution.py:73
  136.1 12.8 %fusion.38 = (bf16[2176,384]{1,0:T(8,128)(2,1)}, f32[2176,384]{1,0:T(8,128)S(1)}) fusion(bf16[3200,384]{1,0:T(8,128)(2,1)} %bitcast.66, bf16[1,2176,3200]{2,1,0:T(8,128)(2,1)} %all-gather.7.cloned.1.call-done, f32[3200]{0:T(1024)S(1)} %copy-done.9, f32[2176]{0:T(1024)S(1)} %add_rsqrt_fusion), kind=kOutput, calls=%fused_computation.92 | convolution fusion | flops 5376425984 | bytes 21419008 | tf_op jit(solution)/shard_map/dot_general | solution.py:75
  150.4 5.8 %all-to-all-start.1 = ((f32[16,2,2176]{2,1,0:T(2,128)}), f32[16,2,2176]{2,1,0:T(2,128)}, u32[]{:S(2)}, u32[]{:S(2)}) async-start(f32[16,2,2176]{2,1,0:T(2,128)} %broadcast_in_dim.100), calls=%async_computation.1 | async-start | bytes 557056 | tf_op jit(solution)/shard_map/all_to_all | solution.py:51
  156.3 7.1 %all-to-all-done.1 = f32[16,2,2176]{2,1,0:T(2,128)} async-done(((f32[16,2,2176]{2,1,0:T(2,128)}), f32[16,2,2176]{2,1,0:T(2,128)}, u32[]{:S(2)}, u32[]{:S(2)}) %all-to-all-start.1) | async-done | bytes 278560 | tf_op jit(solution)/shard_map/all_to_all | solution.py:51
  168.0 2.6 fusion.12
  170.8 1.8 fusion.37
  173.3 2.7 fusion.13
  177.0 32.9 %all_gather.23 = bf16[128,3200]{0,1:T(8,128)(2,1)} all-gather(bf16[128,400]{0,1:T(8,128)(2,1)S(1)} %copy-done.5), channel_id=1, replica_groups=mesh['fsdp'=8,'dp'=16] {'fsdp'}, dimensions={1}, use_global_device_ids=true | all-gather | bytes 921600 | tf_op jit(solution)/shard_map/all_gather | solution.py:117
  209.9 5.7 %all-to-all-start.2 = ((bf16[128,16,200]{0,2,1:T(8,128)(2,1)}), bf16[128,16,200]{0,2,1:T(8,128)(2,1)S(1)}, u32[]{:S(2)}, u32[]{:S(2)}) async-start(bf16[128,16,200]{0,2,1:T(8,128)(2,1)} %bitcast.15), calls=%async_computation.2 | async-start | bytes 1638400 | tf_op jit(solution)/shard_map/all_to_all | solution.py:118
  215.7 2.8 constant_dynamic-slice_fusion.1
  218.7 11.8 %all-to-all-done.2 = bf16[128,16,200]{0,2,1:T(8,128)(2,1)S(1)} async-done(((bf16[128,16,200]{0,2,1:T(8,128)(2,1)}), bf16[128,16,200]{0,2,1:T(8,128)(2,1)S(1)}, u32[]{:S(2)}, u32[]{:S(2)}) %all-to-all-start.2) | async-done | bytes 819232 | tf_op jit(solution)/shard_map/all_to_all | solution.py:118
  230.5 2.2 all-gather.11.cloned.1.call-done
  232.7 5.0 %convolution_convert_fusion.1 = bf16[16,1024,200]{1,2,0:T(8,128)(2,1)S(1)} fusion(bf16[16,1024,128]{2,1,0:T(8,128)(2,1)} %bitcast.65, bf16[128,16,200]{0,2,1:T(8,128)(2,1)S(1)} %all-to-all-done.2), kind=kOutput, calls=%fused_computation.12 | convolution fusion | flops 842137600 | bytes 11567104 | tf_op jit(solution)/shard_map/hsc,hcd->hsd/dot_general | solution.py:123
  240.7 4.9 %copy.40 = bf16[16,16,200,2,2]{1,0,4,3,2:T(8,128)(2,1)S(1)} copy(bf16[16,16,200,2,2]{2,4,1,3,0:T(2,128)(2,1)} %bitcast.67) | data formatting | bytes 819200 | tf_op jit(solution)/shard_map/transpose | solution.py:132
  245.6 3.9 broadcast_in_dim.103
  249.5 3.0 broadcast_select_fusion.1
  252.5 8.4 %all-to-all-start.3 = ((bf16[8,256,800]{1,2,0:T(8,128)(2,1)}), bf16[8,256,800]{1,2,0:T(8,128)(2,1)S(1)}, u32[]{:S(2)}, u32[]{:S(2)}) async-start(bf16[8,256,800]{1,2,0:T(8,128)(2,1)} %broadcast_select_fusion.1), calls=%async_computation.3 | async-start | bytes 6553600 | tf_op jit(solution)/shard_map/all_to_all | solution.py:138
  260.9 2.0 copy.49
  262.9 57.7 %all-gather.9.cloned.1.call-done = bf16[16384,128]{1,0:T(8,128)(2,1)} async-done(((bf16[1024,128]{1,0:T(8,128)(2,1)}), bf16[16384,128]{1,0:T(8,128)(2,1)}) %all-gather.9.cloned.1.call-update) | async-done | bytes 4194320 | tf_op jit(solution)/shard_map/all_gather | solution.py:115
  320.6 5.3 %convolution_convert_fusion = bf16[16,1024,200]{1,2,0:T(8,128)(2,1)S(1)} fusion(bf16[16,1024,128]{2,1,0:T(8,128)(2,1)} %bitcast.64, bf16[128,16,200]{0,2,1:T(8,128)(2,1)} %copy-done), kind=kOutput, calls=%fused_computation.11 | convolution fusion | flops 842137600 | bytes 11567104 | tf_op jit(solution)/shard_map/hsc,hcd->hsd/dot_general | solution.py:123
  328.4 2.0 copy.41
  330.4 2.1 reshape.164
  332.5 5.6 %copy.42 = bf16[16,16,200,2,2]{1,0,4,3,2:T(8,128)(2,1)} copy(bf16[16,16,200,2,2]{2,4,1,3,0:T(2,128)(2,1)} %bitcast.68) | data formatting | bytes 819200 | tf_op jit(solution)/shard_map/transpose | solution.py:132
  338.0 5.2 %broadcast_in_dim.108 = bf16[256,800]{0,1:T(8,128)(2,1)} reshape(bf16[16,16,200,2,2]{1,0,4,3,2:T(8,128)(2,1)} %copy.42) | data formatting | bytes 819200 | tf_op jit(solution)/shard_map/jit(_where)/broadcast_in_dim | solution.py:134
  343.3 3.0 broadcast_select_fusion
  346.3 4.8 %all-to-all-start.4 = ((bf16[8,256,800]{1,2,0:T(8,128)(2,1)}), bf16[8,256,800]{1,2,0:T(8,128)(2,1)}, u32[]{:S(2)}, u32[]{:S(2)}) async-start(bf16[8,256,800]{1,2,0:T(8,128)(2,1)} %broadcast_select_fusion), calls=%async_computation.4 | async-start | bytes 6553600 | tf_op jit(solution)/shard_map/all_to_all | solution.py:138
  362.1 36.7 %all-to-all-done.4 = bf16[8,256,800]{1,2,0:T(8,128)(2,1)} async-done(((bf16[8,256,800]{1,2,0:T(8,128)(2,1)}), bf16[8,256,800]{1,2,0:T(8,128)(2,1)}, u32[]{:S(2)}, u32[]{:S(2)}) %all-to-all-start.4) | async-done | bytes 3276832 | tf_op jit(solution)/shard_map/all_to_all | solution.py:138
  398.8 2.5 pad_maximum_fusion
  401.4 2.6 dynamic-slice_select_fusion.3
  (66 shorter events, 20.7 us)
Async XLA Ops:
  6.5 120.4 %all-gather.7.cloned.1.call-start = ((), (), s32[]{:S(2)}) async-start(), calls=%async_computation.5 | async-start | bytes 14796800 | tf_op jit(solution)/shard_map/all_gather | solution.py:70
  9.9 124.8 %all-to-all-start = ((bf16[8,400,384]{2,1,0:T(8,128)(2,1)}), bf16[8,400,384]{2,1,0:T(8,128)(2,1)S(1)}, u32[]{:S(2)}, u32[]{:S(2)}) async-start(bf16[8,400,384]{2,1,0:T(8,128)(2,1)} %broadcast_in_dim.99), calls=%async_computation | async-start | bytes 4915200 | tf_op jit(solution)/shard_map/all_to_all | solution.py:57
  15.5 120.6 %copy-start.9 = (f32[3200]{0:T(1024)S(1)}, f32[3200]{0:T(1024)}, u32[]{:S(2)}) copy-start(f32[3200]{0:T(1024)} %param.9) | copy-start | bytes 38404
  134.7 1.4 copy-start.1
  136.1 20.2 %copy-start.6 = (f32[2,128]{1,0:T(2,128)S(1)}, f32[2,128]{1,0:T(2,128)}, u32[]{:S(2)}) copy-start(f32[2,128]{1,0:T(2,128)} %param.11) | copy-start | bytes 3076
  150.4 13.0 %all-to-all-start.1 = ((f32[16,2,2176]{2,1,0:T(2,128)}), f32[16,2,2176]{2,1,0:T(2,128)}, u32[]{:S(2)}, u32[]{:S(2)}) async-start(f32[16,2,2176]{2,1,0:T(2,128)} %broadcast_in_dim.100), calls=%async_computation.1 | async-start | bytes 557056 | tf_op jit(solution)/shard_map/all_to_all | solution.py:51
  156.3 76.4 %all-gather.11.cloned.1.call-start = ((), (), s32[]{:S(2)}) async-start(), calls=%async_computation.7 | async-start | bytes 4456448 | tf_op jit(solution)/shard_map/all_gather | solution.py:115
  165.8 0.8 copy-start.2
  165.8 1.6 copy-start.3
  170.6 150.0 %all-gather.9.cloned.1.call-start = ((), (), s32[]{:S(2)}) async-start(), calls=%async_computation.6 | async-start | bytes 4456448 | tf_op jit(solution)/shard_map/all_gather | solution.py:115
  173.3 3.6 copy-start.7
  173.3 3.6 copy-start.8
  173.3 3.7 copy-start.5
  209.9 20.6 %all-to-all-start.2 = ((bf16[128,16,200]{0,2,1:T(8,128)(2,1)}), bf16[128,16,200]{0,2,1:T(8,128)(2,1)S(1)}, u32[]{:S(2)}, u32[]{:S(2)}) async-start(bf16[128,16,200]{0,2,1:T(8,128)(2,1)} %bitcast.15), calls=%async_computation.2 | async-start | bytes 1638400 | tf_op jit(solution)/shard_map/all_to_all | solution.py:118
  230.5 7.2 %copy-start = (bf16[128,16,200]{0,2,1:T(8,128)(2,1)}, bf16[128,16,200]{0,2,1:T(8,128)(2,1)S(1)}, u32[]{:S(2)}) copy-start(bf16[128,16,200]{0,2,1:T(8,128)(2,1)S(1)} %all-to-all-done.2) | copy-start | bytes 2457604
  252.5 68.1 %all-to-all-start.3 = ((bf16[8,256,800]{1,2,0:T(8,128)(2,1)}), bf16[8,256,800]{1,2,0:T(8,128)(2,1)S(1)}, u32[]{:S(2)}, u32[]{:S(2)}) async-start(bf16[8,256,800]{1,2,0:T(8,128)(2,1)} %broadcast_select_fusion.1), calls=%async_computation.3 | async-start | bytes 6553600 | tf_op jit(solution)/shard_map/all_to_all | solution.py:138
  325.9 1.6 copy-start.4
  346.3 52.5 %all-to-all-start.4 = ((bf16[8,256,800]{1,2,0:T(8,128)(2,1)}), bf16[8,256,800]{1,2,0:T(8,128)(2,1)}, u32[]{:S(2)}, u32[]{:S(2)}) async-start(bf16[8,256,800]{1,2,0:T(8,128)(2,1)} %broadcast_select_fusion), calls=%async_computation.4 | async-start | bytes 6553600 | tf_op jit(solution)/shard_map/all_to_all | solution.py:138
Sparse Core Ops, SparseCore 0:
  9.8 117.1 all-gather.6
  170.7 61.8 all-gather.10
  235.1 85.4 all-gather.8

commit v8 on v7

--- a/solution.py
+++ b/solution.py
@@ -112,31 +112,39 @@
         )
         if not slot_received:
             late_weight, tile_out = lax.optimization_barrier((out_weight, tile_out))
-        all_heads = lax.all_gather(tile_out, "dp", axis=0, tiled=False)
-        if not slot_received:
-            head_rows = lax.all_gather(late_weight, "fsdp", axis=1, tiled=True)
-            weight_block = lax.all_to_all(
-                head_rows, "dp", split_axis=1, concat_axis=0, tiled=True
+        pieces = 2
+        piece_rows = tile_out.shape[0] // pieces
+        piece_received = []
+        for piece in range(pieces):
+            piece_out = tile_out[piece * piece_rows : (piece + 1) * piece_rows]
+            all_heads = lax.all_gather(piece_out, "dp", axis=0, tiled=False)
+            if not slot_received and not piece_received:
+                head_rows = lax.all_gather(late_weight, "fsdp", axis=1, tiled=True)
+                weight_block = lax.all_to_all(
+                    head_rows, "dp", split_axis=1, concat_axis=0, tiled=True
+                )
+            last = piece_received if piece_received else slot_received
+            if last:
+                all_heads, last[-1] = lax.optimization_barrier((all_heads, last[-1]))
+            head_terms = jnp.einsum(
+                "hsc,hcd->hsd",
+                all_heads,
+                weight_block.reshape(groups, HEAD_DIM, block),
+                preferred_element_type=jnp.float32,
+            ).astype(jnp.bfloat16)
+            attention = jnp.sum(lax.optimization_barrier(head_terms).astype(jnp.float32), axis=0)
+            start = first + 1 + piece * piece_rows
+            patches = own_block[start : start + piece_rows]
+            updated = (patches.astype(jnp.float32) + scale_block * attention).astype(jnp.bfloat16)
+            square = updated.reshape(halves // pieces, 2, halves, 2, block).transpose(0, 2, 4, 1, 3)
+            merged = square.reshape(halves * halves // pieces, block * 4)
+            outgoing = jnp.where(
+                sending[:, tile_slot, None, None], merged[None], jnp.zeros((), jnp.bfloat16)
             )
-        if slot_received:
-            all_heads, slot_received[-1] = lax.optimization_barrier((all_heads, slot_received[-1]))
-        head_terms = jnp.einsum(
-            "hsc,hcd->hsd",
-            all_heads,
-            weight_block.reshape(groups, HEAD_DIM, block),
-            preferred_element_type=jnp.float32,
-        ).astype(jnp.bfloat16)
-        attention = jnp.sum(lax.optimization_barrier(head_terms).astype(jnp.float32), axis=0)
-        patches = own_block[first + 1 : first + TILE]
-        updated = (patches.astype(jnp.float32) + scale_block * attention).astype(jnp.bfloat16)
-        square = updated.reshape(halves, 2, halves, 2, block).transpose(0, 2, 4, 1, 3)
-        merged = square.reshape(halves * halves, block * 4)
-        outgoing = jnp.where(
-            sending[:, tile_slot, None, None], merged[None], jnp.zeros((), jnp.bfloat16)
-        )
-        slot_received.append(
-            lax.all_to_all(outgoing, "fsdp", split_axis=0, concat_axis=0, tiled=True)
-        )
+            piece_received.append(
+                lax.all_to_all(outgoing, "fsdp", split_axis=0, concat_axis=0, tiled=True)
+            )
+        slot_received.append(jnp.concatenate(piece_received, axis=1))
     received = jnp.stack(slot_received, axis=1)
     return place_tiles(received, holder, living, row_index)
 

time: 413 us -> 442 us (1.070)
  waiting for transfers between devices: 228 us -> 263 us
  local copies, waits for them, and re-layouts: 36.5 us -> 26.6 us
    all_gather x2 -> x4, waiting for transfers between devices: 59.9 us -> 95.6 us  [body(): all_heads = lax.all_gather(piece_out, 'dp', axis=0, tiled=False)]
    all_to_all x1, waiting for transfers between devices: 11.8 us -> 7.17 us  [body(): lax.all_to_all(head_rows, 'dp', split_axis=1, concat_axis=0, tiled=True)]
    all_to_all x2 -> x4, starting transfers between devices: 13.2 us -> 16.5 us  [body(): lax.all_to_all(outgoing, 'fsdp', split_axis=0, concat_axis=0, tiled=True)]
    all_to_all x2 -> x4, waiting for transfers between devices: 36.7 us -> 39.9 us  [body(): lax.all_to_all(outgoing, 'fsdp', split_axis=0, concat_axis=0, tiled=True)]
    transpose x2 -> x4, local copies, waits for them, and re-layouts: 10.4 us -> 7.36 us  [body(): updated.reshape(halves // pieces, 2, halves, 2, block)]
    broadcast_in_dim x3 -> x5, local copies, waits for them, and re-layouts: 9.08 us -> 6.79 us  [body(): jnp.where(sending[:, tile_slot, None, None], merged[None], jnp.zeros((),...]
    dot_general x2 -> x4, matrix products: 10.3 us -> 12.3 us  [body(): jnp.einsum('hsc,hcd->hsd', all_heads, weight_block.reshape(groups, HEAD_D...]
  transfers between devices with their start and end apart: 8 -> 12, of which waited for: 6 -> 8; matrix products, arithmetic and copies ran while one was open for 11% -> 12% of each run, Pallas kernels for 0% -> 0%
where the time goes in v8:
time: 442 us; the launch traced here: 441 us
  waiting for transfers between devices  263 us (60%)
  other arithmetic  34.5 us (8%)
  starting transfers between devices  33.8 us (8%)
  blocking collectives  32.5 us (7%)
  matrix products  29.9 us (7%)
  local copies, waits for them, and re-layouts  26.6 us (6%)
  between operations  20.7 us (5%)
    all_gather x1, waiting for transfers between devices, body(): gathered = lax.all_gather(own_rows, 'dp', axis=0, tiled=True)  111 us
    all_gather x4, waiting for transfers between devices, body(): all_heads = lax.all_gather(piece_out, 'dp', axis=0, tiled=False)  95.6 us
    all_to_all x4, waiting for transfers between devices, body(): lax.all_to_all(outgoing, 'fsdp', split_axis=0, concat_axis=0, tiled=True)  39.9 us
    all_gather x1, blocking collectives, body(): head_rows = lax.all_gather(late_weight, 'fsdp', axis=1, tiled=True)  32.5 us
    all_to_all x4, starting transfers between devices, body(): lax.all_to_all(outgoing, 'fsdp', split_axis=0, concat_axis=0, tiled=True)  16.5 us
    dot_general x4, matrix products, body(): jnp.einsum('hsc,hcd->hsd', all_heads, weight_block.reshape(groups, HEAD_D...  12.3 us
    dot_general x1, matrix products, body(): projected = jnp.dot(normed, full_qkv, preferred_element_type=jnp.float32)  12.1 us
  transfers between devices with their start and end apart: 12, of which 8 were waited for; matrix products, arithmetic and copies ran while one was open for 12% of the time, Pallas kernels for 0%

profile of v8, /device:TPU:8, one launch (start us, length us, event | category | flops | bytes accessed | tf_op | source)
XLA Modules:
  0.0 440.7 jit_solution(15658303118645032298)
XLA Ops:
  7.3 2.6 broadcast_in_dim.123
  9.9 5.7 %all-to-all-start = ((bf16[8,400,384]{2,1,0:T(8,128)(2,1)}), bf16[8,400,384]{2,1,0:T(8,128)(2,1)S(1)}, u32[]{:S(2)}, u32[]{:S(2)}) async-start(bf16[8,400,384]{2,1,0:T(8,128)(2,1)} %broadcast_in_dim.123), calls=%async_computation | async-start | bytes 4915200 | tf_op jit(solution)/shard_map/all_to_all | solution.py:57
  15.5 111.4 %all-gather.11.cloned.1.call-done = bf16[1,2176,3200]{2,1,0:T(8,128)(2,1)} async-done(((bf16[1,136,3200]{2,1,0:T(8,128)(2,1)}), bf16[1,2176,3200]{2,1,0:T(8,128)(2,1)}) %all-gather.11.cloned.1.call-update) | async-done | bytes 13926416 | tf_op jit(solution)/shard_map/all_gather | solution.py:70
  127.0 7.7 %fusion = f32[2176]{0:T(1024)S(1)} fusion(bf16[1,2176,3200]{2,1,0:T(8,128)(2,1)} %all-gather.11.cloned.1.call-done), kind=kLoop, calls=%fused_computation.2 | loop fusion | flops 20887424 | bytes 13935104 | tf_op jit(solution)/shard_map/reduce_sum | solution.py:73
  134.7 12.1 %fusion.44 = (bf16[2176,384]{1,0:T(8,128)(2,1)}, f32[2176,384]{1,0:T(8,128)S(1)}) fusion(bf16[3200,384]{1,0:T(8,128)(2,1)S(1)} %bitcast.89, bf16[1,2176,3200]{2,1,0:T(8,128)(2,1)} %all-gather.11.cloned.1.call-done, f32[3200]{0:T(1024)S(1)} %copy-done.6, f32[2176]{0:T(1024)S(1)} %add_rsqrt_fusion), kind=kOutput, calls=%fused_computation.110 | convolution fusion | flops 5376425984 | bytes 21419008 | tf_op jit(solution)/shard_map/dot_general | solution.py:75
  150.0 5.2 %all-to-all-start.1 = ((f32[16,2,2176]{2,1,0:T(2,128)}), f32[16,2,2176]{2,1,0:T(2,128)S(1)}, u32[]{:S(2)}, u32[]{:S(2)}) async-start(f32[16,2,2176]{2,1,0:T(2,128)} %broadcast_in_dim.124), calls=%async_computation.1 | async-start | bytes 557056 | tf_op jit(solution)/shard_map/all_to_all | solution.py:51
  155.3 7.0 %all-to-all-done.1 = f32[16,2,2176]{2,1,0:T(2,128)S(1)} async-done(((f32[16,2,2176]{2,1,0:T(2,128)}), f32[16,2,2176]{2,1,0:T(2,128)S(1)}, u32[]{:S(2)}, u32[]{:S(2)}) %all-to-all-start.1) | async-done | bytes 278560 | tf_op jit(solution)/shard_map/all_to_all | solution.py:51
  162.5 2.4 multiply_convert_fusion.1
  170.8 2.0 constant_dynamic-slice_fusion.3
  172.9 32.5 %all_gather.37 = bf16[128,3200]{0,1:T(8,128)(2,1)} all-gather(bf16[128,400]{0,1:T(8,128)(2,1)S(1)} %copy-done.2), channel_id=1, replica_groups=mesh['fsdp'=8,'dp'=16] {'fsdp'}, dimensions={1}, use_global_device_ids=true | all-gather | bytes 921600 | tf_op jit(solution)/shard_map/all_gather | solution.py:122
  205.4 5.9 %all-to-all-start.2 = ((bf16[128,16,200]{0,2,1:T(8,128)(2,1)}), bf16[128,16,200]{0,2,1:T(8,128)(2,1)S(1)}, u32[]{:S(2)}, u32[]{:S(2)}) async-start(bf16[128,16,200]{0,2,1:T(8,128)(2,1)} %bitcast.16), calls=%async_computation.2 | async-start | bytes 1638400 | tf_op jit(solution)/shard_map/all_to_all | solution.py:123
  212.7 2.0 fusion.13
  215.5 7.2 %all-to-all-done.2 = bf16[128,16,200]{0,2,1:T(8,128)(2,1)S(1)} async-done(((bf16[128,16,200]{0,2,1:T(8,128)(2,1)}), bf16[128,16,200]{0,2,1:T(8,128)(2,1)S(1)}, u32[]{:S(2)}, u32[]{:S(2)}) %all-to-all-start.2) | async-done | bytes 819232 | tf_op jit(solution)/shard_map/all_to_all | solution.py:123
  222.6 3.1 convolution_convert_fusion.3
  230.5 4.3 all-to-all-start.3
  234.9 37.3 %all-gather.15.cloned.1.call-done = bf16[8192,128]{1,0:T(8,128)(2,1)} async-done(((bf16[512,128]{1,0:T(8,128)(2,1)}), bf16[8192,128]{1,0:T(8,128)(2,1)}) %all-gather.15.cloned.1.call-update) | async-done | bytes 2097168 | tf_op jit(solution)/shard_map/all_gather | solution.py:120
  272.2 3.1 convolution_convert_fusion.2
  277.8 2.2 copy.56
  280.0 2.4 broadcast_in_dim.130
  283.7 4.3 all-to-all-start.4
  288.8 25.1 %all-to-all-done.4 = bf16[8,128,800]{1,2,0:T(8,128)(2,1)} async-done(((bf16[8,128,800]{1,2,0:T(8,128)(2,1)}), bf16[8,128,800]{1,2,0:T(8,128)(2,1)}, u32[]{:S(2)}, u32[]{:S(2)}) %all-to-all-start.4) | async-done | bytes 1638432 | tf_op jit(solution)/shard_map/all_to_all | solution.py:145
  313.9 3.5 pad_maximum_fusion.1
  317.4 7.5 %all-gather.13.cloned.1.call-done = bf16[8192,128]{1,0:T(8,128)(2,1)} async-done(((bf16[512,128]{1,0:T(8,128)(2,1)}), bf16[8192,128]{1,0:T(8,128)(2,1)}) %all-gather.13.cloned.1.call-update) | async-done | bytes 2097168 | tf_op jit(solution)/shard_map/all_gather | solution.py:120
  324.9 3.1 convolution_convert_fusion.1
  332.7 3.6 all-to-all-start.5
  336.5 50.8 %all-gather.19.cloned.1.call-done = bf16[8192,128]{1,0:T(8,128)(2,1)} async-done(((bf16[512,128]{1,0:T(8,128)(2,1)}), bf16[8192,128]{1,0:T(8,128)(2,1)}) %all-gather.19.cloned.1.call-update) | async-done | bytes 2097168 | tf_op jit(solution)/shard_map/all_gather | solution.py:120
  387.2 3.1 convolution_convert_fusion
  391.2 2.2 copy.60
  393.5 2.4 broadcast_in_dim.136
  397.2 4.3 all-to-all-start.6
  412.3 14.8 %all-to-all-done.6 = bf16[8,128,800]{1,2,0:T(8,128)(2,1)} async-done(((bf16[8,128,800]{1,2,0:T(8,128)(2,1)}), bf16[8,128,800]{1,2,0:T(8,128)(2,1)}, u32[]{:S(2)}, u32[]{:S(2)}) %all-to-all-start.6) | async-done | bytes 1638432 | tf_op jit(solution)/shard_map/all_to_all | solution.py:145
  430.1 2.6 dynamic-slice_select_fusion.3
  (92 shorter events, 36.7 us)
Async XLA Ops:
  6.5 120.4 %all-gather.11.cloned.1.call-start = ((), (), s32[]{:S(2)}) async-start(), calls=%async_computation.7 | async-start | bytes 14796800 | tf_op jit(solution)/shard_map/all_gather | solution.py:70
  9.9 124.8 %all-to-all-start = ((bf16[8,400,384]{2,1,0:T(8,128)(2,1)}), bf16[8,400,384]{2,1,0:T(8,128)(2,1)S(1)}, u32[]{:S(2)}, u32[]{:S(2)}) async-start(bf16[8,400,384]{2,1,0:T(8,128)(2,1)} %broadcast_in_dim.123), calls=%async_computation | async-start | bytes 4915200 | tf_op jit(solution)/shard_map/all_to_all | solution.py:57
  15.5 119.2 %copy-start.6 = (f32[3200]{0:T(1024)S(1)}, f32[3200]{0:T(1024)}, u32[]{:S(2)}) copy-start(f32[3200]{0:T(1024)} %param.9) | copy-start | bytes 38404
  134.7 20.6 %copy-start.3 = (f32[2,128]{1,0:T(2,128)S(1)}, f32[2,128]{1,0:T(2,128)}, u32[]{:S(2)}) copy-start(f32[2,128]{1,0:T(2,128)} %param.11) | copy-start | bytes 3076
  146.8 1.7 copy-start.1
  150.0 12.3 %all-to-all-start.1 = ((f32[16,2,2176]{2,1,0:T(2,128)}), f32[16,2,2176]{2,1,0:T(2,128)S(1)}, u32[]{:S(2)}, u32[]{:S(2)}) async-start(f32[16,2,2176]{2,1,0:T(2,128)} %broadcast_in_dim.124), calls=%async_computation.1 | async-start | bytes 557056 | tf_op jit(solution)/shard_map/all_to_all | solution.py:51
  155.3 67.4 %all-gather.17.cloned.1.call-start = ((), (), s32[]{:S(2)}) async-start(), calls=%async_computation.10 | async-start | bytes 2228224 | tf_op jit(solution)/shard_map/all_gather | solution.py:120
  166.3 4.2 copy-start.4
  166.3 4.2 copy-start.5
  168.2 4.7 %copy-start.2 = (bf16[128,400]{0,1:T(8,128)(2,1)S(1)}, bf16[128,400]{0,1:T(8,128)(2,1)}, u32[]{:S(2)}) copy-start(bf16[128,400]{0,1:T(8,128)(2,1)} %param.12) | copy-start | bytes 307204
  169.0 103.2 %all-gather.15.cloned.1.call-start = ((), (), s32[]{:S(2)}) async-start(), calls=%async_computation.9 | async-start | bytes 2228224 | tf_op jit(solution)/shard_map/all_gather | solution.py:120
  205.4 17.3 %all-to-all-start.2 = ((bf16[128,16,200]{0,2,1:T(8,128)(2,1)}), bf16[128,16,200]{0,2,1:T(8,128)(2,1)S(1)}, u32[]{:S(2)}, u32[]{:S(2)}) async-start(bf16[128,16,200]{0,2,1:T(8,128)(2,1)} %bitcast.16), calls=%async_computation.2 | async-start | bytes 1638400 | tf_op jit(solution)/shard_map/all_to_all | solution.py:123
  211.2 113.7 %all-gather.13.cloned.1.call-start = ((), (), s32[]{:S(2)}) async-start(), calls=%async_computation.8 | async-start | bytes 2228224 | tf_op jit(solution)/shard_map/all_gather | solution.py:120
  230.5 41.7 %all-to-all-start.3 = ((bf16[8,128,800]{1,2,0:T(8,128)(2,1)}), bf16[8,128,800]{1,2,0:T(8,128)(2,1)S(1)}, u32[]{:S(2)}, u32[]{:S(2)}) async-start(bf16[8,128,800]{1,2,0:T(8,128)(2,1)} %broadcast_select_fusion.3), calls=%async_computation.3 | async-start | bytes 3276800 | tf_op jit(solution)/shard_map/all_to_all | solution.py:145
  283.7 30.2 %all-to-all-start.4 = ((bf16[8,128,800]{1,2,0:T(8,128)(2,1)}), bf16[8,128,800]{1,2,0:T(8,128)(2,1)}, u32[]{:S(2)}, u32[]{:S(2)}) async-start(bf16[8,128,800]{1,2,0:T(8,128)(2,1)} %broadcast_select_fusion.2), calls=%async_computation.4 | async-start | bytes 3276800 | tf_op jit(solution)/shard_map/all_to_all | solution.py:145
  288.1 99.2 %all-gather.19.cloned.1.call-start = ((), (), s32[]{:S(2)}) async-start(), calls=%async_computation.11 | async-start | bytes 2228224 | tf_op jit(solution)/shard_map/all_gather | solution.py:120
  332.7 54.5 %all-to-all-start.5 = ((bf16[8,128,800]{1,2,0:T(8,128)(2,1)}), bf16[8,128,800]{1,2,0:T(8,128)(2,1)S(1)}, u32[]{:S(2)}, u32[]{:S(2)}) async-start(bf16[8,128,800]{1,2,0:T(8,128)(2,1)} %broadcast_select_fusion.1), calls=%async_computation.5 | async-start | bytes 3276800 | tf_op jit(solution)/shard_map/all_to_all | solution.py:145
  397.2 29.9 %all-to-all-start.6 = ((bf16[8,128,800]{1,2,0:T(8,128)(2,1)}), bf16[8,128,800]{1,2,0:T(8,128)(2,1)}, u32[]{:S(2)}, u32[]{:S(2)}) async-start(bf16[8,128,800]{1,2,0:T(8,128)(2,1)} %broadcast_select_fusion), calls=%async_computation.6 | async-start | bytes 3276800 | tf_op jit(solution)/shard_map/all_to_all | solution.py:145
  427.1 2.4 copy-start
Sparse Core Ops, SparseCore 0:
  9.8 117.1 all-gather.10
  169.1 49.3 all-gather.16
  221.0 51.1 all-gather.14
  274.5 50.3 all-gather.12
  327.2 59.9 all-gather.18

commit v9 on v3

--- a/solution.py
+++ b/solution.py
@@ -66,10 +66,7 @@
     row_count = lax.axis_size("fsdp")
     model_width = own_rows.shape[1]
     block = model_width // groups
-    head_rows = lax.all_gather(out_weight, "fsdp", axis=1, tiled=True)
-    weight_block = lax.all_to_all(head_rows, "dp", split_axis=1, concat_axis=0, tiled=True)
     full_qkv = gather_blocks(qkv_weight, "fsdp", row_count)
-    full_qkv, weight_block = lax.optimization_barrier((full_qkv, weight_block))
     gathered = lax.all_gather(own_rows, "dp", axis=0, tiled=True)
     values = gathered.astype(jnp.float32)
     normed = (
@@ -99,8 +96,7 @@
     own_living = living[row_index]
     destination = jnp.arange(row_count, dtype=jnp.int32)[:, None]
     sending = jnp.logical_and(destination == own_holder[None, :], own_living[None, :])
-    halves = GRID // 2
-    slot_received = []
+    outs = []
     for tile_slot in range(SLOTS):
         first = tile_slot * TILE
         tile_query = queries[first : first + TILE]
@@ -110,28 +106,30 @@
         highest = jnp.max(scores, axis=-1, keepdims=True)
         exponent = jnp.exp(scores - highest)
         weights = (exponent / jnp.sum(exponent, axis=-1, keepdims=True)).astype(jnp.bfloat16)
-        tile_out = jnp.dot(weights, tile_value, preferred_element_type=jnp.float32).astype(
-            jnp.bfloat16
+        outs.append(
+            jnp.dot(weights, tile_value, preferred_element_type=jnp.float32).astype(jnp.bfloat16)
         )
-        all_heads = lax.all_gather(tile_out, "dp", axis=0, tiled=False)
-        head_terms = jnp.einsum(
-            "hsc,hcd->hsd",
-            all_heads,
-            weight_block.reshape(groups, HEAD_DIM, block),
-            preferred_element_type=jnp.float32,
-        ).astype(jnp.bfloat16)
-        attention = jnp.sum(lax.optimization_barrier(head_terms).astype(jnp.float32), axis=0)
-        patches = own_block[first + 1 : first + TILE]
-        updated = (patches.astype(jnp.float32) + scale_block * attention).astype(jnp.bfloat16)
-        square = updated.reshape(halves, 2, halves, 2, block).transpose(0, 2, 4, 1, 3)
-        merged = square.reshape(halves * halves, block * 4)
-        outgoing = jnp.where(
-            sending[:, tile_slot, None, None], merged[None], jnp.zeros((), jnp.bfloat16)
-        )
-        slot_received.append(
-            lax.all_to_all(outgoing, "fsdp", split_axis=0, concat_axis=0, tiled=True)
-        )
-    received = jnp.stack(slot_received, axis=1)
+    tile_out = jnp.stack(outs)
+    late_weight, tile_out = lax.optimization_barrier((out_weight, tile_out))
+    all_heads = lax.all_gather(tile_out, "dp", axis=0, tiled=False)
+    head_rows = lax.all_gather(late_weight, "fsdp", axis=1, tiled=True)
+    weight_block = lax.all_to_all(head_rows, "dp", split_axis=1, concat_axis=0, tiled=True)
+    head_terms = jnp.einsum(
+        "htsc,hcd->htsd",
+        all_heads,
+        weight_block.reshape(groups, HEAD_DIM, block),
+        preferred_element_type=jnp.float32,
+    ).astype(jnp.bfloat16)
+    attention = jnp.sum(lax.optimization_barrier(head_terms).astype(jnp.float32), axis=0)
+    patches = jnp.stack(
+        [own_block[slot * TILE + 1 : (slot + 1) * TILE] for slot in range(SLOTS)]
+    )
+    updated = (patches.astype(jnp.float32) + scale_block * attention).astype(jnp.bfloat16)
+    halves = GRID // 2
+    square = updated.reshape(SLOTS, halves, 2, halves, 2, block).transpose(0, 1, 3, 5, 2, 4)
+    merged = square.reshape(SLOTS, halves * halves, block * 4)
+    outgoing = jnp.where(sending[:, :, None, None], merged[None], jnp.zeros((), jnp.bfloat16))
+    received = lax.all_to_all(outgoing, "fsdp", split_axis=0, concat_axis=0, tiled=True)
     return place_tiles(received, holder, living, row_index)
 
 

time: 442 us -> 413 us (0.934)
  blocking collectives: 52.5 us -> 32.7 us
  waiting for transfers between devices: 247 us -> 240 us
  local copies, waits for them, and re-layouts: 34.4 us -> 28.1 us
    all_gather x1, waiting for transfers between devices: 40 us -> 111 us  [body(): gathered = lax.all_gather(own_rows, 'dp', axis=0, tiled=True)]
    all_gather x2 -> x1, waiting for transfers between devices: 96.2 us -> 29 us  [body(): all_heads = lax.all_gather(tile_out, 'dp', axis=0, tiled=False)]
    all_to_all x1, waiting for transfers between devices: 37.4 us -> 0.01 us  [gather_blocks(): lax.all_to_all(spread, axis_name, split_axis=0, concat_axis=0, tiled=True)]
    all_to_all x1 -> x0, blocking collectives: 20.6 us -> none  [body(): lax.all_to_all(head_rows, 'dp', split_axis=1, concat_axis=0, tiled=True)]
    all_to_all x2 -> x1, waiting for transfers between devices: 65.5 us -> 80.3 us  [body(): lax.all_to_all(outgoing, 'fsdp', split_axis=0, concat_axis=0, tiled=True)]
    all_to_all x0 -> x1, waiting for transfers between devices: none -> 11.2 us  [body(): lax.all_to_all(head_rows, 'dp', split_axis=1, concat_axis=0, tiled=True)]
    all_to_all x0 -> x1, starting transfers between devices: none -> 6.64 us  [body(): lax.all_to_all(head_rows, 'dp', split_axis=1, concat_axis=0, tiled=True)]
    reduce_sum x1, other arithmetic: 4.09 us -> 9.31 us  [body(): jnp.sum(lax.optimization_barrier(head_terms).astype(jnp.float32), axis=0)]
  transfers between devices with their start and end apart: 7 -> 6, of which waited for: 7 -> 5; matrix products, arithmetic and copies ran while one was open for 9% -> 5% of each run, Pallas kernels for 0% -> 0%
where the time goes in v9:
time: 413 us; the launch traced here: 410 us
  waiting for transfers between devices  240 us (58%)
  other arithmetic  36.3 us (9%)
  blocking collectives  32.7 us (8%)
  matrix products  28.9 us (7%)
  local copies, waits for them, and re-layouts  28.1 us (7%)
  starting transfers between devices  23.1 us (6%)
  between operations  21.4 us (5%)
    all_gather x1, waiting for transfers between devices, body(): gathered = lax.all_gather(own_rows, 'dp', axis=0, tiled=True)  111 us
    all_to_all x1, waiting for transfers between devices, body(): lax.all_to_all(outgoing, 'fsdp', split_axis=0, concat_axis=0, tiled=True)  80.3 us
    all_gather x1, blocking collectives, body(): head_rows = lax.all_gather(late_weight, 'fsdp', axis=1, tiled=True)  32.7 us
    all_gather x1, waiting for transfers between devices, body(): all_heads = lax.all_gather(tile_out, 'dp', axis=0, tiled=False)  29 us
    dot_general x1, matrix products, body(): projected = jnp.dot(normed, full_qkv, preferred_element_type=jnp.float32)  12.8 us
    all_to_all x1, waiting for transfers between devices, body(): lax.all_to_all(head_rows, 'dp', split_axis=1, concat_axis=0, tiled=True)  11.2 us
    dot_general x1, matrix products, body(): jnp.einsum('htsc,hcd->htsd', all_heads, weight_block.reshape(groups, HEAD...  10.6 us
    reduce_sum x1, other arithmetic, body(): jnp.sum(lax.optimization_barrier(head_terms).astype(jnp.float32), axis=0)  9.31 us
  transfers between devices with their start and end apart: 6, of which 5 were waited for; matrix products, arithmetic and copies ran while one was open for 5% of the time, Pallas kernels for 0%

profile of v9, /device:TPU:8, one launch (start us, length us, event | category | flops | bytes accessed | tf_op | source)
XLA Modules:
  0.0 409.9 jit_solution(9472612087322636246)
XLA Ops:
  7.3 2.6 broadcast_in_dim.83
  9.9 5.7 %all-to-all-start = ((bf16[8,400,384]{2,1,0:T(8,128)(2,1)}), bf16[8,400,384]{2,1,0:T(8,128)(2,1)S(1)}, u32[]{:S(2)}, u32[]{:S(2)}) async-start(bf16[8,400,384]{2,1,0:T(8,128)(2,1)} %broadcast_in_dim.83), calls=%async_computation | async-start | bytes 4915200 | tf_op jit(solution)/shard_map/all_to_all | solution.py:57
  15.5 111.4 %all-gather.5.cloned.1.call-done = bf16[1,2176,3200]{2,1,0:T(8,128)(2,1)} async-done(((bf16[1,136,3200]{2,1,0:T(8,128)(2,1)}), bf16[1,2176,3200]{2,1,0:T(8,128)(2,1)}) %all-gather.5.cloned.1.call-update) | async-done | bytes 13926416 | tf_op jit(solution)/shard_map/all_gather | solution.py:70
  127.0 7.7 %fusion = f32[2176]{0:T(1024)S(1)} fusion(bf16[1,2176,3200]{2,1,0:T(8,128)(2,1)} %all-gather.5.cloned.1.call-done), kind=kLoop, calls=%fused_computation.2 | loop fusion | flops 20887424 | bytes 13935104 | tf_op jit(solution)/shard_map/reduce_sum | solution.py:73
  134.7 1.4 copy-done
  136.1 12.8 %fusion.41 = (bf16[2176,384]{1,0:T(8,128)(2,1)}, f32[2176,384]{1,0:T(8,128)S(1)}) fusion(bf16[3200,384]{1,0:T(8,128)(2,1)} %bitcast.51, bf16[1,2176,3200]{2,1,0:T(8,128)(2,1)} %all-gather.5.cloned.1.call-done, f32[3200]{0:T(1024)S(1)} %copy-done.5, f32[2176]{0:T(1024)S(1)} %add_rsqrt_fusion), kind=kOutput, calls=%fused_computation.89 | convolution fusion | flops 5376425984 | bytes 21419008 | tf_op jit(solution)/shard_map/dot_general | solution.py:75
  149.7 0.8 broadcast_in_dim.84
  150.4 5.8 %all-to-all-start.1 = ((f32[16,2,2176]{2,1,0:T(2,128)}), f32[16,2,2176]{2,1,0:T(2,128)}, u32[]{:S(2)}, u32[]{:S(2)}) async-start(f32[16,2,2176]{2,1,0:T(2,128)} %broadcast_in_dim.84), calls=%async_computation.1 | async-start | bytes 557056 | tf_op jit(solution)/shard_map/all_to_all | solution.py:51
  156.5 6.9 %all-to-all-done.1 = f32[16,2,2176]{2,1,0:T(2,128)} async-done(((f32[16,2,2176]{2,1,0:T(2,128)}), f32[16,2,2176]{2,1,0:T(2,128)}, u32[]{:S(2)}, u32[]{:S(2)}) %all-to-all-start.1) | async-done | bytes 278560 | tf_op jit(solution)/shard_map/all_to_all | solution.py:51
  163.4 1.0 reduce_sum.68
  164.6 1.2 multiply_convert_fusion.1
  168.0 2.0 fusion.17
  170.6 1.9 fusion.16
  172.5 0.8 pad_maximum_fusion.1
  174.3 32.7 %all_gather.15 = bf16[128,3200]{0,1:T(8,128)(2,1)} all-gather(bf16[128,400]{0,1:T(8,128)(2,1)S(1)} %copy-done.1), channel_id=1, replica_groups=mesh['fsdp'=8,'dp'=16] {'fsdp'}, dimensions={1}, use_global_device_ids=true | all-gather | bytes 921600 | tf_op jit(solution)/shard_map/all_gather | solution.py:115
  207.0 6.6 %all-to-all-start.2 = ((bf16[128,16,200]{0,2,1:T(8,128)(2,1)}), bf16[128,16,200]{0,2,1:T(8,128)(2,1)S(1)}, u32[]{:S(2)}, u32[]{:S(2)}) async-start(bf16[128,16,200]{0,2,1:T(8,128)(2,1)} %bitcast.14), calls=%async_computation.2 | async-start | bytes 1638400 | tf_op jit(solution)/shard_map/all_to_all | solution.py:116
  213.7 2.0 constant_dynamic-slice_fusion
  216.0 0.9 copy.27
  217.2 0.9 copy.28
  218.1 11.2 %all-to-all-done.2 = bf16[128,16,200]{0,2,1:T(8,128)(2,1)S(1)} async-done(((bf16[128,16,200]{0,2,1:T(8,128)(2,1)}), bf16[128,16,200]{0,2,1:T(8,128)(2,1)S(1)}, u32[]{:S(2)}, u32[]{:S(2)}) %all-to-all-start.2) | async-done | bytes 819232 | tf_op jit(solution)/shard_map/all_to_all | solution.py:116
  229.3 29.0 %all-gather.7.cloned.1.call-done = bf16[32,1024,128]{2,1,0:T(8,128)(2,1)} async-done(((bf16[2,1024,128]{2,1,0:T(8,128)(2,1)}), bf16[32,1024,128]{2,1,0:T(8,128)(2,1)}) %all-gather.7.cloned.1.call-update) | async-done | bytes 8388624 | tf_op jit(solution)/shard_map/all_gather | solution.py:114
  258.3 10.6 %convolution_convert_fusion = bf16[16,2,1024,200]{2,3,1,0:T(8,128)(2,1)} fusion(bf16[16,2,1024,128]{3,2,1,0:T(8,128)(2,1)} %bitcast.49, bf16[128,16,200]{0,2,1:T(8,128)(2,1)S(1)} %all-to-all-done.2), kind=kOutput, calls=%fused_computation.10 | convolution fusion | flops 1684275200 | bytes 22315008 | tf_op jit(solution)/shard_map/htsc,hcd->htsd/dot_general | solution.py:117
  268.9 9.3 %convert_reduce_fusion = f32[2,1024,200]{1,2,0:T(8,128)} fusion(bf16[16,2,1024,200]{2,3,1,0:T(8,128)(2,1)} %convolution_convert_fusion), kind=kLoop, calls=%fused_computation.5 | loop fusion | flops 12697600 | bytes 14745600 | tf_op jit(solution)/shard_map/reduce_sum | solution.py:123
  278.2 2.8 copy.30
  280.9 1.7 fusion.18
  282.6 7.1 %copy.32 = bf16[2,16,16,200,2,2]{2,1,5,4,3,0:T(8,128)(2,1)} copy(bf16[2,16,16,200,2,2]{3,2,5,4,1,0:T(8,128)(2,1)S(1)} %fusion.18) | data formatting | bytes 1638400 | tf_op jit(solution)/shard_map/transpose | solution.py:129
  289.7 8.1 %broadcast_in_dim.85 = bf16[2,256,800]{1,2,0:T(8,128)(2,1)S(1)} reshape(bf16[2,16,16,200,2,2]{2,1,5,4,3,0:T(8,128)(2,1)} %copy.32) | data formatting | bytes 1638400 | tf_op jit(solution)/shard_map/jit(_where)/broadcast_in_dim | solution.py:131
  297.8 3.3 broadcast_select_fusion
  301.2 4.8 %all-to-all-start.3 = ((bf16[8,2,256,800]{2,3,1,0:T(8,128)(2,1)}), bf16[8,2,256,800]{2,3,1,0:T(8,128)(2,1)}, u32[]{:S(2)}, u32[]{:S(2)}) async-start(bf16[8,2,256,800]{2,3,1,0:T(8,128)(2,1)} %broadcast_select_fusion), calls=%async_computation.3 | async-start | bytes 13107200 | tf_op jit(solution)/shard_map/all_to_all | solution.py:132
  317.5 80.3 %all-to-all-done.3 = bf16[8,2,256,800]{2,3,1,0:T(8,128)(2,1)} async-done(((bf16[8,2,256,800]{2,3,1,0:T(8,128)(2,1)}), bf16[8,2,256,800]{2,3,1,0:T(8,128)(2,1)}, u32[]{:S(2)}, u32[]{:S(2)}) %all-to-all-start.3) | async-done | bytes 6553632 | tf_op jit(solution)/shard_map/all_to_all | solution.py:132
  397.7 4.0 dynamic-slice_select_fusion.3
  401.7 1.4 pad_maximum_fusion
  (45 shorter events, 9.8 us)
Async XLA Ops:
  6.5 120.4 %all-gather.5.cloned.1.call-start = ((), (), s32[]{:S(2)}) async-start(), calls=%async_computation.4 | async-start | bytes 14796800 | tf_op jit(solution)/shard_map/all_gather | solution.py:70
  9.9 124.8 %all-to-all-start = ((bf16[8,400,384]{2,1,0:T(8,128)(2,1)}), bf16[8,400,384]{2,1,0:T(8,128)(2,1)S(1)}, u32[]{:S(2)}, u32[]{:S(2)}) async-start(bf16[8,400,384]{2,1,0:T(8,128)(2,1)} %broadcast_in_dim.83), calls=%async_computation | async-start | bytes 4915200 | tf_op jit(solution)/shard_map/all_to_all | solution.py:57
  15.5 120.6 %copy-start.5 = (f32[3200]{0:T(1024)S(1)}, f32[3200]{0:T(1024)}, u32[]{:S(2)}) copy-start(f32[3200]{0:T(1024)} %param.9) | copy-start | bytes 38404
  134.7 1.4 copy-start
  136.1 20.4 %copy-start.2 = (f32[2,128]{1,0:T(2,128)S(1)}, f32[2,128]{1,0:T(2,128)}, u32[]{:S(2)}) copy-start(f32[2,128]{1,0:T(2,128)} %param.11) | copy-start | bytes 3076
  150.4 13.0 %all-to-all-start.1 = ((f32[16,2,2176]{2,1,0:T(2,128)}), f32[16,2,2176]{2,1,0:T(2,128)}, u32[]{:S(2)}, u32[]{:S(2)}) async-start(f32[16,2,2176]{2,1,0:T(2,128)} %broadcast_in_dim.84), calls=%async_computation.1 | async-start | bytes 557056 | tf_op jit(solution)/shard_map/all_to_all | solution.py:51
  156.3 102.0 %all-gather.7.cloned.1.call-start = ((), (), s32[]{:S(2)}) async-start(), calls=%async_computation.5 | async-start | bytes 8912896 | tf_op jit(solution)/shard_map/all_gather | solution.py:114
  170.6 3.6 copy-start.3
  170.6 3.6 copy-start.4
  170.6 3.7 copy-start.1
  207.0 22.3 %all-to-all-start.2 = ((bf16[128,16,200]{0,2,1:T(8,128)(2,1)}), bf16[128,16,200]{0,2,1:T(8,128)(2,1)S(1)}, u32[]{:S(2)}, u32[]{:S(2)}) async-start(bf16[128,16,200]{0,2,1:T(8,128)(2,1)} %bitcast.14), calls=%async_computation.2 | async-start | bytes 1638400 | tf_op jit(solution)/shard_map/all_to_all | solution.py:116
  301.2 96.6 %all-to-all-start.3 = ((bf16[8,2,256,800]{2,3,1,0:T(8,128)(2,1)}), bf16[8,2,256,800]{2,3,1,0:T(8,128)(2,1)}, u32[]{:S(2)}, u32[]{:S(2)}) async-start(bf16[8,2,256,800]{2,3,1,0:T(8,128)(2,1)} %broadcast_select_fusion), calls=%async_computation.3 | async-start | bytes 13107200 | tf_op jit(solution)/shard_map/all_to_all | solution.py:132
Sparse Core Ops, SparseCore 0:
  9.8 117.1 all-gather.4
  173.5 84.6 all-gather.6

commit v10 on v9

--- a/solution.py
+++ b/solution.py
@@ -32,11 +32,15 @@
     return (holder, living)
 
 
-def place_tiles(received, holder, living, target):
+def place_tiles(received, holder, living, target, shifted_from=None):
     owned_flag = jnp.logical_and(living, holder == target).reshape(-1).astype(jnp.int32)
     before = jnp.cumsum(owned_flag) - owned_flag
     flattened = received.reshape((received.shape[0] * received.shape[1],) + received.shape[2:])
     sources = jnp.arange(flattened.shape[0], dtype=jnp.int32)
+    if shifted_from is not None:
+        rows = received.shape[0]
+        slots = received.shape[1]
+        sources = ((shifted_from - sources // slots) % rows) * slots + sources % slots
     placed = []
     for slot in range(CAP):
         match = jnp.logical_and(before == slot, owned_flag == 1)
@@ -128,9 +132,16 @@
     halves = GRID // 2
     square = updated.reshape(SLOTS, halves, 2, halves, 2, block).transpose(0, 1, 3, 5, 2, 4)
     merged = square.reshape(SLOTS, halves * halves, block * 4)
-    outgoing = jnp.where(sending[:, :, None, None], merged[None], jnp.zeros((), jnp.bfloat16))
-    received = lax.all_to_all(outgoing, "fsdp", split_axis=0, concat_axis=0, tiled=True)
-    return place_tiles(received, holder, living, row_index)
+    zero = jnp.zeros((), jnp.bfloat16)
+    arrived = [None] * row_count
+    arrived[0] = jnp.where(sending[row_index][:, None, None], merged, zero)
+    for shift in range(1, row_count):
+        target = (row_index + shift) % row_count
+        outgoing = jnp.where(sending[target][:, None, None], merged, zero)
+        ring = [(source, (source + shift) % row_count) for source in range(row_count)]
+        arrived[shift] = lax.ppermute(outgoing, "fsdp", ring)
+    by_shift = jnp.stack(arrived)
+    return place_tiles(by_shift, holder, living, row_index, row_index)
 
 
 def solution(mesh):

time: 413 us -> 424 us (1.027)
  starting transfers between devices: 23.1 us -> 43.3 us
  waiting for transfers between devices: 240 us -> 226 us
  local copies, waits for them, and re-layouts: 28.1 us -> 36.6 us
    all_to_all x1 -> x0, waiting for transfers between devices: 80.3 us -> none  [body(): lax.all_to_all(outgoing, 'fsdp', split_axis=0, concat_axis=0, tiled=True)]
    ppermute x0 -> x7, waiting for transfers between devices: none -> 67 us  [body(): arrived[shift] = lax.ppermute(outgoing, 'fsdp', ring)]
    ppermute x0 -> x7, starting transfers between devices: none -> 24.9 us  [body(): arrived[shift] = lax.ppermute(outgoing, 'fsdp', ring)]
    reshape x0 -> x2, local copies, waits for them, and re-layouts: none -> 16.2 us  [body(): merged = square.reshape(SLOTS, halves * halves, block * 4)]
    broadcast_in_dim x1, local copies, waits for them, and re-layouts: 8.1 us -> 0.02 us  [body(): outgoing = jnp.where(sending[target][:, None, None], merged, zero)]
    all_to_all x1 -> x0, starting transfers between devices: 4.76 us -> none  [body(): lax.all_to_all(outgoing, 'fsdp', split_axis=0, concat_axis=0, tiled=True)]
  transfers between devices with their start and end apart: 6 -> 12, of which waited for: 5 -> 6; matrix products, arithmetic and copies ran while one was open for 5% -> 6% of each run, Pallas kernels for 0% -> 0%
where the time goes in v10:
time: 424 us; the launch traced here: 421 us
  waiting for transfers between devices  226 us (53%)
  starting transfers between devices  43.3 us (10%)
  local copies, waits for them, and re-layouts  36.6 us (9%)
  blocking collectives  32.7 us (8%)
  other arithmetic  32.5 us (8%)
  matrix products  28.9 us (7%)
  between operations  21.5 us (5%)
    all_gather x1, waiting for transfers between devices, body(): gathered = lax.all_gather(own_rows, 'dp', axis=0, tiled=True)  111 us
    ppermute x7, waiting for transfers between devices, body(): arrived[shift] = lax.ppermute(outgoing, 'fsdp', ring)  67 us
    all_gather x1, blocking collectives, body(): head_rows = lax.all_gather(late_weight, 'fsdp', axis=1, tiled=True)  32.7 us
    all_gather x1, waiting for transfers between devices, body(): all_heads = lax.all_gather(tile_out, 'dp', axis=0, tiled=False)  28.9 us
    ppermute x7, starting transfers between devices, body(): arrived[shift] = lax.ppermute(outgoing, 'fsdp', ring)  24.9 us
    reshape x2, local copies, waits for them, and re-layouts, body(): merged = square.reshape(SLOTS, halves * halves, block * 4)  16.2 us
    dot_general x1, matrix products, body(): projected = jnp.dot(normed, full_qkv, preferred_element_type=jnp.float32)  12.8 us
    all_to_all x1, waiting for transfers between devices, body(): lax.all_to_all(head_rows, 'dp', split_axis=1, concat_axis=0, tiled=True)  11.1 us
  transfers between devices with their start and end apart: 12, of which 6 were waited for; matrix products, arithmetic and copies ran while one was open for 6% of the time, Pallas kernels for 0%

profile of v10, /device:TPU:8, one launch (start us, length us, event | category | flops | bytes accessed | tf_op | source)
XLA Modules:
  0.0 421.4 jit_solution(6016886823988938758)
XLA Ops:
  7.3 2.6 broadcast_in_dim.133
  9.9 5.7 %all-to-all-start = ((bf16[8,400,384]{2,1,0:T(8,128)(2,1)}), bf16[8,400,384]{2,1,0:T(8,128)(2,1)S(1)}, u32[]{:S(2)}, u32[]{:S(2)}) async-start(bf16[8,400,384]{2,1,0:T(8,128)(2,1)} %broadcast_in_dim.133), calls=%async_computation | async-start | bytes 4915200 | tf_op jit(solution)/shard_map/all_to_all | solution.py:61
  15.5 111.4 %all-gather.5.cloned.1.call-done = bf16[1,2176,3200]{2,1,0:T(8,128)(2,1)} async-done(((bf16[1,136,3200]{2,1,0:T(8,128)(2,1)}), bf16[1,2176,3200]{2,1,0:T(8,128)(2,1)}) %all-gather.5.cloned.1.call-update) | async-done | bytes 13926416 | tf_op jit(solution)/shard_map/all_gather | solution.py:74
  127.0 7.7 %fusion = f32[2176]{0:T(1024)S(1)} fusion(bf16[1,2176,3200]{2,1,0:T(8,128)(2,1)} %all-gather.5.cloned.1.call-done), kind=kLoop, calls=%fused_computation.2 | loop fusion | flops 20887424 | bytes 13935104 | tf_op jit(solution)/shard_map/reduce_sum | solution.py:77
  134.7 1.4 copy-done
  136.1 12.8 %fusion.53 = (bf16[2176,384]{1,0:T(8,128)(2,1)}, f32[2176,384]{1,0:T(8,128)S(1)}) fusion(bf16[3200,384]{1,0:T(8,128)(2,1)} %bitcast.85, bf16[1,2176,3200]{2,1,0:T(8,128)(2,1)} %all-gather.5.cloned.1.call-done, f32[3200]{0:T(1024)S(1)} %copy-done.5, f32[2176]{0:T(1024)S(1)} %add_rsqrt_fusion), kind=kOutput, calls=%fused_computation.131 | convolution fusion | flops 5376425984 | bytes 21419008 | tf_op jit(solution)/shard_map/dot_general | solution.py:79
  150.4 5.8 %all-to-all-start.1 = ((f32[16,2,2176]{2,1,0:T(2,128)}), f32[16,2,2176]{2,1,0:T(2,128)}, u32[]{:S(2)}, u32[]{:S(2)}) async-start(f32[16,2,2176]{2,1,0:T(2,128)} %broadcast_in_dim.134), calls=%async_computation.1 | async-start | bytes 557056 | tf_op jit(solution)/shard_map/all_to_all | solution.py:55
  156.5 6.9 %all-to-all-done.1 = f32[16,2,2176]{2,1,0:T(2,128)} async-done(((f32[16,2,2176]{2,1,0:T(2,128)}), f32[16,2,2176]{2,1,0:T(2,128)}, u32[]{:S(2)}, u32[]{:S(2)}) %all-to-all-start.1) | async-done | bytes 278560 | tf_op jit(solution)/shard_map/all_to_all | solution.py:55
  164.6 1.2 multiply_convert_fusion.1
  168.0 2.0 fusion.17
  170.6 1.9 fusion.16
  174.4 32.7 %all_gather.15 = bf16[128,3200]{0,1:T(8,128)(2,1)} all-gather(bf16[128,400]{0,1:T(8,128)(2,1)S(1)} %copy-done.1), channel_id=1, replica_groups=mesh['fsdp'=8,'dp'=16] {'fsdp'}, dimensions={1}, use_global_device_ids=true | all-gather | bytes 921600 | tf_op jit(solution)/shard_map/all_gather | solution.py:119
  207.1 6.7 %all-to-all-start.2 = ((bf16[128,16,200]{0,2,1:T(8,128)(2,1)}), bf16[128,16,200]{0,2,1:T(8,128)(2,1)S(1)}, u32[]{:S(2)}, u32[]{:S(2)}) async-start(bf16[128,16,200]{0,2,1:T(8,128)(2,1)} %bitcast.15), calls=%async_computation.2 | async-start | bytes 1638400 | tf_op jit(solution)/shard_map/all_to_all | solution.py:120
  213.9 2.0 constant_dynamic-slice_fusion
  218.2 11.1 %all-to-all-done.2 = bf16[128,16,200]{0,2,1:T(8,128)(2,1)S(1)} async-done(((bf16[128,16,200]{0,2,1:T(8,128)(2,1)}), bf16[128,16,200]{0,2,1:T(8,128)(2,1)S(1)}, u32[]{:S(2)}, u32[]{:S(2)}) %all-to-all-start.2) | async-done | bytes 819232 | tf_op jit(solution)/shard_map/all_to_all | solution.py:120
  229.3 28.9 %all-gather.7.cloned.1.call-done = bf16[32,1024,128]{2,1,0:T(8,128)(2,1)} async-done(((bf16[2,1024,128]{2,1,0:T(8,128)(2,1)}), bf16[32,1024,128]{2,1,0:T(8,128)(2,1)}) %all-gather.7.cloned.1.call-update) | async-done | bytes 8388624 | tf_op jit(solution)/shard_map/all_gather | solution.py:118
  258.3 10.6 %convolution_convert_fusion = bf16[16,2,1024,200]{2,3,1,0:T(8,128)(2,1)} fusion(bf16[16,2,1024,128]{3,2,1,0:T(8,128)(2,1)} %bitcast.83, bf16[128,16,200]{0,2,1:T(8,128)(2,1)S(1)} %all-to-all-done.2), kind=kOutput, calls=%fused_computation.10 | convolution fusion | flops 1684275200 | bytes 22315008 | tf_op jit(solution)/shard_map/htsc,hcd->htsd/dot_general | solution.py:121
  268.9 9.3 %convert_reduce_fusion = f32[2,1024,200]{1,2,0:T(8,128)} fusion(bf16[16,2,1024,200]{2,3,1,0:T(8,128)(2,1)} %convolution_convert_fusion), kind=kLoop, calls=%fused_computation.5 | loop fusion | flops 12697600 | bytes 14745600 | tf_op jit(solution)/shard_map/reduce_sum | solution.py:127
  278.2 2.8 copy.36
  281.0 1.7 fusion.18
  282.7 7.1 %copy.38 = bf16[2,16,16,200,2,2]{2,1,5,4,3,0:T(8,128)(2,1)} copy(bf16[2,16,16,200,2,2]{3,2,5,4,1,0:T(8,128)(2,1)S(1)} %fusion.18) | data formatting | bytes 1638400 | tf_op jit(solution)/shard_map/transpose | solution.py:133
  289.8 8.1 %reshape.182 = bf16[2,256,800]{1,2,0:T(8,128)(2,1)S(1)} reshape(bf16[2,16,16,200,2,2]{2,1,5,4,3,0:T(8,128)(2,1)} %copy.38) | data formatting | bytes 1638400 | tf_op jit(solution)/shard_map/reshape | solution.py:134
  297.9 2.7 broadcast_select_fusion
  301.2 1.3 collective-permute-start.1
  303.6 3.1 collective-permute-start.2
  315.0 8.1 %reshape.181 = bf16[1,2,256,800]{2,3,1,0:T(8,128)(2,1)S(1)} reshape(bf16[2,16,16,200,2,2]{2,1,5,4,3,0:T(8,128)(2,1)} %copy.38) | data formatting | bytes 1638400 | tf_op jit(solution)/shard_map/reshape | solution.py:134
  323.2 2.4 collective-permute-start.6
  326.1 16.1 %collective-permute-start.4 = (bf16[2,256,800]{1,2,0:T(8,128)(2,1)}, bf16[2,256,800]{1,2,0:T(8,128)(2,1)S(1)}, u32[]{:S(2)}, u32[]{:S(2)}) collective-permute-start(bf16[2,256,800]{1,2,0:T(8,128)(2,1)} %get-tuple-element.31), channel_id=1, source_target_pairs={{0,80},{16,96},{32,112},{48,0},{64,16},{80,32},{96,48},{112,64},{1... | collective-permute-start | bytes 2457608 | tf_op jit(solution)/shard_map/ppermute | solution.py:142
  343.3 43.4 %collective-permute-done.2 = bf16[2,256,800]{1,2,0:T(8,128)(2,1)S(1)} collective-permute-done((bf16[2,256,800]{1,2,0:T(8,128)(2,1)}, bf16[2,256,800]{1,2,0:T(8,128)(2,1)S(1)}, u32[]{:S(2)}, u32[]{:S(2)}) %collective-permute-start.2) | collective-permute-done | bytes 819232 | tf_op jit(solution)/shard_map/ppermute | solution.py:142
  386.9 23.6 %collective-permute-done.5 = bf16[2,256,800]{1,2,0:T(8,128)(2,1)S(1)} collective-permute-done((bf16[2,256,800]{1,2,0:T(8,128)(2,1)}, bf16[2,256,800]{1,2,0:T(8,128)(2,1)S(1)}, u32[]{:S(2)}, u32[]{:S(2)}) %collective-permute-start.5) | collective-permute-done | bytes 819232 | tf_op jit(solution)/shard_map/ppermute | solution.py:142
  410.6 2.6 dynamic-slice_select_fusion.3
  413.2 1.4 pad_maximum_fusion
  (64 shorter events, 14.8 us)
Async XLA Ops:
  6.5 120.4 %all-gather.5.cloned.1.call-start = ((), (), s32[]{:S(2)}) async-start(), calls=%async_computation.3 | async-start | bytes 14796800 | tf_op jit(solution)/shard_map/all_gather | solution.py:74
  9.9 124.8 %all-to-all-start = ((bf16[8,400,384]{2,1,0:T(8,128)(2,1)}), bf16[8,400,384]{2,1,0:T(8,128)(2,1)S(1)}, u32[]{:S(2)}, u32[]{:S(2)}) async-start(bf16[8,400,384]{2,1,0:T(8,128)(2,1)} %broadcast_in_dim.133), calls=%async_computation | async-start | bytes 4915200 | tf_op jit(solution)/shard_map/all_to_all | solution.py:61
  15.5 120.6 %copy-start.5 = (f32[3200]{0:T(1024)S(1)}, f32[3200]{0:T(1024)}, u32[]{:S(2)}) copy-start(f32[3200]{0:T(1024)} %param.9) | copy-start | bytes 38404
  134.7 1.4 copy-start
  136.1 20.4 %copy-start.2 = (f32[2,128]{1,0:T(2,128)S(1)}, f32[2,128]{1,0:T(2,128)}, u32[]{:S(2)}) copy-start(f32[2,128]{1,0:T(2,128)} %param.11) | copy-start | bytes 3076
  150.4 13.0 %all-to-all-start.1 = ((f32[16,2,2176]{2,1,0:T(2,128)}), f32[16,2,2176]{2,1,0:T(2,128)}, u32[]{:S(2)}, u32[]{:S(2)}) async-start(f32[16,2,2176]{2,1,0:T(2,128)} %broadcast_in_dim.134), calls=%async_computation.1 | async-start | bytes 557056 | tf_op jit(solution)/shard_map/all_to_all | solution.py:55
  156.3 102.0 %all-gather.7.cloned.1.call-start = ((), (), s32[]{:S(2)}) async-start(), calls=%async_computation.4 | async-start | bytes 8912896 | tf_op jit(solution)/shard_map/all_gather | solution.py:118
  170.6 3.7 copy-start.3
  170.6 3.7 copy-start.4
  170.6 3.8 copy-start.1
  207.1 22.3 %all-to-all-start.2 = ((bf16[128,16,200]{0,2,1:T(8,128)(2,1)}), bf16[128,16,200]{0,2,1:T(8,128)(2,1)S(1)}, u32[]{:S(2)}, u32[]{:S(2)}) async-start(bf16[128,16,200]{0,2,1:T(8,128)(2,1)} %bitcast.15), calls=%async_computation.2 | async-start | bytes 1638400 | tf_op jit(solution)/shard_map/all_to_all | solution.py:120
  300.5 25.5 %collective-permute-start = (bf16[2,256,800]{1,2,0:T(8,128)(2,1)}, bf16[2,256,800]{1,2,0:T(8,128)(2,1)S(1)}, u32[]{:S(2)}, u32[]{:S(2)}) collective-permute-start(bf16[2,256,800]{1,2,0:T(8,128)(2,1)} %get-tuple-element.35), channel_id=1, source_target_pairs={{0,16},{16,32},{32,48},{48,64},{64,80},{80,96},{96,112},{112,0},{1... | collective-permute-start | bytes 2457608 | tf_op jit(solution)/shard_map/ppermute | solution.py:142
  301.2 41.1 %collective-permute-start.1 = (bf16[2,256,800]{1,2,0:T(8,128)(2,1)}, bf16[2,256,800]{1,2,0:T(8,128)(2,1)S(1)}, u32[]{:S(2)}, u32[]{:S(2)}) collective-permute-start(bf16[2,256,800]{1,2,0:T(8,128)(2,1)} %get-tuple-element.34), channel_id=1, source_target_pairs={{0,32},{16,48},{32,64},{48,80},{64,96},{80,112},{96,0},{112,16},{1... | collective-permute-start | bytes 2457608 | tf_op jit(solution)/shard_map/ppermute | solution.py:142
  303.6 83.1 %collective-permute-start.2 = (bf16[2,256,800]{1,2,0:T(8,128)(2,1)}, bf16[2,256,800]{1,2,0:T(8,128)(2,1)S(1)}, u32[]{:S(2)}, u32[]{:S(2)}) collective-permute-start(bf16[2,256,800]{1,2,0:T(8,128)(2,1)} %get-tuple-element.33), channel_id=1, source_target_pairs={{0,48},{16,64},{32,80},{48,96},{64,112},{80,0},{96,16},{112,32},{1... | collective-permute-start | bytes 2457608 | tf_op jit(solution)/shard_map/ppermute | solution.py:142
  323.2 87.4 %collective-permute-start.6 = (bf16[2,256,800]{1,2,0:T(8,128)(2,1)}, bf16[2,256,800]{1,2,0:T(8,128)(2,1)S(1)}, u32[]{:S(2)}, u32[]{:S(2)}) collective-permute-start(bf16[2,256,800]{1,2,0:T(8,128)(2,1)} %get-tuple-element.29), channel_id=1, source_target_pairs={{0,112},{16,0},{32,16},{48,32},{64,48},{80,64},{96,80},{112,96},{1... | collective-permute-start | bytes 2457608 | tf_op jit(solution)/shard_map/ppermute | solution.py:142
  325.6 61.2 %collective-permute-start.3 = (bf16[2,256,800]{1,2,0:T(8,128)(2,1)}, bf16[2,256,800]{1,2,0:T(8,128)(2,1)S(1)}, u32[]{:S(2)}, u32[]{:S(2)}) collective-permute-start(bf16[2,256,800]{1,2,0:T(8,128)(2,1)} %get-tuple-element.32), channel_id=1, source_target_pairs={{0,64},{16,80},{32,96},{48,112},{64,0},{80,16},{96,32},{112,48},{1... | collective-permute-start | bytes 2457608 | tf_op jit(solution)/shard_map/ppermute | solution.py:142
  326.1 60.7 %collective-permute-start.4 = (bf16[2,256,800]{1,2,0:T(8,128)(2,1)}, bf16[2,256,800]{1,2,0:T(8,128)(2,1)S(1)}, u32[]{:S(2)}, u32[]{:S(2)}) collective-permute-start(bf16[2,256,800]{1,2,0:T(8,128)(2,1)} %get-tuple-element.31), channel_id=1, source_target_pairs={{0,80},{16,96},{32,112},{48,0},{64,16},{80,32},{96,48},{112,64},{1... | collective-permute-start | bytes 2457608 | tf_op jit(solution)/shard_map/ppermute | solution.py:142
  342.3 68.2 %collective-permute-start.5 = (bf16[2,256,800]{1,2,0:T(8,128)(2,1)}, bf16[2,256,800]{1,2,0:T(8,128)(2,1)S(1)}, u32[]{:S(2)}, u32[]{:S(2)}) collective-permute-start(bf16[2,256,800]{1,2,0:T(8,128)(2,1)} %get-tuple-element.30), channel_id=1, source_target_pairs={{0,96},{16,112},{32,0},{48,16},{64,32},{80,48},{96,64},{112,80},{1... | collective-permute-start | bytes 2457608 | tf_op jit(solution)/shard_map/ppermute | solution.py:142
Sparse Core Ops, SparseCore 0:
  9.8 117.1 all-gather.4
  173.5 84.7 all-gather.6

commit v11 on v6

--- a/solution.py
+++ b/solution.py
@@ -77,10 +77,17 @@
     model_width = own_rows.shape[1]
     block = model_width // groups
     swap = [(0, 1), (1, 0)]
-    head_rows = lax.all_gather(out_weight, "fsdp", axis=1, tiled=True)
+    spread = jnp.broadcast_to(out_weight[None], (row_count,) + out_weight.shape)
+    head_rows = lax.all_to_all(spread, "fsdp", split_axis=0, concat_axis=0, tiled=True)
+    per_row = out_weight.shape[1] // block
+    head_rows = head_rows.reshape(row_count, HEAD_DIM, per_row, block).transpose(0, 2, 1, 3)
     weight_block = lax.all_to_all(
-        head_rows, ("chip", "core"), split_axis=1, concat_axis=0, tiled=True
-    )
+        head_rows.reshape(groups, HEAD_DIM, block),
+        ("chip", "core"),
+        split_axis=0,
+        concat_axis=0,
+        tiled=True,
+    ).reshape(groups * HEAD_DIM, block)
     pair_weight = pair_up(weight_block, core, swap, 1)
     full_qkv = gather_blocks(qkv_weight, "fsdp", row_count)
     pair_qkv = pair_up(full_qkv, core, swap, 1)

time: 409 us -> 397 us (0.971)
  blocking collectives: 63.1 us -> 19 us
  waiting for transfers between devices: 190 us -> 220 us
    all_gather x1 -> x0, blocking collectives: 63.1 us -> none  [body(): head_rows = lax.all_gather(out_weight, 'fsdp', axis=1, tiled=True)]
    all_to_all x1, waiting for transfers between devices: 0.01 us -> 30.7 us  [gather_blocks(): lax.all_to_all(spread, axis_name, split_axis=0, concat_axis=0, tiled=True)]
    all_to_all x0 -> x1, blocking collectives: none -> 19 us  [body(): lax.all_to_all(spread, 'fsdp', split_axis=0, concat_axis=0, tiled=True)]
    reshape x0 -> x3, local copies, waits for them, and re-layouts: none -> 4.42 us  [the longest x2 3.44 us: body(): head_rows.reshape(groups, HEAD_DIM, block)]
  transfers between devices with their start and end apart: 11 -> 11, of which waited for: 8 -> 9; matrix products, arithmetic and copies ran while one was open for 5% -> 6% of each run, Pallas kernels for 0% -> 0%
where the time goes in v11:
time: 397 us; the launch traced here: 396 us
  waiting for transfers between devices  220 us (55%)
  local copies, waits for them, and re-layouts  39.9 us (10%)
  other arithmetic  36.8 us (9%)
  starting transfers between devices  29.1 us (7%)
  matrix products  29 us (7%)
  between operations  21.5 us (5%)
  blocking collectives  19 us (5%)
    all_to_all x1, waiting for transfers between devices, body(): lax.all_to_all(outgoing, 'fsdp', split_axis=0, concat_axis=0, tiled=True)  80.9 us
    all_to_all x1, waiting for transfers between devices, body(): lax.all_to_all(outgoing.reshape(groups, half_length, HEAD_DIM), ('chip',...  55.5 us
    all_to_all x1, waiting for transfers between devices, gather_blocks(): lax.all_to_all(spread, axis_name, split_axis=0, concat_axis=0, tiled=True)  30.7 us
    all_gather x1, waiting for transfers between devices, body(): half = lax.all_gather(own_rows, 'chip', axis=0, tiled=True)  26.1 us
    all_to_all x1, blocking collectives, body(): lax.all_to_all(spread, 'fsdp', split_axis=0, concat_axis=0, tiled=True)  19 us
    all_to_all x1, waiting for transfers between devices, body(): lax.all_to_all(head_rows.reshape(groups, HEAD_DIM, block), ('chip', 'core...  15 us
    dot_general x1, matrix products, body(): jnp.einsum('hsc,hcd->hsd', all_heads, pair_weight.reshape(groups, HEAD_DI...  11.4 us
    transpose x2, local copies, waits for them, and re-layouts, merge_tiles(): patches.reshape(halves, 2, halves, 2, columns).transpose(0, 2, 4, 1, 3)  9.74 us
  transfers between devices with their start and end apart: 11, of which 9 were waited for; matrix products, arithmetic and copies ran while one was open for 6% of the time, Pallas kernels for 0%

profile of v11, /device:TPU:8, one launch (start us, length us, event | category | flops | bytes accessed | tf_op | source)
XLA Modules:
  0.0 395.7 jit_solution(15600557721737662386)
XLA Ops:
  8.3 19.0 %all_to_all.30 = bf16[8,128,400]{1,2,0:T(8,128)(2,1)S(1)} all-to-all(bf16[8,128,400]{1,2,0:T(8,128)(2,1)S(1)} %broadcast_in_dim.95), channel_id=1, replica_groups=mesh['fsdp'=8,'chip'=8,'core'=2] {'fsdp'}, dimensions={0} | all-to-all | bytes 1638400 | tf_op jit(solution)/shard_map/all_to_all | solution.py:81
  27.3 1.7 broadcast_in_dim.94
  29.0 3.6 all-to-all-start
  34.1 2.3 copy.108
  36.4 30.7 %all-to-all-done = bf16[8,400,384]{2,1,0:T(8,128)(2,1)S(1)} async-done(((bf16[8,400,384]{2,1,0:T(8,128)(2,1)}), bf16[8,400,384]{2,1,0:T(8,128)(2,1)S(1)}, u32[]{:S(2)}, u32[]{:S(2)}) %all-to-all-start) | async-done | bytes 2457632 | tf_op jit(solution)/shard_map/all_to_all | solution.py:57
  67.1 8.0 %all-to-all-start.2 = ((bf16[16,128,200]{1,2,0:T(8,128)(2,1)}), bf16[16,128,200]{1,2,0:T(8,128)(2,1)S(1)}, u32[]{:S(2)}, u32[]{:S(2)}) async-start(bf16[16,128,200]{1,2,0:T(8,128)(2,1)} %copy.108), calls=%async_computation.2 | async-start | bytes 1638400 | tf_op jit(solution)/shard_map/all_to_all | solution.py:84
  75.2 15.0 %all-to-all-done.2 = bf16[16,128,200]{1,2,0:T(8,128)(2,1)S(1)} async-done(((bf16[16,128,200]{1,2,0:T(8,128)(2,1)}), bf16[16,128,200]{1,2,0:T(8,128)(2,1)S(1)}, u32[]{:S(2)}, u32[]{:S(2)}) %all-to-all-start.2) | async-done | bytes 819232 | tf_op jit(solution)/shard_map/all_to_all | solution.py:84
  91.8 2.3 collective-permute-done.2
  97.4 2.1 broadcast_select_fusion.2
  99.6 2.7 pad_maximum_fusion
  102.2 26.1 %all-gather.3.cloned.1.call-done = bf16[1,1088,3200]{2,1,0:T(8,128)(2,1)} async-done(((bf16[1,136,3200]{2,1,0:T(8,128)(2,1)}), bf16[1,1088,3200]{2,1,0:T(8,128)(2,1)}) %all-gather.3.cloned.1.call-update) | async-done | bytes 6963216 | tf_op jit(solution)/shard_map/all_gather | solution.py:96
  128.3 4.6 %fusion.2 = f32[1088]{0:T(1024)S(1)} fusion(bf16[1,1088,3200]{2,1,0:T(8,128)(2,1)} %all-gather.3.cloned.1.call-done), kind=kLoop, calls=%fused_computation.7 | loop fusion | flops 10443712 | bytes 6967552 | tf_op jit(solution)/shard_map/reduce_sum | solution.py:101
  133.3 9.5 %fusion.6 = f32[1088,768]{0,1:T(8,128)S(1)} fusion(bf16[3200,768]{1,0:T(8,128)(2,1)} %pad_maximum_fusion, bf16[1,1088,3200]{2,1,0:T(8,128)(2,1)S(1)} %copy-done, f32[3200]{0:T(1024)S(1)} %copy-done.8, f32[1088]{0:T(1024)S(1)} %add_rsqrt_fusion), kind=kOutput, calls=%fused_computation.12 | convolution fusion | flops 5361664000 | bytes 15237888 | tf_op jit(solution)/shard_map/dot_general | solution.py:103
  143.8 5.6 %all-to-all-start.3 = ((f32[8,2,1088]{2,1,0:T(2,128)}), f32[8,2,1088]{2,1,0:T(2,128)}, u32[]{:S(2)}, u32[]{:S(2)}) async-start(f32[8,2,1088]{2,1,0:T(2,128)} %broadcast_in_dim.96), calls=%async_computation.3 | async-start | bytes 147456 | tf_op jit(solution)/shard_map/all_to_all | solution.py:51
  150.3 5.9 %all-to-all-done.3 = f32[8,2,1088]{2,1,0:T(2,128)} async-done(((f32[8,2,1088]{2,1,0:T(2,128)}), f32[8,2,1088]{2,1,0:T(2,128)}, u32[]{:S(2)}, u32[]{:S(2)}) %all-to-all-start.3) | async-done | bytes 69664 | tf_op jit(solution)/shard_map/all_to_all | solution.py:51
  162.9 3.2 fusion.45
  166.2 4.9 %fusion.12 = bf16[2,1025,128]{2,1,0:T(8,128)(2,1)S(1)} fusion(bf16[2,1025,128]{2,1,0:T(8,128)(2,1)S(1)} %reshape_squeeze.11, f32[2,1025]{1,0:T(2,128)S(1)} %fusion.45, bf16[2,1025,128]{2,1,0:T(8,128)(2,1)S(1)} %reshape_squeeze.9, bf16[2,1025,128]{2,1,0:T(8,128)(2,1)S(1)} %reshape_squeeze.10), kind=kOutput, calls=%fused_computation.19 | convolution fusion | flops 1084510464 | bytes 2107400 | tf_op jit(solution)/shard_map/sqk,skc->sqc/dot_general | solution.py:142
  171.2 3.0 broadcast_in_dim.98
  174.3 5.7 %all-to-all-start.4 = ((bf16[16,1088,128]{2,1,0:T(8,128)(2,1)}), bf16[16,1088,128]{2,1,0:T(8,128)(2,1)}, u32[]{:S(2)}, u32[]{:S(2)}) async-start(bf16[16,1088,128]{2,1,0:T(8,128)(2,1)} %bitcast.100), calls=%async_computation.4 | async-start | bytes 8912896 | tf_op jit(solution)/shard_map/all_to_all | solution.py:155
  181.1 1.9 constant_dynamic-slice_fusion.3
  184.5 55.5 %all-to-all-done.4 = bf16[16,1088,128]{2,1,0:T(8,128)(2,1)} async-done(((bf16[16,1088,128]{2,1,0:T(8,128)(2,1)}), bf16[16,1088,128]{2,1,0:T(8,128)(2,1)}, u32[]{:S(2)}, u32[]{:S(2)}) %all-to-all-start.4) | async-done | bytes 4456480 | tf_op jit(solution)/shard_map/all_to_all | solution.py:155
  240.0 11.4 %convolution_convert_fusion = bf16[16,1088,400]{1,2,0:T(8,128)(2,1)} fusion(bf16[16,1088,128]{2,1,0:T(8,128)(2,1)} %all-to-all-done.4, bf16[2048,400]{0,1:T(8,128)(2,1)S(1)} %copy-done.1), kind=kOutput, calls=%fused_computation.2 | convolution fusion | flops 1789542400 | bytes 20021248 | tf_op jit(solution)/shard_map/hsc,hcd->hsd/dot_general | solution.py:162
  251.4 7.8 %convert_reduce_fusion = f32[1088,400]{0,1:T(8,128)S(1)} fusion(bf16[16,1088,400]{1,2,0:T(8,128)(2,1)} %convolution_convert_fusion), kind=kLoop, calls=%fused_computation.1 | loop fusion | flops 13491200 | bytes 15667200 | tf_op jit(solution)/shard_map/reduce_sum | solution.py:168
  260.0 1.8 collective-permute-done.4
  265.1 4.9 %copy.125 = bf16[16,16,200,2,2]{1,0,4,3,2:T(8,128)(2,1)S(1)} copy(bf16[16,16,200,2,2]{2,4,1,3,0:T(2,128)(2,1)} %bitcast.115) | data formatting | bytes 819200 | tf_op jit(solution)/shard_map/transpose | solution.py:22
  270.0 3.9 stack_reshape.23
  273.8 4.9 %copy.124 = bf16[16,16,200,2,2]{1,0,4,3,2:T(8,128)(2,1)S(1)} copy(bf16[16,16,200,2,2]{2,4,1,3,0:T(2,128)(2,1)} %bitcast.114) | data formatting | bytes 819200 | tf_op jit(solution)/shard_map/transpose | solution.py:22
  278.7 3.8 stack_reshape.22
  283.8 3.3 broadcast_select_fusion
  287.1 4.8 %all-to-all-start.5 = ((bf16[8,2,256,800]{2,3,1,0:T(8,128)(2,1)}), bf16[8,2,256,800]{2,3,1,0:T(8,128)(2,1)}, u32[]{:S(2)}, u32[]{:S(2)}) async-start(bf16[8,2,256,800]{2,3,1,0:T(8,128)(2,1)} %broadcast_select_fusion), calls=%async_computation.5 | async-start | bytes 13107200 | tf_op jit(solution)/shard_map/all_to_all | solution.py:185
  302.7 80.9 %all-to-all-done.5 = bf16[8,2,256,800]{2,3,1,0:T(8,128)(2,1)} async-done(((bf16[8,2,256,800]{2,3,1,0:T(8,128)(2,1)}), bf16[8,2,256,800]{2,3,1,0:T(8,128)(2,1)}, u32[]{:S(2)}, u32[]{:S(2)}) %all-to-all-start.5) | async-done | bytes 6553632 | tf_op jit(solution)/shard_map/all_to_all | solution.py:185
  383.6 3.9 dynamic-slice_select_fusion.3
  (92 shorter events, 29.6 us)
Async XLA Ops:
  6.5 20.7 %copy-start.4 = (bf16[400,384]{1,0:T(8,128)(2,1)S(1)}, bf16[400,384]{1,0:T(8,128)(2,1)}, u32[]{:S(2)}) copy-start(bf16[400,384]{1,0:T(8,128)(2,1)} %param.10) | copy-start | bytes 921604
  6.5 121.8 %all-gather.3.cloned.1.call-start = ((), (), s32[]{:S(2)}) async-start(), calls=%async_computation.6 | async-start | bytes 7833600 | tf_op jit(solution)/shard_map/all_gather | solution.py:96
  29.0 38.1 %all-to-all-start = ((bf16[8,400,384]{2,1,0:T(8,128)(2,1)}), bf16[8,400,384]{2,1,0:T(8,128)(2,1)S(1)}, u32[]{:S(2)}, u32[]{:S(2)}) async-start(bf16[8,400,384]{2,1,0:T(8,128)(2,1)} %broadcast_in_dim.94), calls=%async_computation | async-start | bytes 4915200 | tf_op jit(solution)/shard_map/all_to_all | solution.py:57
  34.1 57.7 %copy-start.7 = (f32[2,128]{1,0:T(2,128)S(1)}, f32[2,128]{1,0:T(2,128)}, u32[]{:S(2)}) copy-start(f32[2,128]{1,0:T(2,128)} %param.11) | copy-start | bytes 3076
  67.1 23.1 %all-to-all-start.2 = ((bf16[16,128,200]{1,2,0:T(8,128)(2,1)}), bf16[16,128,200]{1,2,0:T(8,128)(2,1)S(1)}, u32[]{:S(2)}, u32[]{:S(2)}) async-start(bf16[16,128,200]{1,2,0:T(8,128)(2,1)} %copy.108), calls=%async_computation.2 | async-start | bytes 1638400 | tf_op jit(solution)/shard_map/all_to_all | solution.py:84
  75.1 22.3 %collective-permute-start = (bf16[3200,384]{1,0:T(8,128)(2,1)S(1)}, bf16[3200,384]{1,0:T(8,128)(2,1)}, u32[]{:S(2)}, u32[]{:S(2)}) collective-permute-start(bf16[3200,384]{1,0:T(8,128)(2,1)S(1)} %bitcast.101), channel_id=1, source_target_pairs={{0,1},{1,0},{2,3},{3,2},{4,5},{5,4},{6,7},{7,6},{8,9},{9,8},{10,11... | collective-permute-start | bytes 7372808 | tf_op jit(solution)/shard_map/ppermute | solution.py:62
  91.1 3.5 collective-permute-start.1
  91.8 2.3 collective-permute-start.2
  128.3 5.0 %copy-start = (bf16[1,1088,3200]{2,1,0:T(8,128)(2,1)S(1)}, bf16[1,1088,3200]{2,1,0:T(8,128)(2,1)}, u32[]{:S(2)}) copy-start(bf16[1,1088,3200]{2,1,0:T(8,128)(2,1)} %all-gather.3.cloned.1.call-done) | copy-start | bytes 20889604
  128.3 5.0 %copy-start.8 = (f32[3200]{0:T(1024)S(1)}, f32[3200]{0:T(1024)}, u32[]{:S(2)}) copy-start(f32[3200]{0:T(1024)} %param.9) | copy-start | bytes 38404
  143.8 12.4 %all-to-all-start.3 = ((f32[8,2,1088]{2,1,0:T(2,128)}), f32[8,2,1088]{2,1,0:T(2,128)}, u32[]{:S(2)}, u32[]{:S(2)}) async-start(f32[8,2,1088]{2,1,0:T(2,128)} %broadcast_in_dim.96), calls=%async_computation.3 | async-start | bytes 147456 | tf_op jit(solution)/shard_map/all_to_all | solution.py:51
  157.1 1.1 copy-start.3
  159.4 2.6 collective-permute-start.3
  174.3 6.6 %copy-start.5 = (s32[8,2]{0,1:T(2,128)S(1)}, s32[8,2]{0,1:T(2,128)}, u32[]{:S(2)}) copy-start(s32[8,2]{0,1:T(2,128)} %param.14) | copy-start | bytes 196
  174.3 6.6 %copy-start.6 = (s32[8,2]{0,1:T(2,128)S(1)}, s32[8,2]{0,1:T(2,128)}, u32[]{:S(2)}) copy-start(s32[8,2]{0,1:T(2,128)} %param.15) | copy-start | bytes 196
  174.3 65.7 %all-to-all-start.4 = ((bf16[16,1088,128]{2,1,0:T(8,128)(2,1)}), bf16[16,1088,128]{2,1,0:T(8,128)(2,1)}, u32[]{:S(2)}, u32[]{:S(2)}) async-start(bf16[16,1088,128]{2,1,0:T(8,128)(2,1)} %bitcast.100), calls=%async_computation.4 | async-start | bytes 8912896 | tf_op jit(solution)/shard_map/all_to_all | solution.py:155
  180.0 60.0 %copy-start.1 = (bf16[2048,400]{0,1:T(8,128)(2,1)S(1)}, bf16[2048,400]{0,1:T(8,128)(2,1)}, u32[]{:S(2)}) copy-start(bf16[2048,400]{0,1:T(8,128)(2,1)} %pad_maximum_fusion.3) | copy-start | bytes 4915204
  251.4 7.8 %copy-start.2 = (bf16[1,1088,400]{1,2,0:T(8,128)(2,1)S(1)}, bf16[1,1088,400]{1,2,0:T(8,128)(2,1)}, u32[]{:S(2)}) copy-start(bf16[1,1088,400]{1,2,0:T(8,128)(2,1)} %copy.130) | copy-start | bytes 2611204
  259.6 2.2 collective-permute-start.4
  287.1 96.5 %all-to-all-start.5 = ((bf16[8,2,256,800]{2,3,1,0:T(8,128)(2,1)}), bf16[8,2,256,800]{2,3,1,0:T(8,128)(2,1)}, u32[]{:S(2)}, u32[]{:S(2)}) async-start(bf16[8,2,256,800]{2,3,1,0:T(8,128)(2,1)} %broadcast_select_fusion), calls=%async_computation.5 | async-start | bytes 13107200 | tf_op jit(solution)/shard_map/all_to_all | solution.py:185
Sparse Core Ops, SparseCore 0:
  9.7 118.6 all-gather.2

commit v12 on v11

--- a/solution.py
+++ b/solution.py
@@ -1,6 +1,7 @@
 import jax
 import jax.numpy as jnp
 from jax import lax
+from jax.experimental import pallas as pl
 from jax.sharding import Mesh, PartitionSpec as P
 
 HEAD_DIM = 128
@@ -56,6 +57,31 @@
     spread = jnp.broadcast_to(block_value[None], (groups,) + block_value.shape)
     collected = lax.all_to_all(spread, axis_name, split_axis=0, concat_axis=0, tiled=True)
     return collected.reshape((groups * block_value.shape[0],) + block_value.shape[1:])
+
+
+def head_sum_kernel(heads_ref, weight_ref, out_ref):
+    total = jnp.zeros(out_ref.shape, jnp.float32)
+    for head in range(heads_ref.shape[0]):
+        term = jnp.dot(heads_ref[head], weight_ref[head], preferred_element_type=jnp.float32)
+        total = total + term.astype(jnp.bfloat16).astype(jnp.float32)
+    out_ref[...] = total
+
+
+def head_sum(heads, weight):
+    count, rows, width = heads.shape
+    columns = weight.shape[2]
+    steps = 2
+    tile = rows // steps
+    return pl.pallas_call(
+        head_sum_kernel,
+        grid=(steps,),
+        in_specs=[
+            pl.BlockSpec((count, tile, width), lambda i: (0, i, 0)),
+            pl.BlockSpec((count, width, columns), lambda i: (0, 0, 0)),
+        ],
+        out_specs=pl.BlockSpec((tile, columns), lambda i: (i, 0)),
+        out_shape=jax.ShapeDtypeStruct((rows, columns), jnp.float32),
+    )(heads, weight)
 
 
 def pair_up(value, core, swap, axis):
@@ -159,13 +185,7 @@
         concat_axis=0,
         tiled=True,
     )
-    head_terms = jnp.einsum(
-        "hsc,hcd->hsd",
-        all_heads,
-        pair_weight.reshape(groups, HEAD_DIM, cores * block),
-        preferred_element_type=jnp.float32,
-    ).astype(jnp.bfloat16)
-    attention = jnp.sum(lax.optimization_barrier(head_terms).astype(jnp.float32), axis=0)
+    attention = head_sum(all_heads, pair_weight.reshape(groups, HEAD_DIM, cores * block))
     pair_tokens = lax.dynamic_slice_in_dim(half, chip * cores * block, cores * block, axis=1)
     pair_scale = lax.dynamic_slice_in_dim(layer_scale, chip * cores * block, cores * block)
     updated_half = (pair_tokens.astype(jnp.float32) + pair_scale * attention).astype(jnp.bfloat16)

time: 397 us -> 390 us (0.982)
  matrix products: 29 us -> 17.6 us
  Pallas kernels: 0 us -> 8.29 us
  other arithmetic: 36.8 us -> 31 us
    dot_general x1 -> x0, matrix products: 11.4 us -> none  [body(): jnp.einsum('hsc,hcd->hsd', all_heads, pair_weight.reshape(groups, HEAD_DI...]
    pallas_call x0 -> x1, Pallas kernels: none -> 8.29 us  [head_sum(): pl.pallas_call(head_sum_kernel, grid=(steps,), in_specs=[pl.BlockSpec((co...]
    reduce_sum x1 -> x0, other arithmetic: 7.82 us -> none  [body(): jnp.sum(lax.optimization_barrier(head_terms).astype(jnp.float32), axis=0)]
where the time goes in v12:
time: 390 us; the launch traced here: 389 us
  waiting for transfers between devices  222 us (57%)
  local copies, waits for them, and re-layouts  40.8 us (10%)
  other arithmetic  31 us (8%)
  starting transfers between devices  28.8 us (7%)
  between operations  21.4 us (5%)
  blocking collectives  19 us (5%)
  matrix products  17.6 us (5%)
  Pallas kernels  8.29 us (2%)
    all_to_all x1, waiting for transfers between devices, body(): lax.all_to_all(outgoing, 'fsdp', split_axis=0, concat_axis=0, tiled=True)  81.6 us
    all_to_all x1, waiting for transfers between devices, body(): lax.all_to_all(outgoing.reshape(groups, half_length, HEAD_DIM), ('chip',...  56.7 us
    all_to_all x1, waiting for transfers between devices, gather_blocks(): lax.all_to_all(spread, axis_name, split_axis=0, concat_axis=0, tiled=True)  30.7 us
    all_gather x1, waiting for transfers between devices, body(): half = lax.all_gather(own_rows, 'chip', axis=0, tiled=True)  26.1 us
    all_to_all x1, blocking collectives, body(): lax.all_to_all(spread, 'fsdp', split_axis=0, concat_axis=0, tiled=True)  19 us
    all_to_all x1, waiting for transfers between devices, body(): lax.all_to_all(head_rows.reshape(groups, HEAD_DIM, block), ('chip', 'core...  15 us
    transpose x2, local copies, waits for them, and re-layouts, merge_tiles(): patches.reshape(halves, 2, halves, 2, columns).transpose(0, 2, 4, 1, 3)  9.74 us
    dot_general x1, matrix products, body(): projected = jnp.dot(normed, pair_qkv, preferred_element_type=jnp.float32)  9.55 us
  transfers between devices with their start and end apart: 11, of which 9 were waited for; matrix products, arithmetic and copies ran while one was open for 6% of the time, Pallas kernels for 0%

profile of v12, /device:TPU:8, one launch (start us, length us, event | category | flops | bytes accessed | tf_op | source)
XLA Modules:
  0.0 389.1 jit_solution(13202650970801439037)
XLA Ops:
  8.3 19.0 %all_to_all.30 = bf16[8,128,400]{1,2,0:T(8,128)(2,1)S(1)} all-to-all(bf16[8,128,400]{1,2,0:T(8,128)(2,1)S(1)} %broadcast_in_dim.95), channel_id=1, replica_groups=mesh['fsdp'=8,'chip'=8,'core'=2] {'fsdp'}, dimensions={0} | all-to-all | bytes 1638400 | tf_op jit(solution)/shard_map/all_to_all | solution.py:107
  29.0 3.6 all-to-all-start
  34.1 2.3 copy.106
  36.4 30.7 %all-to-all-done = bf16[8,400,384]{2,1,0:T(8,128)(2,1)S(1)} async-done(((bf16[8,400,384]{2,1,0:T(8,128)(2,1)}), bf16[8,400,384]{2,1,0:T(8,128)(2,1)S(1)}, u32[]{:S(2)}, u32[]{:S(2)}) %all-to-all-start) | async-done | bytes 2457632 | tf_op jit(solution)/shard_map/all_to_all | solution.py:58
  67.1 8.0 %all-to-all-start.2 = ((bf16[16,128,200]{1,2,0:T(8,128)(2,1)}), bf16[16,128,200]{1,2,0:T(8,128)(2,1)S(1)}, u32[]{:S(2)}, u32[]{:S(2)}) async-start(bf16[16,128,200]{1,2,0:T(8,128)(2,1)} %copy.106), calls=%async_computation.2 | async-start | bytes 1638400 | tf_op jit(solution)/shard_map/all_to_all | solution.py:110
  75.2 15.0 %all-to-all-done.2 = bf16[16,128,200]{1,2,0:T(8,128)(2,1)S(1)} async-done(((bf16[16,128,200]{1,2,0:T(8,128)(2,1)}), bf16[16,128,200]{1,2,0:T(8,128)(2,1)S(1)}, u32[]{:S(2)}, u32[]{:S(2)}) %all-to-all-start.2) | async-done | bytes 819232 | tf_op jit(solution)/shard_map/all_to_all | solution.py:110
  91.8 2.3 collective-permute-done.2
  97.4 2.1 broadcast_select_fusion.2
  99.6 2.7 pad_maximum_fusion
  102.2 26.1 %all-gather.3.cloned.1.call-done = bf16[1,1088,3200]{2,1,0:T(8,128)(2,1)} async-done(((bf16[1,136,3200]{2,1,0:T(8,128)(2,1)}), bf16[1,1088,3200]{2,1,0:T(8,128)(2,1)}) %all-gather.3.cloned.1.call-update) | async-done | bytes 6963216 | tf_op jit(solution)/shard_map/all_gather | solution.py:122
  128.3 4.6 %fusion.2 = f32[1088]{0:T(1024)S(1)} fusion(bf16[1,1088,3200]{2,1,0:T(8,128)(2,1)} %all-gather.3.cloned.1.call-done), kind=kLoop, calls=%fused_computation.5 | loop fusion | flops 10443712 | bytes 6967552 | tf_op jit(solution)/shard_map/reduce_sum | solution.py:127
  133.3 9.5 %fusion.6 = f32[1088,768]{0,1:T(8,128)S(1)} fusion(bf16[3200,768]{1,0:T(8,128)(2,1)} %pad_maximum_fusion, bf16[1,1088,3200]{2,1,0:T(8,128)(2,1)S(1)} %copy-done, f32[3200]{0:T(1024)S(1)} %copy-done.7, f32[1088]{0:T(1024)S(1)} %add_rsqrt_fusion), kind=kOutput, calls=%fused_computation.10 | convolution fusion | flops 5361664000 | bytes 15237888 | tf_op jit(solution)/shard_map/dot_general | solution.py:129
  143.8 5.6 %all-to-all-start.3 = ((f32[8,2,1088]{2,1,0:T(2,128)}), f32[8,2,1088]{2,1,0:T(2,128)}, u32[]{:S(2)}, u32[]{:S(2)}) async-start(f32[8,2,1088]{2,1,0:T(2,128)} %broadcast_in_dim.96), calls=%async_computation.3 | async-start | bytes 147456 | tf_op jit(solution)/shard_map/all_to_all | solution.py:52
  150.3 5.9 %all-to-all-done.3 = f32[8,2,1088]{2,1,0:T(2,128)} async-done(((f32[8,2,1088]{2,1,0:T(2,128)}), f32[8,2,1088]{2,1,0:T(2,128)}, u32[]{:S(2)}, u32[]{:S(2)}) %all-to-all-start.3) | async-done | bytes 69664 | tf_op jit(solution)/shard_map/all_to_all | solution.py:52
  162.9 3.2 fusion.43
  166.2 4.9 %fusion.12 = bf16[2,1025,128]{2,1,0:T(8,128)(2,1)S(1)} fusion(bf16[2,1025,128]{2,1,0:T(8,128)(2,1)S(1)} %reshape_squeeze.11, f32[2,1025]{1,0:T(2,128)S(1)} %fusion.43, bf16[2,1025,128]{2,1,0:T(8,128)(2,1)S(1)} %reshape_squeeze.9, bf16[2,1025,128]{2,1,0:T(8,128)(2,1)S(1)} %reshape_squeeze.10), kind=kOutput, calls=%fused_computation.17 | convolution fusion | flops 1084510464 | bytes 2107400 | tf_op jit(solution)/shard_map/sqk,skc->sqc/dot_general | solution.py:168
  171.2 3.0 broadcast_in_dim.98
  174.2 5.7 %all-to-all-start.4 = ((bf16[16,1088,128]{2,1,0:T(8,128)(2,1)}), bf16[16,1088,128]{2,1,0:T(8,128)(2,1)}, u32[]{:S(2)}, u32[]{:S(2)}) async-start(bf16[16,1088,128]{2,1,0:T(8,128)(2,1)} %bitcast.97), calls=%async_computation.4 | async-start | bytes 8912896 | tf_op jit(solution)/shard_map/all_to_all | solution.py:181
  180.8 2.4 copy.118
  183.3 56.7 %all-to-all-done.4.heads_ref = bf16[16,1088,128]{2,1,0:T(8,128)(2,1)} async-done(((bf16[16,1088,128]{2,1,0:T(8,128)(2,1)}), bf16[16,1088,128]{2,1,0:T(8,128)(2,1)}, u32[]{:S(2)}, u32[]{:S(2)}) %all-to-all-start.4) | async-done | bytes 4456480 | tf_op jit(solution)/shard_map/all_to_all | solution.py:181
  239.9 8.3 %shard_map.82 = f32[1088,400]{1,0:T(8,128)} custom-call(bf16[16,1088,128]{2,1,0:T(8,128)(2,1)} %all-to-all-done.4.heads_ref, bf16[16,128,400]{2,1,0:T(8,128)(2,1)} %bitcast.99), custom_call_target="tpu_custom_call" | custom-call | tf_op jit(solution)/shard_map/pallas_call | solution.py:75
  248.2 2.7 fusion.13
  251.6 1.8 collective-permute-done.4
  256.3 4.9 %copy.124 = bf16[16,16,200,2,2]{1,0,4,3,2:T(8,128)(2,1)S(1)} copy(bf16[16,16,200,2,2]{2,4,1,3,0:T(2,128)(2,1)} %bitcast.112) | data formatting | bytes 819200 | tf_op jit(solution)/shard_map/transpose | solution.py:23
  261.2 3.9 stack_reshape.22
  265.0 2.1 reshape.276
  267.1 4.9 %copy.125 = bf16[16,16,200,2,2]{1,0,4,3,2:T(8,128)(2,1)S(1)} copy(bf16[16,16,200,2,2]{2,4,1,3,0:T(2,128)(2,1)} %bitcast.113) | data formatting | bytes 819200 | tf_op jit(solution)/shard_map/transpose | solution.py:23
  272.0 3.9 stack_reshape.23
  277.1 3.3 broadcast_select_fusion
  280.4 4.8 %all-to-all-start.5 = ((bf16[8,2,256,800]{2,3,1,0:T(8,128)(2,1)}), bf16[8,2,256,800]{2,3,1,0:T(8,128)(2,1)}, u32[]{:S(2)}, u32[]{:S(2)}) async-start(bf16[8,2,256,800]{2,3,1,0:T(8,128)(2,1)} %broadcast_select_fusion), calls=%async_computation.5 | async-start | bytes 13107200 | tf_op jit(solution)/shard_map/all_to_all | solution.py:205
  295.2 81.6 %all-to-all-done.5 = bf16[8,2,256,800]{2,3,1,0:T(8,128)(2,1)} async-done(((bf16[8,2,256,800]{2,3,1,0:T(8,128)(2,1)}), bf16[8,2,256,800]{2,3,1,0:T(8,128)(2,1)}, u32[]{:S(2)}, u32[]{:S(2)}) %all-to-all-start.5) | async-done | bytes 6553632 | tf_op jit(solution)/shard_map/all_to_all | solution.py:205
  376.8 4.0 %dynamic-slice_select_fusion.3 = (bf16[1,256,800]{1,2,0:T(8,128)(2,1)S(1)}, bf16[1,256,800]{1,2,0:T(8,128)(2,1)S(1)}, bf16[1,256,800]{1,2,0:T(8,128)(2,1)S(1)}, bf16[1,256,800]{1,2,0:T(8,128)(2,1)S(1)}) fusion(bf16[16,256,800]{1,2,0:T(8,128)(2,1)} %bitcast.33, s32[]{:T(128)S(6)} %select_n.180, pred[]{:T(512)} %get-tuple-element.44, s32[]{:T(128)S(6)} %select_n.192, ...), kind=kLoop, calls=%fused_computation.50 | loop fusion | flops 819200 | bytes 3276820 | tf_op jit(solution)/shard_map/jit(_where)/select_n | solution.py:46
  (86 shorter events, 28.5 us)
Async XLA Ops:
  6.5 20.7 %copy-start.3 = (bf16[400,384]{1,0:T(8,128)(2,1)S(1)}, bf16[400,384]{1,0:T(8,128)(2,1)}, u32[]{:S(2)}) copy-start(bf16[400,384]{1,0:T(8,128)(2,1)} %param.10) | copy-start | bytes 921604
  6.5 121.8 %all-gather.3.cloned.1.call-start = ((), (), s32[]{:S(2)}) async-start(), calls=%async_computation.6 | async-start | bytes 7833600 | tf_op jit(solution)/shard_map/all_gather | solution.py:122
  29.0 38.1 %all-to-all-start = ((bf16[8,400,384]{2,1,0:T(8,128)(2,1)}), bf16[8,400,384]{2,1,0:T(8,128)(2,1)S(1)}, u32[]{:S(2)}, u32[]{:S(2)}) async-start(bf16[8,400,384]{2,1,0:T(8,128)(2,1)} %broadcast_in_dim.94), calls=%async_computation | async-start | bytes 4915200 | tf_op jit(solution)/shard_map/all_to_all | solution.py:58
  34.1 57.7 %copy-start.6 = (f32[2,128]{1,0:T(2,128)S(1)}, f32[2,128]{1,0:T(2,128)}, u32[]{:S(2)}) copy-start(f32[2,128]{1,0:T(2,128)} %param.11) | copy-start | bytes 3076
  67.1 23.1 %all-to-all-start.2 = ((bf16[16,128,200]{1,2,0:T(8,128)(2,1)}), bf16[16,128,200]{1,2,0:T(8,128)(2,1)S(1)}, u32[]{:S(2)}, u32[]{:S(2)}) async-start(bf16[16,128,200]{1,2,0:T(8,128)(2,1)} %copy.106), calls=%async_computation.2 | async-start | bytes 1638400 | tf_op jit(solution)/shard_map/all_to_all | solution.py:110
  75.1 22.3 %collective-permute-start = (bf16[3200,384]{1,0:T(8,128)(2,1)S(1)}, bf16[3200,384]{1,0:T(8,128)(2,1)}, u32[]{:S(2)}, u32[]{:S(2)}) collective-permute-start(bf16[3200,384]{1,0:T(8,128)(2,1)S(1)} %bitcast.98), channel_id=1, source_target_pairs={{0,1},{1,0},{2,3},{3,2},{4,5},{5,4},{6,7},{7,6},{8,9},{9,8},{10,11... | collective-permute-start | bytes 7372808 | tf_op jit(solution)/shard_map/ppermute | solution.py:88
  91.1 3.5 collective-permute-start.1
  91.8 2.3 collective-permute-start.2
  128.3 5.0 %copy-start = (bf16[1,1088,3200]{2,1,0:T(8,128)(2,1)S(1)}, bf16[1,1088,3200]{2,1,0:T(8,128)(2,1)}, u32[]{:S(2)}) copy-start(bf16[1,1088,3200]{2,1,0:T(8,128)(2,1)} %all-gather.3.cloned.1.call-done) | copy-start | bytes 20889604
  128.3 5.0 %copy-start.7 = (f32[3200]{0:T(1024)S(1)}, f32[3200]{0:T(1024)}, u32[]{:S(2)}) copy-start(f32[3200]{0:T(1024)} %param.9) | copy-start | bytes 38404
  143.8 12.4 %all-to-all-start.3 = ((f32[8,2,1088]{2,1,0:T(2,128)}), f32[8,2,1088]{2,1,0:T(2,128)}, u32[]{:S(2)}, u32[]{:S(2)}) async-start(f32[8,2,1088]{2,1,0:T(2,128)} %broadcast_in_dim.96), calls=%async_computation.3 | async-start | bytes 147456 | tf_op jit(solution)/shard_map/all_to_all | solution.py:52
  157.1 1.1 copy-start.2
  159.4 2.6 collective-permute-start.3
  174.2 6.5 %copy-start.4 = (s32[8,2]{0,1:T(2,128)S(1)}, s32[8,2]{0,1:T(2,128)}, u32[]{:S(2)}) copy-start(s32[8,2]{0,1:T(2,128)} %param.14) | copy-start | bytes 196
  174.2 6.5 %copy-start.5 = (s32[8,2]{0,1:T(2,128)S(1)}, s32[8,2]{0,1:T(2,128)}, u32[]{:S(2)}) copy-start(s32[8,2]{0,1:T(2,128)} %param.15) | copy-start | bytes 196
  174.2 6.6 %copy-start.1 = (bf16[2048,400]{0,1:T(8,128)(2,1)S(1)}, bf16[2048,400]{0,1:T(8,128)(2,1)}, u32[]{:S(2)}) copy-start(bf16[2048,400]{0,1:T(8,128)(2,1)} %pad_maximum_fusion.3) | copy-start | bytes 4915204
  174.2 65.7 %all-to-all-start.4 = ((bf16[16,1088,128]{2,1,0:T(8,128)(2,1)}), bf16[16,1088,128]{2,1,0:T(8,128)(2,1)}, u32[]{:S(2)}, u32[]{:S(2)}) async-start(bf16[16,1088,128]{2,1,0:T(8,128)(2,1)} %bitcast.97), calls=%async_computation.4 | async-start | bytes 8912896 | tf_op jit(solution)/shard_map/all_to_all | solution.py:181
  251.4 1.9 collective-permute-start.4
  280.4 96.5 %all-to-all-start.5 = ((bf16[8,2,256,800]{2,3,1,0:T(8,128)(2,1)}), bf16[8,2,256,800]{2,3,1,0:T(8,128)(2,1)}, u32[]{:S(2)}, u32[]{:S(2)}) async-start(bf16[8,2,256,800]{2,3,1,0:T(8,128)(2,1)} %broadcast_select_fusion), calls=%async_computation.5 | async-start | bytes 13107200 | tf_op jit(solution)/shard_map/all_to_all | solution.py:205
Sparse Core Ops, SparseCore 0:
  9.7 118.6 all-gather.2

commit v13 on v12

--- a/solution.py
+++ b/solution.py
@@ -70,7 +70,7 @@
 def head_sum(heads, weight):
     count, rows, width = heads.shape
     columns = weight.shape[2]
-    steps = 2
+    steps = 4
     tile = rows // steps
     return pl.pallas_call(
         head_sum_kernel,

time: 390 us -> 391 us (level)
  no operation moved by 1% of the time
where the time goes in v13:
time: 391 us; the launch traced here: 389 us
  waiting for transfers between devices  222 us (57%)
  local copies, waits for them, and re-layouts  40.8 us (10%)
  other arithmetic  31 us (8%)
  starting transfers between devices  29 us (7%)
  between operations  21.4 us (5%)
  blocking collectives  19 us (5%)
  matrix products  17.6 us (5%)
  Pallas kernels  8.25 us (2%)
    all_to_all x1, waiting for transfers between devices, body(): lax.all_to_all(outgoing, 'fsdp', split_axis=0, concat_axis=0, tiled=True)  81.6 us
    all_to_all x1, waiting for transfers between devices, body(): lax.all_to_all(outgoing.reshape(groups, half_length, HEAD_DIM), ('chip',...  56.8 us
    all_to_all x1, waiting for transfers between devices, gather_blocks(): lax.all_to_all(spread, axis_name, split_axis=0, concat_axis=0, tiled=True)  30.7 us
    all_gather x1, waiting for transfers between devices, body(): half = lax.all_gather(own_rows, 'chip', axis=0, tiled=True)  26.1 us
    all_to_all x1, blocking collectives, body(): lax.all_to_all(spread, 'fsdp', split_axis=0, concat_axis=0, tiled=True)  19 us
    all_to_all x1, waiting for transfers between devices, body(): lax.all_to_all(head_rows.reshape(groups, HEAD_DIM, block), ('chip', 'core...  15 us
    transpose x2, local copies, waits for them, and re-layouts, merge_tiles(): patches.reshape(halves, 2, halves, 2, columns).transpose(0, 2, 4, 1, 3)  9.74 us
    dot_general x1, matrix products, body(): projected = jnp.dot(normed, pair_qkv, preferred_element_type=jnp.float32)  9.55 us
  transfers between devices with their start and end apart: 11, of which 9 were waited for; matrix products, arithmetic and copies ran while one was open for 6% of the time, Pallas kernels for 0%

profile of v13, /device:TPU:8, one launch (start us, length us, event | category | flops | bytes accessed | tf_op | source)
XLA Modules:
  0.0 389.5 jit_solution(3960832070101270575)
XLA Ops:
  8.3 19.0 %all_to_all.30 = bf16[8,128,400]{1,2,0:T(8,128)(2,1)S(1)} all-to-all(bf16[8,128,400]{1,2,0:T(8,128)(2,1)S(1)} %broadcast_in_dim.95), channel_id=1, replica_groups=mesh['fsdp'=8,'chip'=8,'core'=2] {'fsdp'}, dimensions={0} | all-to-all | bytes 1638400 | tf_op jit(solution)/shard_map/all_to_all | solution.py:107
  29.0 3.6 all-to-all-start
  34.1 2.3 copy.106
  36.4 30.7 %all-to-all-done = bf16[8,400,384]{2,1,0:T(8,128)(2,1)S(1)} async-done(((bf16[8,400,384]{2,1,0:T(8,128)(2,1)}), bf16[8,400,384]{2,1,0:T(8,128)(2,1)S(1)}, u32[]{:S(2)}, u32[]{:S(2)}) %all-to-all-start) | async-done | bytes 2457632 | tf_op jit(solution)/shard_map/all_to_all | solution.py:58
  67.1 8.0 %all-to-all-start.2 = ((bf16[16,128,200]{1,2,0:T(8,128)(2,1)}), bf16[16,128,200]{1,2,0:T(8,128)(2,1)S(1)}, u32[]{:S(2)}, u32[]{:S(2)}) async-start(bf16[16,128,200]{1,2,0:T(8,128)(2,1)} %copy.106), calls=%async_computation.2 | async-start | bytes 1638400 | tf_op jit(solution)/shard_map/all_to_all | solution.py:110
  75.2 15.0 %all-to-all-done.2 = bf16[16,128,200]{1,2,0:T(8,128)(2,1)S(1)} async-done(((bf16[16,128,200]{1,2,0:T(8,128)(2,1)}), bf16[16,128,200]{1,2,0:T(8,128)(2,1)S(1)}, u32[]{:S(2)}, u32[]{:S(2)}) %all-to-all-start.2) | async-done | bytes 819232 | tf_op jit(solution)/shard_map/all_to_all | solution.py:110
  91.8 2.3 collective-permute-done.2
  97.4 2.1 broadcast_select_fusion.2
  99.6 2.7 pad_maximum_fusion
  102.2 26.1 %all-gather.3.cloned.1.call-done = bf16[1,1088,3200]{2,1,0:T(8,128)(2,1)} async-done(((bf16[1,136,3200]{2,1,0:T(8,128)(2,1)}), bf16[1,1088,3200]{2,1,0:T(8,128)(2,1)}) %all-gather.3.cloned.1.call-update) | async-done | bytes 6963216 | tf_op jit(solution)/shard_map/all_gather | solution.py:122
  128.3 4.6 %fusion.2 = f32[1088]{0:T(1024)S(1)} fusion(bf16[1,1088,3200]{2,1,0:T(8,128)(2,1)} %all-gather.3.cloned.1.call-done), kind=kLoop, calls=%fused_computation.5 | loop fusion | flops 10443712 | bytes 6967552 | tf_op jit(solution)/shard_map/reduce_sum | solution.py:127
  133.3 9.5 %fusion.6 = f32[1088,768]{0,1:T(8,128)S(1)} fusion(bf16[3200,768]{1,0:T(8,128)(2,1)} %pad_maximum_fusion, bf16[1,1088,3200]{2,1,0:T(8,128)(2,1)S(1)} %copy-done, f32[3200]{0:T(1024)S(1)} %copy-done.7, f32[1088]{0:T(1024)S(1)} %add_rsqrt_fusion), kind=kOutput, calls=%fused_computation.10 | convolution fusion | flops 5361664000 | bytes 15237888 | tf_op jit(solution)/shard_map/dot_general | solution.py:129
  143.8 5.6 %all-to-all-start.3 = ((f32[8,2,1088]{2,1,0:T(2,128)}), f32[8,2,1088]{2,1,0:T(2,128)}, u32[]{:S(2)}, u32[]{:S(2)}) async-start(f32[8,2,1088]{2,1,0:T(2,128)} %broadcast_in_dim.96), calls=%async_computation.3 | async-start | bytes 147456 | tf_op jit(solution)/shard_map/all_to_all | solution.py:52
  150.3 5.9 %all-to-all-done.3 = f32[8,2,1088]{2,1,0:T(2,128)} async-done(((f32[8,2,1088]{2,1,0:T(2,128)}), f32[8,2,1088]{2,1,0:T(2,128)}, u32[]{:S(2)}, u32[]{:S(2)}) %all-to-all-start.3) | async-done | bytes 69664 | tf_op jit(solution)/shard_map/all_to_all | solution.py:52
  162.9 3.2 fusion.43
  166.2 4.9 %fusion.12 = bf16[2,1025,128]{2,1,0:T(8,128)(2,1)S(1)} fusion(bf16[2,1025,128]{2,1,0:T(8,128)(2,1)S(1)} %reshape_squeeze.11, f32[2,1025]{1,0:T(2,128)S(1)} %fusion.43, bf16[2,1025,128]{2,1,0:T(8,128)(2,1)S(1)} %reshape_squeeze.9, bf16[2,1025,128]{2,1,0:T(8,128)(2,1)S(1)} %reshape_squeeze.10), kind=kOutput, calls=%fused_computation.17 | convolution fusion | flops 1084510464 | bytes 2107400 | tf_op jit(solution)/shard_map/sqk,skc->sqc/dot_general | solution.py:168
  171.2 3.0 broadcast_in_dim.98
  174.2 5.7 %all-to-all-start.4 = ((bf16[16,1088,128]{2,1,0:T(8,128)(2,1)}), bf16[16,1088,128]{2,1,0:T(8,128)(2,1)}, u32[]{:S(2)}, u32[]{:S(2)}) async-start(bf16[16,1088,128]{2,1,0:T(8,128)(2,1)} %bitcast.97), calls=%async_computation.4 | async-start | bytes 8912896 | tf_op jit(solution)/shard_map/all_to_all | solution.py:181
  180.8 2.4 copy.118
  183.3 56.8 %all-to-all-done.4.heads_ref = bf16[16,1088,128]{2,1,0:T(8,128)(2,1)} async-done(((bf16[16,1088,128]{2,1,0:T(8,128)(2,1)}), bf16[16,1088,128]{2,1,0:T(8,128)(2,1)}, u32[]{:S(2)}, u32[]{:S(2)}) %all-to-all-start.4) | async-done | bytes 4456480 | tf_op jit(solution)/shard_map/all_to_all | solution.py:181
  240.1 8.2 %shard_map.82 = f32[1088,400]{1,0:T(8,128)} custom-call(bf16[16,1088,128]{2,1,0:T(8,128)(2,1)} %all-to-all-done.4.heads_ref, bf16[16,128,400]{2,1,0:T(8,128)(2,1)} %bitcast.99), custom_call_target="tpu_custom_call" | custom-call | tf_op jit(solution)/shard_map/pallas_call | solution.py:75
  248.3 2.7 fusion.13
  251.9 1.8 collective-permute-done.4
  256.6 4.9 %copy.124 = bf16[16,16,200,2,2]{1,0,4,3,2:T(8,128)(2,1)S(1)} copy(bf16[16,16,200,2,2]{2,4,1,3,0:T(2,128)(2,1)} %bitcast.112) | data formatting | bytes 819200 | tf_op jit(solution)/shard_map/transpose | solution.py:23
  261.5 3.9 stack_reshape.22
  265.4 2.1 reshape.276
  267.5 4.9 %copy.125 = bf16[16,16,200,2,2]{1,0,4,3,2:T(8,128)(2,1)S(1)} copy(bf16[16,16,200,2,2]{2,4,1,3,0:T(2,128)(2,1)} %bitcast.113) | data formatting | bytes 819200 | tf_op jit(solution)/shard_map/transpose | solution.py:23
  272.3 3.9 stack_reshape.23
  277.4 3.3 broadcast_select_fusion
  280.7 4.8 %all-to-all-start.5 = ((bf16[8,2,256,800]{2,3,1,0:T(8,128)(2,1)}), bf16[8,2,256,800]{2,3,1,0:T(8,128)(2,1)}, u32[]{:S(2)}, u32[]{:S(2)}) async-start(bf16[8,2,256,800]{2,3,1,0:T(8,128)(2,1)} %broadcast_select_fusion), calls=%async_computation.5 | async-start | bytes 13107200 | tf_op jit(solution)/shard_map/all_to_all | solution.py:205
  295.5 81.6 %all-to-all-done.5 = bf16[8,2,256,800]{2,3,1,0:T(8,128)(2,1)} async-done(((bf16[8,2,256,800]{2,3,1,0:T(8,128)(2,1)}), bf16[8,2,256,800]{2,3,1,0:T(8,128)(2,1)}, u32[]{:S(2)}, u32[]{:S(2)}) %all-to-all-start.5) | async-done | bytes 6553632 | tf_op jit(solution)/shard_map/all_to_all | solution.py:205
  377.2 4.0 %dynamic-slice_select_fusion.3 = (bf16[1,256,800]{1,2,0:T(8,128)(2,1)S(1)}, bf16[1,256,800]{1,2,0:T(8,128)(2,1)S(1)}, bf16[1,256,800]{1,2,0:T(8,128)(2,1)S(1)}, bf16[1,256,800]{1,2,0:T(8,128)(2,1)S(1)}) fusion(bf16[16,256,800]{1,2,0:T(8,128)(2,1)} %bitcast.33, s32[]{:T(128)S(6)} %select_n.180, pred[]{:T(512)} %get-tuple-element.44, s32[]{:T(128)S(6)} %select_n.192, ...), kind=kLoop, calls=%fused_computation.50 | loop fusion | flops 819200 | bytes 3276820 | tf_op jit(solution)/shard_map/jit(_where)/select_n | solution.py:46
  (86 shorter events, 28.7 us)
Async XLA Ops:
  6.5 20.7 %copy-start.3 = (bf16[400,384]{1,0:T(8,128)(2,1)S(1)}, bf16[400,384]{1,0:T(8,128)(2,1)}, u32[]{:S(2)}) copy-start(bf16[400,384]{1,0:T(8,128)(2,1)} %param.10) | copy-start | bytes 921604
  6.5 121.8 %all-gather.3.cloned.1.call-start = ((), (), s32[]{:S(2)}) async-start(), calls=%async_computation.6 | async-start | bytes 7833600 | tf_op jit(solution)/shard_map/all_gather | solution.py:122
  29.0 38.1 %all-to-all-start = ((bf16[8,400,384]{2,1,0:T(8,128)(2,1)}), bf16[8,400,384]{2,1,0:T(8,128)(2,1)S(1)}, u32[]{:S(2)}, u32[]{:S(2)}) async-start(bf16[8,400,384]{2,1,0:T(8,128)(2,1)} %broadcast_in_dim.94), calls=%async_computation | async-start | bytes 4915200 | tf_op jit(solution)/shard_map/all_to_all | solution.py:58
  34.1 57.7 %copy-start.6 = (f32[2,128]{1,0:T(2,128)S(1)}, f32[2,128]{1,0:T(2,128)}, u32[]{:S(2)}) copy-start(f32[2,128]{1,0:T(2,128)} %param.11) | copy-start | bytes 3076
  67.1 23.1 %all-to-all-start.2 = ((bf16[16,128,200]{1,2,0:T(8,128)(2,1)}), bf16[16,128,200]{1,2,0:T(8,128)(2,1)S(1)}, u32[]{:S(2)}, u32[]{:S(2)}) async-start(bf16[16,128,200]{1,2,0:T(8,128)(2,1)} %copy.106), calls=%async_computation.2 | async-start | bytes 1638400 | tf_op jit(solution)/shard_map/all_to_all | solution.py:110
  75.1 22.3 %collective-permute-start = (bf16[3200,384]{1,0:T(8,128)(2,1)S(1)}, bf16[3200,384]{1,0:T(8,128)(2,1)}, u32[]{:S(2)}, u32[]{:S(2)}) collective-permute-start(bf16[3200,384]{1,0:T(8,128)(2,1)S(1)} %bitcast.98), channel_id=1, source_target_pairs={{0,1},{1,0},{2,3},{3,2},{4,5},{5,4},{6,7},{7,6},{8,9},{9,8},{10,11... | collective-permute-start | bytes 7372808 | tf_op jit(solution)/shard_map/ppermute | solution.py:88
  91.1 3.5 collective-permute-start.1
  91.8 2.3 collective-permute-start.2
  128.3 5.0 %copy-start = (bf16[1,1088,3200]{2,1,0:T(8,128)(2,1)S(1)}, bf16[1,1088,3200]{2,1,0:T(8,128)(2,1)}, u32[]{:S(2)}) copy-start(bf16[1,1088,3200]{2,1,0:T(8,128)(2,1)} %all-gather.3.cloned.1.call-done) | copy-start | bytes 20889604
  128.3 5.0 %copy-start.7 = (f32[3200]{0:T(1024)S(1)}, f32[3200]{0:T(1024)}, u32[]{:S(2)}) copy-start(f32[3200]{0:T(1024)} %param.9) | copy-start | bytes 38404
  143.8 12.4 %all-to-all-start.3 = ((f32[8,2,1088]{2,1,0:T(2,128)}), f32[8,2,1088]{2,1,0:T(2,128)}, u32[]{:S(2)}, u32[]{:S(2)}) async-start(f32[8,2,1088]{2,1,0:T(2,128)} %broadcast_in_dim.96), calls=%async_computation.3 | async-start | bytes 147456 | tf_op jit(solution)/shard_map/all_to_all | solution.py:52
  157.1 1.1 copy-start.2
  159.4 2.6 collective-permute-start.3
  174.2 6.5 %copy-start.4 = (s32[8,2]{0,1:T(2,128)S(1)}, s32[8,2]{0,1:T(2,128)}, u32[]{:S(2)}) copy-start(s32[8,2]{0,1:T(2,128)} %param.14) | copy-start | bytes 196
  174.2 6.5 %copy-start.5 = (s32[8,2]{0,1:T(2,128)S(1)}, s32[8,2]{0,1:T(2,128)}, u32[]{:S(2)}) copy-start(s32[8,2]{0,1:T(2,128)} %param.15) | copy-start | bytes 196
  174.2 6.6 %copy-start.1 = (bf16[2048,400]{0,1:T(8,128)(2,1)S(1)}, bf16[2048,400]{0,1:T(8,128)(2,1)}, u32[]{:S(2)}) copy-start(bf16[2048,400]{0,1:T(8,128)(2,1)} %pad_maximum_fusion.3) | copy-start | bytes 4915204
  174.2 65.9 %all-to-all-start.4 = ((bf16[16,1088,128]{2,1,0:T(8,128)(2,1)}), bf16[16,1088,128]{2,1,0:T(8,128)(2,1)}, u32[]{:S(2)}, u32[]{:S(2)}) async-start(bf16[16,1088,128]{2,1,0:T(8,128)(2,1)} %bitcast.97), calls=%async_computation.4 | async-start | bytes 8912896 | tf_op jit(solution)/shard_map/all_to_all | solution.py:181
  251.5 2.1 collective-permute-start.4
  280.7 96.5 %all-to-all-start.5 = ((bf16[8,2,256,800]{2,3,1,0:T(8,128)(2,1)}), bf16[8,2,256,800]{2,3,1,0:T(8,128)(2,1)}, u32[]{:S(2)}, u32[]{:S(2)}) async-start(bf16[8,2,256,800]{2,3,1,0:T(8,128)(2,1)} %broadcast_select_fusion), calls=%async_computation.5 | async-start | bytes 13107200 | tf_op jit(solution)/shard_map/all_to_all | solution.py:205
Sparse Core Ops, SparseCore 0:
  9.7 118.6 all-gather.2

commit v14 on v13

--- a/solution.py
+++ b/solution.py
@@ -59,15 +59,16 @@
     return collected.reshape((groups * block_value.shape[0],) + block_value.shape[1:])
 
 
-def head_sum_kernel(heads_ref, weight_ref, out_ref):
+def head_sum_kernel(heads_ref, weight_ref, tokens_ref, scale_ref, out_ref):
     total = jnp.zeros(out_ref.shape, jnp.float32)
     for head in range(heads_ref.shape[0]):
         term = jnp.dot(heads_ref[head], weight_ref[head], preferred_element_type=jnp.float32)
         total = total + term.astype(jnp.bfloat16).astype(jnp.float32)
-    out_ref[...] = total
-
-
-def head_sum(heads, weight):
+    updated = tokens_ref[...].astype(jnp.float32) + scale_ref[...] * total
+    out_ref[...] = updated.astype(out_ref.dtype)
+
+
+def head_sum(heads, weight, tokens, scale):
     count, rows, width = heads.shape
     columns = weight.shape[2]
     steps = 4
@@ -78,10 +79,12 @@
         in_specs=[
             pl.BlockSpec((count, tile, width), lambda i: (0, i, 0)),
             pl.BlockSpec((count, width, columns), lambda i: (0, 0, 0)),
+            pl.BlockSpec((tile, columns), lambda i: (i, 0)),
+            pl.BlockSpec((1, columns), lambda i: (0, 0)),
         ],
         out_specs=pl.BlockSpec((tile, columns), lambda i: (i, 0)),
-        out_shape=jax.ShapeDtypeStruct((rows, columns), jnp.float32),
-    )(heads, weight)
+        out_shape=jax.ShapeDtypeStruct((rows, columns), tokens.dtype),
+    )(heads, weight, tokens, scale.reshape(1, columns))
 
 
 def pair_up(value, core, swap, axis):
@@ -185,10 +188,11 @@
         concat_axis=0,
         tiled=True,
     )
-    attention = head_sum(all_heads, pair_weight.reshape(groups, HEAD_DIM, cores * block))
     pair_tokens = lax.dynamic_slice_in_dim(half, chip * cores * block, cores * block, axis=1)
     pair_scale = lax.dynamic_slice_in_dim(layer_scale, chip * cores * block, cores * block)
-    updated_half = (pair_tokens.astype(jnp.float32) + pair_scale * attention).astype(jnp.bfloat16)
+    updated_half = head_sum(
+        all_heads, pair_weight.reshape(groups, HEAD_DIM, cores * block), pair_tokens, pair_scale
+    )
     keep = lax.dynamic_slice_in_dim(updated_half, core * block, block, axis=1)
     give = lax.dynamic_slice_in_dim(updated_half, (1 - core) * block, block, axis=1)
     taken = lax.ppermute(give, "core", swap)

time: 391 us -> 389 us (level)
  local copies, waits for them, and re-layouts: 40.8 us -> 45.4 us
  transfers between devices with their start and end apart: 11 -> 11, of which waited for: 9 -> 9; matrix products, arithmetic and copies ran while one was open for 6% -> 7% of each run, Pallas kernels for 0% -> 0%
where the time goes in v14:
time: 389 us; the launch traced here: 388 us
  waiting for transfers between devices  219 us (56%)
  local copies, waits for them, and re-layouts  45.4 us (12%)
  starting transfers between devices  29 us (7%)
  other arithmetic  28.2 us (7%)
  between operations  21.4 us (6%)
  blocking collectives  19 us (5%)
  matrix products  17.6 us (5%)
  Pallas kernels  8.24 us (2%)
    all_to_all x1, waiting for transfers between devices, body(): lax.all_to_all(outgoing, 'fsdp', split_axis=0, concat_axis=0, tiled=True)  81.6 us
    all_to_all x1, waiting for transfers between devices, body(): lax.all_to_all(outgoing.reshape(groups, half_length, HEAD_DIM), ('chip',...  53.4 us
    all_to_all x1, waiting for transfers between devices, gather_blocks(): lax.all_to_all(spread, axis_name, split_axis=0, concat_axis=0, tiled=True)  30.7 us
    all_gather x1, waiting for transfers between devices, body(): half = lax.all_gather(own_rows, 'chip', axis=0, tiled=True)  26.1 us
    all_to_all x1, blocking collectives, body(): lax.all_to_all(spread, 'fsdp', split_axis=0, concat_axis=0, tiled=True)  19 us
    all_to_all x1, waiting for transfers between devices, body(): lax.all_to_all(head_rows.reshape(groups, HEAD_DIM, block), ('chip', 'core...  15 us
    transpose x2, local copies, waits for them, and re-layouts, merge_tiles(): patches.reshape(halves, 2, halves, 2, columns).transpose(0, 2, 4, 1, 3)  9.74 us
    dot_general x1, matrix products, body(): projected = jnp.dot(normed, pair_qkv, preferred_element_type=jnp.float32)  9.55 us
  transfers between devices with their start and end apart: 11, of which 9 were waited for; matrix products, arithmetic and copies ran while one was open for 7% of the time, Pallas kernels for 0%

profile of v14, /device:TPU:8, one launch (start us, length us, event | category | flops | bytes accessed | tf_op | source)
XLA Modules:
  0.0 387.9 jit_solution(13922000971826123566)
XLA Ops:
  8.3 19.0 %all_to_all.30 = bf16[8,128,400]{1,2,0:T(8,128)(2,1)S(1)} all-to-all(bf16[8,128,400]{1,2,0:T(8,128)(2,1)S(1)} %broadcast_in_dim.94), channel_id=1, replica_groups=mesh['fsdp'=8,'chip'=8,'core'=2] {'fsdp'}, dimensions={0} | all-to-all | bytes 1638400 | tf_op jit(solution)/shard_map/all_to_all | solution.py:110
  29.0 3.6 all-to-all-start
  34.1 2.3 copy.106
  36.4 30.7 %all-to-all-done = bf16[8,400,384]{2,1,0:T(8,128)(2,1)S(1)} async-done(((bf16[8,400,384]{2,1,0:T(8,128)(2,1)}), bf16[8,400,384]{2,1,0:T(8,128)(2,1)S(1)}, u32[]{:S(2)}, u32[]{:S(2)}) %all-to-all-start) | async-done | bytes 2457632 | tf_op jit(solution)/shard_map/all_to_all | solution.py:58
  67.1 8.0 %all-to-all-start.2 = ((bf16[16,128,200]{1,2,0:T(8,128)(2,1)}), bf16[16,128,200]{1,2,0:T(8,128)(2,1)S(1)}, u32[]{:S(2)}, u32[]{:S(2)}) async-start(bf16[16,128,200]{1,2,0:T(8,128)(2,1)} %copy.106), calls=%async_computation.2 | async-start | bytes 1638400 | tf_op jit(solution)/shard_map/all_to_all | solution.py:113
  75.2 15.0 %all-to-all-done.2 = bf16[16,128,200]{1,2,0:T(8,128)(2,1)S(1)} async-done(((bf16[16,128,200]{1,2,0:T(8,128)(2,1)}), bf16[16,128,200]{1,2,0:T(8,128)(2,1)S(1)}, u32[]{:S(2)}, u32[]{:S(2)}) %all-to-all-start.2) | async-done | bytes 819232 | tf_op jit(solution)/shard_map/all_to_all | solution.py:113
  91.8 2.3 collective-permute-done.2
  97.4 2.1 broadcast_select_fusion.2
  99.6 2.7 pad_maximum_fusion
  102.2 26.1 %all-gather.3.cloned.1.call-done = bf16[1,1088,3200]{2,1,0:T(8,128)(2,1)} async-done(((bf16[1,136,3200]{2,1,0:T(8,128)(2,1)}), bf16[1,1088,3200]{2,1,0:T(8,128)(2,1)}) %all-gather.3.cloned.1.call-update) | async-done | bytes 6963216 | tf_op jit(solution)/shard_map/all_gather | solution.py:125
  128.3 4.6 %fusion.2 = f32[1088]{0:T(1024)S(1)} fusion(bf16[1,1088,3200]{2,1,0:T(8,128)(2,1)} %all-gather.3.cloned.1.call-done), kind=kLoop, calls=%fused_computation.5 | loop fusion | flops 10443712 | bytes 6967552 | tf_op jit(solution)/shard_map/reduce_sum | solution.py:130
  133.3 9.5 %fusion.6 = f32[1088,768]{0,1:T(8,128)S(1)} fusion(bf16[3200,768]{1,0:T(8,128)(2,1)} %pad_maximum_fusion, bf16[1,1088,3200]{2,1,0:T(8,128)(2,1)S(1)} %copy-done, f32[3200]{0:T(1024)S(1)} %copy-done.8, f32[1088]{0:T(1024)S(1)} %add_rsqrt_fusion), kind=kOutput, calls=%fused_computation.10 | convolution fusion | flops 5361664000 | bytes 15237888 | tf_op jit(solution)/shard_map/dot_general | solution.py:132
  143.8 5.6 %all-to-all-start.3 = ((f32[8,2,1088]{2,1,0:T(2,128)}), f32[8,2,1088]{2,1,0:T(2,128)}, u32[]{:S(2)}, u32[]{:S(2)}) async-start(f32[8,2,1088]{2,1,0:T(2,128)} %broadcast_in_dim.95), calls=%async_computation.3 | async-start | bytes 147456 | tf_op jit(solution)/shard_map/all_to_all | solution.py:52
  150.3 5.9 %all-to-all-done.3 = f32[8,2,1088]{2,1,0:T(2,128)} async-done(((f32[8,2,1088]{2,1,0:T(2,128)}), f32[8,2,1088]{2,1,0:T(2,128)}, u32[]{:S(2)}, u32[]{:S(2)}) %all-to-all-start.3) | async-done | bytes 69664 | tf_op jit(solution)/shard_map/all_to_all | solution.py:52
  162.9 3.2 fusion.42
  166.2 4.9 %fusion.12 = bf16[2,1025,128]{2,1,0:T(8,128)(2,1)S(1)} fusion(bf16[2,1025,128]{2,1,0:T(8,128)(2,1)S(1)} %reshape_squeeze.11, f32[2,1025]{1,0:T(2,128)S(1)} %fusion.42, bf16[2,1025,128]{2,1,0:T(8,128)(2,1)S(1)} %reshape_squeeze.9, bf16[2,1025,128]{2,1,0:T(8,128)(2,1)S(1)} %reshape_squeeze.10), kind=kOutput, calls=%fused_computation.17 | convolution fusion | flops 1084510464 | bytes 2107400 | tf_op jit(solution)/shard_map/sqk,skc->sqc/dot_general | solution.py:171
  171.2 3.0 broadcast_in_dim.97
  174.2 5.7 %all-to-all-start.4 = ((bf16[16,1088,128]{2,1,0:T(8,128)(2,1)}), bf16[16,1088,128]{2,1,0:T(8,128)(2,1)}, u32[]{:S(2)}, u32[]{:S(2)}) async-start(bf16[16,1088,128]{2,1,0:T(8,128)(2,1)} %bitcast.97), calls=%async_computation.4 | async-start | bytes 8912896 | tf_op jit(solution)/shard_map/all_to_all | solution.py:184
  181.4 2.4 copy.118
  183.8 2.8 dynamic-slice_bitcast_fusion.tokens_ref
  186.7 53.4 %all-to-all-done.4.heads_ref = bf16[16,1088,128]{2,1,0:T(8,128)(2,1)} async-done(((bf16[16,1088,128]{2,1,0:T(8,128)(2,1)}), bf16[16,1088,128]{2,1,0:T(8,128)(2,1)}, u32[]{:S(2)}, u32[]{:S(2)}) %all-to-all-start.4) | async-done | bytes 4456480 | tf_op jit(solution)/shard_map/all_to_all | solution.py:184
  240.1 8.2 %shard_map.82 = bf16[1088,400]{1,0:T(8,128)(2,1)} custom-call(bf16[16,1088,128]{2,1,0:T(8,128)(2,1)} %all-to-all-done.4.heads_ref, bf16[16,128,400]{2,1,0:T(8,128)(2,1)} %bitcast.99, bf16[1088,400]{1,0:T(8,128)(2,1)} %dynamic-slice_bitcast_fusion.tokens_ref, f32[1,400]{1,0:T(1,128)} %bitcast.115), custom_call_target="tpu_custom_call" | custom-call | tf_op jit(solution)/shard_map/pallas_call | solution.py:76
  250.4 1.8 collective-permute-done.4
  255.2 4.9 %copy.124 = bf16[16,16,200,2,2]{1,0,4,3,2:T(8,128)(2,1)S(1)} copy(bf16[16,16,200,2,2]{2,4,1,3,0:T(2,128)(2,1)} %bitcast.112) | data formatting | bytes 819200 | tf_op jit(solution)/shard_map/transpose | solution.py:23
  260.1 3.9 stack_reshape.22
  263.9 2.1 reshape.279
  266.0 4.9 %copy.125 = bf16[16,16,200,2,2]{1,0,4,3,2:T(8,128)(2,1)S(1)} copy(bf16[16,16,200,2,2]{2,4,1,3,0:T(2,128)(2,1)} %bitcast.113) | data formatting | bytes 819200 | tf_op jit(solution)/shard_map/transpose | solution.py:23
  270.9 3.9 stack_reshape.23
  275.9 3.3 broadcast_select_fusion
  279.3 4.8 %all-to-all-start.5 = ((bf16[8,2,256,800]{2,3,1,0:T(8,128)(2,1)}), bf16[8,2,256,800]{2,3,1,0:T(8,128)(2,1)}, u32[]{:S(2)}, u32[]{:S(2)}) async-start(bf16[8,2,256,800]{2,3,1,0:T(8,128)(2,1)} %broadcast_select_fusion), calls=%async_computation.5 | async-start | bytes 13107200 | tf_op jit(solution)/shard_map/all_to_all | solution.py:209
  294.1 81.6 %all-to-all-done.5 = bf16[8,2,256,800]{2,3,1,0:T(8,128)(2,1)} async-done(((bf16[8,2,256,800]{2,3,1,0:T(8,128)(2,1)}), bf16[8,2,256,800]{2,3,1,0:T(8,128)(2,1)}, u32[]{:S(2)}, u32[]{:S(2)}) %all-to-all-start.5) | async-done | bytes 6553632 | tf_op jit(solution)/shard_map/all_to_all | solution.py:209
  375.7 3.9 %dynamic-slice_select_fusion.3 = (bf16[1,256,800]{1,2,0:T(8,128)(2,1)S(1)}, bf16[1,256,800]{1,2,0:T(8,128)(2,1)S(1)}, bf16[1,256,800]{1,2,0:T(8,128)(2,1)S(1)}, bf16[1,256,800]{1,2,0:T(8,128)(2,1)S(1)}) fusion(bf16[16,256,800]{1,2,0:T(8,128)(2,1)} %bitcast.34, s32[]{:T(128)S(6)} %select_n.180, pred[]{:T(512)} %get-tuple-element.44, s32[]{:T(128)S(6)} %select_n.192, ...), kind=kLoop, calls=%fused_computation.49 | loop fusion | flops 819200 | bytes 3276820 | tf_op jit(solution)/shard_map/jit(_where)/select_n | solution.py:46
  (88 shorter events, 30.5 us)
Async XLA Ops:
  6.5 20.7 %copy-start.4 = (bf16[400,384]{1,0:T(8,128)(2,1)S(1)}, bf16[400,384]{1,0:T(8,128)(2,1)}, u32[]{:S(2)}) copy-start(bf16[400,384]{1,0:T(8,128)(2,1)} %param.10) | copy-start | bytes 921604
  6.5 121.8 %all-gather.3.cloned.1.call-start = ((), (), s32[]{:S(2)}) async-start(), calls=%async_computation.6 | async-start | bytes 7833600 | tf_op jit(solution)/shard_map/all_gather | solution.py:125
  29.0 38.1 %all-to-all-start = ((bf16[8,400,384]{2,1,0:T(8,128)(2,1)}), bf16[8,400,384]{2,1,0:T(8,128)(2,1)S(1)}, u32[]{:S(2)}, u32[]{:S(2)}) async-start(bf16[8,400,384]{2,1,0:T(8,128)(2,1)} %broadcast_in_dim.93), calls=%async_computation | async-start | bytes 4915200 | tf_op jit(solution)/shard_map/all_to_all | solution.py:58
  34.1 57.7 %copy-start.7 = (f32[2,128]{1,0:T(2,128)S(1)}, f32[2,128]{1,0:T(2,128)}, u32[]{:S(2)}) copy-start(f32[2,128]{1,0:T(2,128)} %param.11) | copy-start | bytes 3076
  67.1 23.1 %all-to-all-start.2 = ((bf16[16,128,200]{1,2,0:T(8,128)(2,1)}), bf16[16,128,200]{1,2,0:T(8,128)(2,1)S(1)}, u32[]{:S(2)}, u32[]{:S(2)}) async-start(bf16[16,128,200]{1,2,0:T(8,128)(2,1)} %copy.106), calls=%async_computation.2 | async-start | bytes 1638400 | tf_op jit(solution)/shard_map/all_to_all | solution.py:113
  75.1 22.3 %collective-permute-start = (bf16[3200,384]{1,0:T(8,128)(2,1)S(1)}, bf16[3200,384]{1,0:T(8,128)(2,1)}, u32[]{:S(2)}, u32[]{:S(2)}) collective-permute-start(bf16[3200,384]{1,0:T(8,128)(2,1)S(1)} %bitcast.98), channel_id=1, source_target_pairs={{0,1},{1,0},{2,3},{3,2},{4,5},{5,4},{6,7},{7,6},{8,9},{9,8},{10,11... | collective-permute-start | bytes 7372808 | tf_op jit(solution)/shard_map/ppermute | solution.py:91
  91.1 3.5 collective-permute-start.1
  91.8 2.3 collective-permute-start.2
  128.3 5.0 %copy-start = (bf16[1,1088,3200]{2,1,0:T(8,128)(2,1)S(1)}, bf16[1,1088,3200]{2,1,0:T(8,128)(2,1)}, u32[]{:S(2)}) copy-start(bf16[1,1088,3200]{2,1,0:T(8,128)(2,1)} %all-gather.3.cloned.1.call-done) | copy-start | bytes 20889604
  128.3 5.0 %copy-start.8 = (f32[3200]{0:T(1024)S(1)}, f32[3200]{0:T(1024)}, u32[]{:S(2)}) copy-start(f32[3200]{0:T(1024)} %param.9) | copy-start | bytes 38404
  143.8 12.4 %all-to-all-start.3 = ((f32[8,2,1088]{2,1,0:T(2,128)}), f32[8,2,1088]{2,1,0:T(2,128)}, u32[]{:S(2)}, u32[]{:S(2)}) async-start(f32[8,2,1088]{2,1,0:T(2,128)} %broadcast_in_dim.95), calls=%async_computation.3 | async-start | bytes 147456 | tf_op jit(solution)/shard_map/all_to_all | solution.py:52
  157.1 1.1 copy-start.3
  159.4 2.6 collective-permute-start.3
  174.2 7.0 %copy-start.5 = (s32[8,2]{0,1:T(2,128)S(1)}, s32[8,2]{0,1:T(2,128)}, u32[]{:S(2)}) copy-start(s32[8,2]{0,1:T(2,128)} %param.14) | copy-start | bytes 196
  174.2 7.0 %copy-start.6 = (s32[8,2]{0,1:T(2,128)S(1)}, s32[8,2]{0,1:T(2,128)}, u32[]{:S(2)}) copy-start(s32[8,2]{0,1:T(2,128)} %param.15) | copy-start | bytes 196
  174.2 7.2 %copy-start.1 = (bf16[2048,400]{0,1:T(8,128)(2,1)S(1)}, bf16[2048,400]{0,1:T(8,128)(2,1)}, u32[]{:S(2)}) copy-start(bf16[2048,400]{0,1:T(8,128)(2,1)} %pad_maximum_fusion.3) | copy-start | bytes 4915204
  174.2 65.9 %all-to-all-start.4 = ((bf16[16,1088,128]{2,1,0:T(8,128)(2,1)}), bf16[16,1088,128]{2,1,0:T(8,128)(2,1)}, u32[]{:S(2)}, u32[]{:S(2)}) async-start(bf16[16,1088,128]{2,1,0:T(8,128)(2,1)} %bitcast.97), calls=%async_computation.4 | async-start | bytes 8912896 | tf_op jit(solution)/shard_map/all_to_all | solution.py:184
  248.3 4.1 %copy-start.2 = (bf16[1088,400]{1,0:T(8,128)(2,1)S(1)}, bf16[1088,400]{1,0:T(8,128)(2,1)}, u32[]{:S(2)}) copy-start(bf16[1088,400]{1,0:T(8,128)(2,1)} %shard_map.82) | copy-start | bytes 2611204
  250.1 2.1 collective-permute-start.4
  279.3 96.5 %all-to-all-start.5 = ((bf16[8,2,256,800]{2,3,1,0:T(8,128)(2,1)}), bf16[8,2,256,800]{2,3,1,0:T(8,128)(2,1)}, u32[]{:S(2)}, u32[]{:S(2)}) async-start(bf16[8,2,256,800]{2,3,1,0:T(8,128)(2,1)} %broadcast_select_fusion), calls=%async_computation.5 | async-start | bytes 13107200 | tf_op jit(solution)/shard_map/all_to_all | solution.py:209
Sparse Core Ops, SparseCore 0:
  9.7 118.6 all-gather.2

commit v15 on v14

--- a/solution.py
+++ b/solution.py
@@ -199,7 +199,10 @@
     first_half = jnp.where(core == 0, keep, taken).reshape(chips, piece, block)
     second_half = jnp.where(core == 0, taken, keep).reshape(chips, piece, block)
     updated = jnp.stack([first_half, second_half], axis=1).reshape(length, block)
-    merged = merge_tiles(updated)
+    patches = jnp.stack([updated[slot * TILE + 1 : (slot + 1) * TILE] for slot in range(SLOTS)])
+    halves = GRID // 2
+    square = patches.reshape(SLOTS, halves, 2, halves, 2, block).transpose(0, 1, 3, 5, 2, 4)
+    merged = square.reshape(SLOTS, halves * halves, block * 4)
     holder, living = tile_owners(tile_counts, owners)
     own_holder = holder[row_index]
     own_living = living[row_index]

time: 389 us -> 384 us (0.987)
  local copies, waits for them, and re-layouts: 45.4 us -> 39.8 us
    broadcast_in_dim x0 -> x1, local copies, waits for them, and re-layouts: none -> 8.1 us  [body(): jnp.where(sending[:, :, None, None], merged[None], jnp.zeros((), jnp.bflo...]
    another operation x2, local copies, waits for them, and re-layouts: 7.71 us -> 0.52 us  [body(): jnp.stack([updated[slot * TILE + 1:(slot + 1) * TILE] for slot in range(S...]
    transpose x2 -> x1, local copies, waits for them, and re-layouts: 9.74 us -> 7.13 us  [body(): patches.reshape(SLOTS, halves, 2, halves, 2, block)]
where the time goes in v15:
time: 384 us; the launch traced here: 383 us
  waiting for transfers between devices  219 us (57%)
  local copies, waits for them, and re-layouts  39.8 us (10%)
  starting transfers between devices  29 us (8%)
  other arithmetic  28.7 us (7%)
  between operations  21.4 us (6%)
  blocking collectives  19 us (5%)
  matrix products  17.6 us (5%)
  Pallas kernels  8.24 us (2%)
    all_to_all x1, waiting for transfers between devices, body(): lax.all_to_all(outgoing, 'fsdp', split_axis=0, concat_axis=0, tiled=True)  81.6 us
    all_to_all x1, waiting for transfers between devices, body(): lax.all_to_all(outgoing.reshape(groups, half_length, HEAD_DIM), ('chip',...  53.4 us
    all_to_all x1, waiting for transfers between devices, gather_blocks(): lax.all_to_all(spread, axis_name, split_axis=0, concat_axis=0, tiled=True)  30.7 us
    all_gather x1, waiting for transfers between devices, body(): half = lax.all_gather(own_rows, 'chip', axis=0, tiled=True)  26.1 us
    all_to_all x1, blocking collectives, body(): lax.all_to_all(spread, 'fsdp', split_axis=0, concat_axis=0, tiled=True)  19 us
    all_to_all x1, waiting for transfers between devices, body(): lax.all_to_all(head_rows.reshape(groups, HEAD_DIM, block), ('chip', 'core...  15 us
    dot_general x1, matrix products, body(): projected = jnp.dot(normed, pair_qkv, preferred_element_type=jnp.float32)  9.55 us
    pallas_call x1, Pallas kernels, head_sum(): pl.pallas_call(head_sum_kernel, grid=(steps,), in_specs=[pl.BlockSpec((co...  8.24 us
  transfers between devices with their start and end apart: 11, of which 9 were waited for; matrix products, arithmetic and copies ran while one was open for 7% of the time, Pallas kernels for 0%

profile of v15, /device:TPU:8, one launch (start us, length us, event | category | flops | bytes accessed | tf_op | source)
XLA Modules:
  0.0 382.7 jit_solution(13217679286463460724)
XLA Ops:
  8.3 19.0 %all_to_all.30 = bf16[8,128,400]{1,2,0:T(8,128)(2,1)S(1)} all-to-all(bf16[8,128,400]{1,2,0:T(8,128)(2,1)S(1)} %broadcast_in_dim.95), channel_id=1, replica_groups=mesh['fsdp'=8,'chip'=8,'core'=2] {'fsdp'}, dimensions={0} | all-to-all | bytes 1638400 | tf_op jit(solution)/shard_map/all_to_all | solution.py:110
  27.3 1.7 broadcast_in_dim.94
  29.0 3.6 all-to-all-start
  34.1 2.3 copy.101
  36.4 30.7 %all-to-all-done = bf16[8,400,384]{2,1,0:T(8,128)(2,1)S(1)} async-done(((bf16[8,400,384]{2,1,0:T(8,128)(2,1)}), bf16[8,400,384]{2,1,0:T(8,128)(2,1)S(1)}, u32[]{:S(2)}, u32[]{:S(2)}) %all-to-all-start) | async-done | bytes 2457632 | tf_op jit(solution)/shard_map/all_to_all | solution.py:58
  67.1 8.0 %all-to-all-start.2 = ((bf16[16,128,200]{1,2,0:T(8,128)(2,1)}), bf16[16,128,200]{1,2,0:T(8,128)(2,1)S(1)}, u32[]{:S(2)}, u32[]{:S(2)}) async-start(bf16[16,128,200]{1,2,0:T(8,128)(2,1)} %copy.101), calls=%async_computation.2 | async-start | bytes 1638400 | tf_op jit(solution)/shard_map/all_to_all | solution.py:113
  75.2 15.0 %all-to-all-done.2 = bf16[16,128,200]{1,2,0:T(8,128)(2,1)S(1)} async-done(((bf16[16,128,200]{1,2,0:T(8,128)(2,1)}), bf16[16,128,200]{1,2,0:T(8,128)(2,1)S(1)}, u32[]{:S(2)}, u32[]{:S(2)}) %all-to-all-start.2) | async-done | bytes 819232 | tf_op jit(solution)/shard_map/all_to_all | solution.py:113
  91.8 2.3 collective-permute-done.2
  97.4 2.1 broadcast_select_fusion.2
  99.6 2.7 pad_maximum_fusion
  102.2 26.1 %all-gather.3.cloned.1.call-done = bf16[1,1088,3200]{2,1,0:T(8,128)(2,1)} async-done(((bf16[1,136,3200]{2,1,0:T(8,128)(2,1)}), bf16[1,1088,3200]{2,1,0:T(8,128)(2,1)}) %all-gather.3.cloned.1.call-update) | async-done | bytes 6963216 | tf_op jit(solution)/shard_map/all_gather | solution.py:125
  128.3 4.6 %fusion.2 = f32[1088]{0:T(1024)S(1)} fusion(bf16[1,1088,3200]{2,1,0:T(8,128)(2,1)} %all-gather.3.cloned.1.call-done), kind=kLoop, calls=%fused_computation.5 | loop fusion | flops 10443712 | bytes 6967552 | tf_op jit(solution)/shard_map/reduce_sum | solution.py:130
  133.3 9.5 %fusion.6 = f32[1088,768]{0,1:T(8,128)S(1)} fusion(bf16[3200,768]{1,0:T(8,128)(2,1)} %pad_maximum_fusion, bf16[1,1088,3200]{2,1,0:T(8,128)(2,1)S(1)} %copy-done, f32[3200]{0:T(1024)S(1)} %copy-done.8, f32[1088]{0:T(1024)S(1)} %add_rsqrt_fusion), kind=kOutput, calls=%fused_computation.10 | convolution fusion | flops 5361664000 | bytes 15237888 | tf_op jit(solution)/shard_map/dot_general | solution.py:132
  143.8 5.6 %all-to-all-start.3 = ((f32[8,2,1088]{2,1,0:T(2,128)}), f32[8,2,1088]{2,1,0:T(2,128)}, u32[]{:S(2)}, u32[]{:S(2)}) async-start(f32[8,2,1088]{2,1,0:T(2,128)} %broadcast_in_dim.96), calls=%async_computation.3 | async-start | bytes 147456 | tf_op jit(solution)/shard_map/all_to_all | solution.py:52
  150.3 5.9 %all-to-all-done.3 = f32[8,2,1088]{2,1,0:T(2,128)} async-done(((f32[8,2,1088]{2,1,0:T(2,128)}), f32[8,2,1088]{2,1,0:T(2,128)}, u32[]{:S(2)}, u32[]{:S(2)}) %all-to-all-start.3) | async-done | bytes 69664 | tf_op jit(solution)/shard_map/all_to_all | solution.py:52
  162.9 3.2 fusion.42
  166.2 4.9 %fusion.12 = bf16[2,1025,128]{2,1,0:T(8,128)(2,1)S(1)} fusion(bf16[2,1025,128]{2,1,0:T(8,128)(2,1)S(1)} %reshape_squeeze.11, f32[2,1025]{1,0:T(2,128)S(1)} %fusion.42, bf16[2,1025,128]{2,1,0:T(8,128)(2,1)S(1)} %reshape_squeeze.9, bf16[2,1025,128]{2,1,0:T(8,128)(2,1)S(1)} %reshape_squeeze.10), kind=kOutput, calls=%fused_computation.17 | convolution fusion | flops 1084510464 | bytes 2107400 | tf_op jit(solution)/shard_map/sqk,skc->sqc/dot_general | solution.py:171
  171.2 3.0 broadcast_in_dim.98
  174.2 5.7 %all-to-all-start.4 = ((bf16[16,1088,128]{2,1,0:T(8,128)(2,1)}), bf16[16,1088,128]{2,1,0:T(8,128)(2,1)}, u32[]{:S(2)}, u32[]{:S(2)}) async-start(bf16[16,1088,128]{2,1,0:T(8,128)(2,1)} %bitcast.93), calls=%async_computation.4 | async-start | bytes 8912896 | tf_op jit(solution)/shard_map/all_to_all | solution.py:184
  181.4 2.4 copy.113
  183.8 2.8 dynamic-slice_bitcast_fusion.tokens_ref
  186.7 53.4 %all-to-all-done.4.heads_ref = bf16[16,1088,128]{2,1,0:T(8,128)(2,1)} async-done(((bf16[16,1088,128]{2,1,0:T(8,128)(2,1)}), bf16[16,1088,128]{2,1,0:T(8,128)(2,1)}, u32[]{:S(2)}, u32[]{:S(2)}) %all-to-all-start.4) | async-done | bytes 4456480 | tf_op jit(solution)/shard_map/all_to_all | solution.py:184
  240.1 8.2 %shard_map.82 = bf16[1088,400]{1,0:T(8,128)(2,1)} custom-call(bf16[16,1088,128]{2,1,0:T(8,128)(2,1)} %all-to-all-done.4.heads_ref, bf16[16,128,400]{2,1,0:T(8,128)(2,1)} %bitcast.95, bf16[1088,400]{1,0:T(8,128)(2,1)} %dynamic-slice_bitcast_fusion.tokens_ref, f32[1,400]{1,0:T(1,128)} %bitcast.109), custom_call_target="tpu_custom_call" | custom-call | tf_op jit(solution)/shard_map/pallas_call | solution.py:76
  248.3 1.5 constant_dynamic-slice_fusion
  250.4 1.8 collective-permute-done.4
  253.8 1.7 maximum_bitcast_fusion
  255.5 7.1 %copy.119 = bf16[2,16,16,200,2,2]{2,1,5,4,3,0:T(8,128)(2,1)} copy(bf16[2,16,16,200,2,2]{3,5,2,4,1,0:T(2,128)(2,1)S(1)} %maximum_bitcast_fusion) | data formatting | bytes 1638400 | tf_op jit(solution)/shard_map/transpose | solution.py:204
  262.6 8.1 %broadcast_in_dim.99 = bf16[2,256,800]{1,2,0:T(8,128)(2,1)S(1)} reshape(bf16[2,16,16,200,2,2]{2,1,5,4,3,0:T(8,128)(2,1)} %copy.119) | data formatting | bytes 1638400 | tf_op jit(solution)/shard_map/jit(_where)/broadcast_in_dim | solution.py:211
  270.8 3.3 broadcast_select_fusion
  274.1 4.8 %all-to-all-start.5 = ((bf16[8,2,256,800]{2,3,1,0:T(8,128)(2,1)}), bf16[8,2,256,800]{2,3,1,0:T(8,128)(2,1)}, u32[]{:S(2)}, u32[]{:S(2)}) async-start(bf16[8,2,256,800]{2,3,1,0:T(8,128)(2,1)} %broadcast_select_fusion), calls=%async_computation.5 | async-start | bytes 13107200 | tf_op jit(solution)/shard_map/all_to_all | solution.py:212
  288.9 81.6 %all-to-all-done.5 = bf16[8,2,256,800]{2,3,1,0:T(8,128)(2,1)} async-done(((bf16[8,2,256,800]{2,3,1,0:T(8,128)(2,1)}), bf16[8,2,256,800]{2,3,1,0:T(8,128)(2,1)}, u32[]{:S(2)}, u32[]{:S(2)}) %all-to-all-start.5) | async-done | bytes 6553632 | tf_op jit(solution)/shard_map/all_to_all | solution.py:212
  370.5 3.9 %dynamic-slice_select_fusion.3 = (bf16[1,256,800]{1,2,0:T(8,128)(2,1)S(1)}, bf16[1,256,800]{1,2,0:T(8,128)(2,1)S(1)}, bf16[1,256,800]{1,2,0:T(8,128)(2,1)S(1)}, bf16[1,256,800]{1,2,0:T(8,128)(2,1)S(1)}) fusion(bf16[16,256,800]{1,2,0:T(8,128)(2,1)} %bitcast.33, s32[]{:T(128)S(6)} %select_n.180, pred[]{:T(512)} %get-tuple-element.44, s32[]{:T(128)S(6)} %select_n.192, ...), kind=kLoop, calls=%fused_computation.49 | loop fusion | flops 819200 | bytes 3276820 | tf_op jit(solution)/shard_map/jit(_where)/select_n | solution.py:46
  (86 shorter events, 24.7 us)
Async XLA Ops:
  6.5 20.7 %copy-start.4 = (bf16[400,384]{1,0:T(8,128)(2,1)S(1)}, bf16[400,384]{1,0:T(8,128)(2,1)}, u32[]{:S(2)}) copy-start(bf16[400,384]{1,0:T(8,128)(2,1)} %param.10) | copy-start | bytes 921604
  6.5 121.8 %all-gather.3.cloned.1.call-start = ((), (), s32[]{:S(2)}) async-start(), calls=%async_computation.6 | async-start | bytes 7833600 | tf_op jit(solution)/shard_map/all_gather | solution.py:125
  29.0 38.1 %all-to-all-start = ((bf16[8,400,384]{2,1,0:T(8,128)(2,1)}), bf16[8,400,384]{2,1,0:T(8,128)(2,1)S(1)}, u32[]{:S(2)}, u32[]{:S(2)}) async-start(bf16[8,400,384]{2,1,0:T(8,128)(2,1)} %broadcast_in_dim.94), calls=%async_computation | async-start | bytes 4915200 | tf_op jit(solution)/shard_map/all_to_all | solution.py:58
  34.1 57.7 %copy-start.7 = (f32[2,128]{1,0:T(2,128)S(1)}, f32[2,128]{1,0:T(2,128)}, u32[]{:S(2)}) copy-start(f32[2,128]{1,0:T(2,128)} %param.11) | copy-start | bytes 3076
  67.1 23.1 %all-to-all-start.2 = ((bf16[16,128,200]{1,2,0:T(8,128)(2,1)}), bf16[16,128,200]{1,2,0:T(8,128)(2,1)S(1)}, u32[]{:S(2)}, u32[]{:S(2)}) async-start(bf16[16,128,200]{1,2,0:T(8,128)(2,1)} %copy.101), calls=%async_computation.2 | async-start | bytes 1638400 | tf_op jit(solution)/shard_map/all_to_all | solution.py:113
  75.1 22.3 %collective-permute-start = (bf16[3200,384]{1,0:T(8,128)(2,1)S(1)}, bf16[3200,384]{1,0:T(8,128)(2,1)}, u32[]{:S(2)}, u32[]{:S(2)}) collective-permute-start(bf16[3200,384]{1,0:T(8,128)(2,1)S(1)} %bitcast.94), channel_id=1, source_target_pairs={{0,1},{1,0},{2,3},{3,2},{4,5},{5,4},{6,7},{7,6},{8,9},{9,8},{10,11... | collective-permute-start | bytes 7372808 | tf_op jit(solution)/shard_map/ppermute | solution.py:91
  91.1 3.5 collective-permute-start.1
  91.8 2.3 collective-permute-start.2
  128.3 5.0 %copy-start = (bf16[1,1088,3200]{2,1,0:T(8,128)(2,1)S(1)}, bf16[1,1088,3200]{2,1,0:T(8,128)(2,1)}, u32[]{:S(2)}) copy-start(bf16[1,1088,3200]{2,1,0:T(8,128)(2,1)} %all-gather.3.cloned.1.call-done) | copy-start | bytes 20889604
  128.3 5.0 %copy-start.8 = (f32[3200]{0:T(1024)S(1)}, f32[3200]{0:T(1024)}, u32[]{:S(2)}) copy-start(f32[3200]{0:T(1024)} %param.9) | copy-start | bytes 38404
  143.8 12.4 %all-to-all-start.3 = ((f32[8,2,1088]{2,1,0:T(2,128)}), f32[8,2,1088]{2,1,0:T(2,128)}, u32[]{:S(2)}, u32[]{:S(2)}) async-start(f32[8,2,1088]{2,1,0:T(2,128)} %broadcast_in_dim.96), calls=%async_computation.3 | async-start | bytes 147456 | tf_op jit(solution)/shard_map/all_to_all | solution.py:52
  157.1 1.1 copy-start.3
  159.4 2.6 collective-permute-start.3
  174.2 7.0 %copy-start.5 = (s32[8,2]{0,1:T(2,128)S(1)}, s32[8,2]{0,1:T(2,128)}, u32[]{:S(2)}) copy-start(s32[8,2]{0,1:T(2,128)} %param.14) | copy-start | bytes 196
  174.2 7.0 %copy-start.6 = (s32[8,2]{0,1:T(2,128)S(1)}, s32[8,2]{0,1:T(2,128)}, u32[]{:S(2)}) copy-start(s32[8,2]{0,1:T(2,128)} %param.15) | copy-start | bytes 196
  174.2 7.2 %copy-start.1 = (bf16[2048,400]{0,1:T(8,128)(2,1)S(1)}, bf16[2048,400]{0,1:T(8,128)(2,1)}, u32[]{:S(2)}) copy-start(bf16[2048,400]{0,1:T(8,128)(2,1)} %pad_maximum_fusion.3) | copy-start | bytes 4915204
  174.2 65.9 %all-to-all-start.4 = ((bf16[16,1088,128]{2,1,0:T(8,128)(2,1)}), bf16[16,1088,128]{2,1,0:T(8,128)(2,1)}, u32[]{:S(2)}, u32[]{:S(2)}) async-start(bf16[16,1088,128]{2,1,0:T(8,128)(2,1)} %bitcast.93), calls=%async_computation.4 | async-start | bytes 8912896 | tf_op jit(solution)/shard_map/all_to_all | solution.py:184
  248.3 4.1 %copy-start.2 = (bf16[1088,400]{1,0:T(8,128)(2,1)S(1)}, bf16[1088,400]{1,0:T(8,128)(2,1)}, u32[]{:S(2)}) copy-start(bf16[1088,400]{1,0:T(8,128)(2,1)} %shard_map.82) | copy-start | bytes 2611204
  250.1 2.1 collective-permute-start.4
  274.1 96.5 %all-to-all-start.5 = ((bf16[8,2,256,800]{2,3,1,0:T(8,128)(2,1)}), bf16[8,2,256,800]{2,3,1,0:T(8,128)(2,1)}, u32[]{:S(2)}, u32[]{:S(2)}) async-start(bf16[8,2,256,800]{2,3,1,0:T(8,128)(2,1)} %broadcast_select_fusion), calls=%async_computation.5 | async-start | bytes 13107200 | tf_op jit(solution)/shard_map/all_to_all | solution.py:212
Sparse Core Ops, SparseCore 0:
  9.7 118.6 all-gather.2

commit v16 on v15

--- a/solution.py
+++ b/solution.py
@@ -208,7 +208,7 @@
     own_living = living[row_index]
     destination = jnp.arange(row_count, dtype=jnp.int32)[:, None]
     sending = jnp.logical_and(destination == own_holder[None, :], own_living[None, :])
-    outgoing = jnp.where(sending[:, :, None, None], merged[None], jnp.zeros((), jnp.bfloat16))
+    outgoing = jnp.broadcast_to(merged[None], (row_count,) + merged.shape)
     received = lax.all_to_all(outgoing, "fsdp", split_axis=0, concat_axis=0, tiled=True)
     return place_tiles(received, holder, living, row_index)
 

time: 384 us -> 384 us (level)
    broadcast_in_dim x1 -> x2, local copies, waits for them, and re-layouts: 8.1 us -> 11.4 us  [body(): outgoing = jnp.broadcast_to(merged[None], (row_count,) + merged.shape)]
where the time goes in v16:
time: 384 us; the launch traced here: 383 us
  waiting for transfers between devices  219 us (57%)
  local copies, waits for them, and re-layouts  43.1 us (11%)
  starting transfers between devices  29.2 us (8%)
  other arithmetic  25.4 us (7%)
  between operations  21.4 us (6%)
  blocking collectives  19 us (5%)
  matrix products  17.6 us (5%)
  Pallas kernels  8.24 us (2%)
    all_to_all x1, waiting for transfers between devices, body(): lax.all_to_all(outgoing, 'fsdp', split_axis=0, concat_axis=0, tiled=True)  81.5 us
    all_to_all x1, waiting for transfers between devices, body(): lax.all_to_all(outgoing.reshape(groups, half_length, HEAD_DIM), ('chip',...  53.6 us
    all_to_all x1, waiting for transfers between devices, gather_blocks(): lax.all_to_all(spread, axis_name, split_axis=0, concat_axis=0, tiled=True)  30.7 us
    all_gather x1, waiting for transfers between devices, body(): half = lax.all_gather(own_rows, 'chip', axis=0, tiled=True)  26.1 us
    all_to_all x1, blocking collectives, body(): lax.all_to_all(spread, 'fsdp', split_axis=0, concat_axis=0, tiled=True)  19 us
    all_to_all x1, waiting for transfers between devices, body(): lax.all_to_all(head_rows.reshape(groups, HEAD_DIM, block), ('chip', 'core...  15 us
    broadcast_in_dim x2, local copies, waits for them, and re-layouts, body(): outgoing = jnp.broadcast_to(merged[None], (row_count,) + merged.shape)  11.4 us
    dot_general x1, matrix products, body(): projected = jnp.dot(normed, pair_qkv, preferred_element_type=jnp.float32)  9.55 us
  transfers between devices with their start and end apart: 11, of which 9 were waited for; matrix products, arithmetic and copies ran while one was open for 7% of the time, Pallas kernels for 0%

profile of v16, /device:TPU:8, one launch (start us, length us, event | category | flops | bytes accessed | tf_op | source)
XLA Modules:
  0.0 383.0 jit_solution(8179549574393913863)
XLA Ops:
  8.3 19.0 %all_to_all.30 = bf16[8,128,400]{1,2,0:T(8,128)(2,1)S(1)} all-to-all(bf16[8,128,400]{1,2,0:T(8,128)(2,1)S(1)} %broadcast_in_dim.77), channel_id=1, replica_groups=mesh['fsdp'=8,'chip'=8,'core'=2] {'fsdp'}, dimensions={0} | all-to-all | bytes 1638400 | tf_op jit(solution)/shard_map/all_to_all | solution.py:110
  27.3 1.7 broadcast_in_dim.76
  29.0 3.6 all-to-all-start
  34.1 2.3 copy.101
  36.4 30.7 %all-to-all-done = bf16[8,400,384]{2,1,0:T(8,128)(2,1)S(1)} async-done(((bf16[8,400,384]{2,1,0:T(8,128)(2,1)}), bf16[8,400,384]{2,1,0:T(8,128)(2,1)S(1)}, u32[]{:S(2)}, u32[]{:S(2)}) %all-to-all-start) | async-done | bytes 2457632 | tf_op jit(solution)/shard_map/all_to_all | solution.py:58
  67.1 8.0 %all-to-all-start.2 = ((bf16[16,128,200]{1,2,0:T(8,128)(2,1)}), bf16[16,128,200]{1,2,0:T(8,128)(2,1)S(1)}, u32[]{:S(2)}, u32[]{:S(2)}) async-start(bf16[16,128,200]{1,2,0:T(8,128)(2,1)} %copy.101), calls=%async_computation.2 | async-start | bytes 1638400 | tf_op jit(solution)/shard_map/all_to_all | solution.py:113
  75.2 15.0 %all-to-all-done.2 = bf16[16,128,200]{1,2,0:T(8,128)(2,1)S(1)} async-done(((bf16[16,128,200]{1,2,0:T(8,128)(2,1)}), bf16[16,128,200]{1,2,0:T(8,128)(2,1)S(1)}, u32[]{:S(2)}, u32[]{:S(2)}) %all-to-all-start.2) | async-done | bytes 819232 | tf_op jit(solution)/shard_map/all_to_all | solution.py:113
  91.8 2.3 collective-permute-done.2
  97.4 2.1 broadcast_select_fusion.1
  99.6 2.7 pad_maximum_fusion
  102.2 26.1 %all-gather.3.cloned.1.call-done = bf16[1,1088,3200]{2,1,0:T(8,128)(2,1)} async-done(((bf16[1,136,3200]{2,1,0:T(8,128)(2,1)}), bf16[1,1088,3200]{2,1,0:T(8,128)(2,1)}) %all-gather.3.cloned.1.call-update) | async-done | bytes 6963216 | tf_op jit(solution)/shard_map/all_gather | solution.py:125
  128.3 4.6 %fusion.2 = f32[1088]{0:T(1024)S(1)} fusion(bf16[1,1088,3200]{2,1,0:T(8,128)(2,1)} %all-gather.3.cloned.1.call-done), kind=kLoop, calls=%fused_computation.5 | loop fusion | flops 10443712 | bytes 6967552 | tf_op jit(solution)/shard_map/reduce_sum | solution.py:130
  133.3 9.5 %fusion.6 = f32[1088,768]{0,1:T(8,128)S(1)} fusion(bf16[3200,768]{1,0:T(8,128)(2,1)} %pad_maximum_fusion, bf16[1,1088,3200]{2,1,0:T(8,128)(2,1)S(1)} %copy-done, f32[3200]{0:T(1024)S(1)} %copy-done.8, f32[1088]{0:T(1024)S(1)} %add_rsqrt_fusion), kind=kOutput, calls=%fused_computation.10 | convolution fusion | flops 5361664000 | bytes 15237888 | tf_op jit(solution)/shard_map/dot_general | solution.py:132
  143.8 5.6 %all-to-all-start.3 = ((f32[8,2,1088]{2,1,0:T(2,128)}), f32[8,2,1088]{2,1,0:T(2,128)}, u32[]{:S(2)}, u32[]{:S(2)}) async-start(f32[8,2,1088]{2,1,0:T(2,128)} %broadcast_in_dim.78), calls=%async_computation.3 | async-start | bytes 147456 | tf_op jit(solution)/shard_map/all_to_all | solution.py:52
  150.3 5.9 %all-to-all-done.3 = f32[8,2,1088]{2,1,0:T(2,128)} async-done(((f32[8,2,1088]{2,1,0:T(2,128)}), f32[8,2,1088]{2,1,0:T(2,128)}, u32[]{:S(2)}, u32[]{:S(2)}) %all-to-all-start.3) | async-done | bytes 69664 | tf_op jit(solution)/shard_map/all_to_all | solution.py:52
  162.9 3.2 fusion.40
  166.2 4.9 %fusion.12 = bf16[2,1025,128]{2,1,0:T(8,128)(2,1)S(1)} fusion(bf16[2,1025,128]{2,1,0:T(8,128)(2,1)S(1)} %reshape_squeeze.11, f32[2,1025]{1,0:T(2,128)S(1)} %fusion.40, bf16[2,1025,128]{2,1,0:T(8,128)(2,1)S(1)} %reshape_squeeze.9, bf16[2,1025,128]{2,1,0:T(8,128)(2,1)S(1)} %reshape_squeeze.10), kind=kOutput, calls=%fused_computation.16 | convolution fusion | flops 1084510464 | bytes 2107400 | tf_op jit(solution)/shard_map/sqk,skc->sqc/dot_general | solution.py:171
  171.2 3.0 broadcast_in_dim.80
  174.2 5.7 %all-to-all-start.4 = ((bf16[16,1088,128]{2,1,0:T(8,128)(2,1)}), bf16[16,1088,128]{2,1,0:T(8,128)(2,1)}, u32[]{:S(2)}, u32[]{:S(2)}) async-start(bf16[16,1088,128]{2,1,0:T(8,128)(2,1)} %bitcast.89), calls=%async_computation.4 | async-start | bytes 8912896 | tf_op jit(solution)/shard_map/all_to_all | solution.py:184
  181.2 2.4 copy.113
  183.6 2.8 dynamic-slice_bitcast_fusion.tokens_ref
  186.5 53.6 %all-to-all-done.4.heads_ref = bf16[16,1088,128]{2,1,0:T(8,128)(2,1)} async-done(((bf16[16,1088,128]{2,1,0:T(8,128)(2,1)}), bf16[16,1088,128]{2,1,0:T(8,128)(2,1)}, u32[]{:S(2)}, u32[]{:S(2)}) %all-to-all-start.4) | async-done | bytes 4456480 | tf_op jit(solution)/shard_map/all_to_all | solution.py:184
  240.1 8.2 %shard_map.82 = bf16[1088,400]{1,0:T(8,128)(2,1)} custom-call(bf16[16,1088,128]{2,1,0:T(8,128)(2,1)} %all-to-all-done.4.heads_ref, bf16[16,128,400]{2,1,0:T(8,128)(2,1)} %bitcast.91, bf16[1088,400]{1,0:T(8,128)(2,1)} %dynamic-slice_bitcast_fusion.tokens_ref, f32[1,400]{1,0:T(1,128)} %bitcast.105), custom_call_target="tpu_custom_call" | custom-call | tf_op jit(solution)/shard_map/pallas_call | solution.py:76
  248.3 1.5 constant_dynamic-slice_fusion
  250.4 1.8 collective-permute-done.4
  253.8 1.7 maximum_bitcast_fusion
  255.5 7.1 %copy.119 = bf16[2,16,16,200,2,2]{2,1,5,4,3,0:T(8,128)(2,1)} copy(bf16[2,16,16,200,2,2]{3,5,2,4,1,0:T(2,128)(2,1)S(1)} %maximum_bitcast_fusion) | data formatting | bytes 1638400 | tf_op jit(solution)/shard_map/transpose | solution.py:204
  262.6 8.1 %broadcast_in_dim.81 = bf16[2,256,800]{1,2,0:T(8,128)(2,1)S(1)} reshape(bf16[2,16,16,200,2,2]{2,1,5,4,3,0:T(8,128)(2,1)} %copy.119) | data formatting | bytes 1638400 | tf_op jit(solution)/shard_map/broadcast_in_dim | solution.py:211
  270.8 3.3 broadcast_in_dim.82
  274.1 4.9 %all-to-all-start.5 = ((bf16[8,2,256,800]{2,3,1,0:T(8,128)(2,1)}), bf16[8,2,256,800]{2,3,1,0:T(8,128)(2,1)}, u32[]{:S(2)}, u32[]{:S(2)}) async-start(bf16[8,2,256,800]{2,3,1,0:T(8,128)(2,1)} %broadcast_in_dim.82), calls=%async_computation.5 | async-start | bytes 13107200 | tf_op jit(solution)/shard_map/all_to_all | solution.py:212
  289.2 81.5 %all-to-all-done.5 = bf16[8,2,256,800]{2,3,1,0:T(8,128)(2,1)} async-done(((bf16[8,2,256,800]{2,3,1,0:T(8,128)(2,1)}), bf16[8,2,256,800]{2,3,1,0:T(8,128)(2,1)}, u32[]{:S(2)}, u32[]{:S(2)}) %all-to-all-start.5) | async-done | bytes 6553632 | tf_op jit(solution)/shard_map/all_to_all | solution.py:212
  370.7 4.0 %dynamic-slice_select_fusion.3 = (bf16[1,256,800]{1,2,0:T(8,128)(2,1)S(1)}, bf16[1,256,800]{1,2,0:T(8,128)(2,1)S(1)}, bf16[1,256,800]{1,2,0:T(8,128)(2,1)S(1)}, bf16[1,256,800]{1,2,0:T(8,128)(2,1)S(1)}) fusion(bf16[16,256,800]{1,2,0:T(8,128)(2,1)} %bitcast.31, s32[]{:T(128)S(6)} %select_n.170, pred[]{:T(512)} %get-tuple-element.44, s32[]{:T(128)S(6)} %select_n.182, ...), kind=kLoop, calls=%fused_computation.48 | loop fusion | flops 819200 | bytes 3276820 | tf_op jit(solution)/shard_map/jit(_where)/select_n | solution.py:46
  (82 shorter events, 24.6 us)
Async XLA Ops:
  6.5 20.7 %copy-start.4 = (bf16[400,384]{1,0:T(8,128)(2,1)S(1)}, bf16[400,384]{1,0:T(8,128)(2,1)}, u32[]{:S(2)}) copy-start(bf16[400,384]{1,0:T(8,128)(2,1)} %param.10) | copy-start | bytes 921604
  6.5 121.8 %all-gather.3.cloned.1.call-start = ((), (), s32[]{:S(2)}) async-start(), calls=%async_computation.6 | async-start | bytes 7833600 | tf_op jit(solution)/shard_map/all_gather | solution.py:125
  29.0 38.1 %all-to-all-start = ((bf16[8,400,384]{2,1,0:T(8,128)(2,1)}), bf16[8,400,384]{2,1,0:T(8,128)(2,1)S(1)}, u32[]{:S(2)}, u32[]{:S(2)}) async-start(bf16[8,400,384]{2,1,0:T(8,128)(2,1)} %broadcast_in_dim.76), calls=%async_computation | async-start | bytes 4915200 | tf_op jit(solution)/shard_map/all_to_all | solution.py:58
  34.1 57.7 %copy-start.7 = (f32[2,128]{1,0:T(2,128)S(1)}, f32[2,128]{1,0:T(2,128)}, u32[]{:S(2)}) copy-start(f32[2,128]{1,0:T(2,128)} %param.11) | copy-start | bytes 3076
  67.1 23.1 %all-to-all-start.2 = ((bf16[16,128,200]{1,2,0:T(8,128)(2,1)}), bf16[16,128,200]{1,2,0:T(8,128)(2,1)S(1)}, u32[]{:S(2)}, u32[]{:S(2)}) async-start(bf16[16,128,200]{1,2,0:T(8,128)(2,1)} %copy.101), calls=%async_computation.2 | async-start | bytes 1638400 | tf_op jit(solution)/shard_map/all_to_all | solution.py:113
  75.1 22.3 %collective-permute-start = (bf16[3200,384]{1,0:T(8,128)(2,1)S(1)}, bf16[3200,384]{1,0:T(8,128)(2,1)}, u32[]{:S(2)}, u32[]{:S(2)}) collective-permute-start(bf16[3200,384]{1,0:T(8,128)(2,1)S(1)} %bitcast.90), channel_id=1, source_target_pairs={{0,1},{1,0},{2,3},{3,2},{4,5},{5,4},{6,7},{7,6},{8,9},{9,8},{10,11... | collective-permute-start | bytes 7372808 | tf_op jit(solution)/shard_map/ppermute | solution.py:91
  91.1 3.5 collective-permute-start.1
  91.8 2.3 collective-permute-start.2
  128.3 5.0 %copy-start = (bf16[1,1088,3200]{2,1,0:T(8,128)(2,1)S(1)}, bf16[1,1088,3200]{2,1,0:T(8,128)(2,1)}, u32[]{:S(2)}) copy-start(bf16[1,1088,3200]{2,1,0:T(8,128)(2,1)} %all-gather.3.cloned.1.call-done) | copy-start | bytes 20889604
  128.3 5.0 %copy-start.8 = (f32[3200]{0:T(1024)S(1)}, f32[3200]{0:T(1024)}, u32[]{:S(2)}) copy-start(f32[3200]{0:T(1024)} %param.9) | copy-start | bytes 38404
  143.8 12.4 %all-to-all-start.3 = ((f32[8,2,1088]{2,1,0:T(2,128)}), f32[8,2,1088]{2,1,0:T(2,128)}, u32[]{:S(2)}, u32[]{:S(2)}) async-start(f32[8,2,1088]{2,1,0:T(2,128)} %broadcast_in_dim.78), calls=%async_computation.3 | async-start | bytes 147456 | tf_op jit(solution)/shard_map/all_to_all | solution.py:52
  157.1 1.1 copy-start.3
  159.4 2.6 collective-permute-start.3
  174.2 7.0 %copy-start.1 = (bf16[2048,400]{0,1:T(8,128)(2,1)S(1)}, bf16[2048,400]{0,1:T(8,128)(2,1)}, u32[]{:S(2)}) copy-start(bf16[2048,400]{0,1:T(8,128)(2,1)} %pad_maximum_fusion.3) | copy-start | bytes 4915204
  174.2 65.9 %all-to-all-start.4 = ((bf16[16,1088,128]{2,1,0:T(8,128)(2,1)}), bf16[16,1088,128]{2,1,0:T(8,128)(2,1)}, u32[]{:S(2)}, u32[]{:S(2)}) async-start(bf16[16,1088,128]{2,1,0:T(8,128)(2,1)} %bitcast.89), calls=%async_computation.4 | async-start | bytes 8912896 | tf_op jit(solution)/shard_map/all_to_all | solution.py:184
  248.3 4.1 %copy-start.2 = (bf16[1088,400]{1,0:T(8,128)(2,1)S(1)}, bf16[1088,400]{1,0:T(8,128)(2,1)}, u32[]{:S(2)}) copy-start(bf16[1088,400]{1,0:T(8,128)(2,1)} %shard_map.82) | copy-start | bytes 2611204
  250.1 2.1 collective-permute-start.4
  274.1 4.9 %copy-start.5 = (s32[8,2]{0,1:T(2,128)S(1)}, s32[8,2]{0,1:T(2,128)}, u32[]{:S(2)}) copy-start(s32[8,2]{0,1:T(2,128)} %param.14) | copy-start | bytes 196
  274.1 4.9 %copy-start.6 = (s32[8,2]{0,1:T(2,128)S(1)}, s32[8,2]{0,1:T(2,128)}, u32[]{:S(2)}) copy-start(s32[8,2]{0,1:T(2,128)} %param.15) | copy-start | bytes 196
  274.1 96.6 %all-to-all-start.5 = ((bf16[8,2,256,800]{2,3,1,0:T(8,128)(2,1)}), bf16[8,2,256,800]{2,3,1,0:T(8,128)(2,1)}, u32[]{:S(2)}, u32[]{:S(2)}) async-start(bf16[8,2,256,800]{2,3,1,0:T(8,128)(2,1)} %broadcast_in_dim.82), calls=%async_computation.5 | async-start | bytes 13107200 | tf_op jit(solution)/shard_map/all_to_all | solution.py:212
Sparse Core Ops, SparseCore 0:
  9.7 118.6 all-gather.2
